TPU v7x, 32 devices: a whole 2x2x4 slice. The times are simulated.
32 devices in a mesh: layer: 4 (over x, core), tok: 8 (over z, y).
Axes of the slice: x: 2, y: 2, z: 4, core: 2. Of those that a mesh axis runs over, the one named last changes fastest.
Arguments:
- active_codes: bfloat16 [4, 1024, 32], P('layer', 'tok'), may hold values from 0.19921875 to 3
- latent_ids: int32 [4, 1024, 32], P('layer', 'tok'), may hold values from 0 to 32767, as said below
- decoder: bfloat16 [4, 32768, 4096], P('layer', 'tok'), may hold values from -1 to 1
- carry_gain: float32 [4, 4096], P('layer'), may hold values from 0.1 to 1
- earlier_sum: bfloat16 [1024, 4096], P('tok'), may hold values from -6 to 6
- targets: bfloat16 [4, 1024, 4096], P('layer', 'tok'), may hold values from -6 to 6
Outputs:
- reconstruction: bfloat16 [4, 1024, 4096], P('layer', 'tok')
- code_grad: float32 [4, 1024, 32], P('layer', 'tok')
Inputs may be any that keep to these rules, and one draw needn't show every extreme that they name: `latent_ids`: A token's 32 ids in one layer are distinct. In each layer, the 128 tokens of one aligned block have at most 768 ids in any one range of 4096 consecutive latents, and in every layer one range holds exactly 768 ids of every block.
All inputs are finite; a program needn't handle non-finite values.
Results may differ from a plain program's by a relative error of at most 0.019.
Values may be sent and summed in bfloat16 or wider, within the bound.
No kernel may reach another device: no remote copies, remote signals or barrier semaphores. Data moves between devices by JAX's collectives and lax.ppermute only.
A program may use at most 256 MiB of HBM per device.

v0:
```python
import jax
import jax.numpy as jnp
from jax import lax
from jax.sharding import PartitionSpec as P


def prefix(shard, axis, combine, identity, reverse):
    length, mine = (lax.axis_size(axis), lax.axis_index(axis))
    everything = jax.tree.map(
        lambda part, kind: lax.all_gather(part.astype(kind), axis),
        shard,
        (jnp.bfloat16, jnp.bfloat16),
    )
    start = jax.tree.map(
        lambda part, zero: jnp.broadcast_to(jnp.asarray(zero, part.dtype), part.shape),
        shard,
        identity,
    )

    def lap(k, before):
        at = length - 1 - k if reverse else k
        reached = at > mine if reverse else at < mine
        new = combine(
            before, jax.tree.map(lambda part, own: part[at].astype(own.dtype), everything, shard)
        )
        return jax.tree.map(lambda a, b: jnp.where(reached, a, b), new, before)

    return lax.fori_loop(0, length, lap, start)


def bucket_lists(latent_rows, code_rows, range_size, owners, capacity):
    tok_rows, top_count = latent_rows.shape
    entries = tok_rows * top_count
    flat_ids = latent_rows.reshape(entries)
    owning = flat_ids // range_size
    within = flat_ids % range_size
    positions = jnp.arange(entries, dtype=jnp.int32) // top_count
    ordering = jnp.argsort(owning, stable=True)
    counts = jnp.sum(
        (owning[:, None] == jnp.arange(owners, dtype=jnp.int32)[None, :]).astype(jnp.int32), axis=0
    )
    starts = jnp.cumsum(counts) - counts
    sorted_rank = jnp.arange(entries, dtype=jnp.int32) - starts[owning[ordering]]
    rank_of = jnp.zeros(entries, jnp.int32).at[ordering].set(sorted_rank)
    slot_index = owning * capacity + rank_of
    slot_keys = (
        jnp.zeros(owners * capacity, jnp.int32).at[slot_index].set(within * tok_rows + positions)
    )
    slot_codes = (
        jnp.zeros(owners * capacity, jnp.bfloat16).at[slot_index].set(code_rows.reshape(entries))
    )
    return (slot_keys.reshape(owners, capacity), slot_codes.reshape(owners, capacity), slot_index)


def source_term(rows, slot_keys, slot_codes, tok_rows):
    token_index = slot_keys % tok_rows
    matches = token_index[None, :] == jnp.arange(tok_rows, dtype=jnp.int32)[:, None]
    spread = jnp.where(matches, slot_codes[None, :], jnp.zeros((), jnp.bfloat16))
    return jnp.dot(spread, rows, preferred_element_type=jnp.float32)


def slot_grads_of(rows, slot_keys, grad_block, tok_rows):
    token_index = slot_keys % tok_rows
    products = jnp.einsum("td,cd->tc", grad_block, rows, preferred_element_type=jnp.float32)
    matches = token_index[None, :] == jnp.arange(tok_rows, dtype=jnp.int32)[:, None]
    return jnp.sum(jnp.where(matches, products, 0.0), axis=0)


def compose(earlier_part, later_part):
    return (earlier_part[0] * later_part[0], later_part[0] * earlier_part[1] + later_part[1])


def on_device(active_codes, latent_ids, decoder, carry_gain, earlier_sum, targets):
    owners = lax.axis_size("tok")
    tok_rows = active_codes.shape[1]
    top_count = active_codes.shape[2]
    range_size = decoder.shape[1]
    model_width = decoder.shape[2]
    capacity = 3 * tok_rows * top_count // (2 * owners)
    weights = decoder[0]
    slot_keys, slot_codes, slot_index = bucket_lists(
        latent_ids[0], active_codes[0], range_size, owners, capacity
    )
    recv_keys, recv_codes = (
        lax.all_to_all(slot_keys, "tok", split_axis=0, concat_axis=0, tiled=True),
        lax.all_to_all(slot_codes, "tok", split_axis=0, concat_axis=0, tiled=True),
    )
    row_cache = jnp.take(weights, recv_keys // tok_rows, axis=0)

    def one_source(triple):
        return source_term(triple[2], triple[0], triple[1], tok_rows)

    keys_part = recv_keys
    rows_part = row_cache
    term_blocks = lax.map(one_source, (keys_part, recv_codes, rows_part))
    decoded = lax.psum_scatter(
        term_blocks.reshape(lax.axis_size("tok") * tok_rows, model_width).astype(jnp.bfloat16),
        "tok",
        scatter_dimension=0,
        tiled=True,
    ).astype(jnp.float32)
    identity = (jnp.ones_like(carry_gain), jnp.zeros_like(decoded))
    ahead_gain, ahead_sum = prefix((carry_gain, decoded), "layer", compose, identity, False)
    recon_full = carry_gain * (ahead_gain * earlier_sum.astype(jnp.float32) + ahead_sum) + decoded
    misfit = recon_full - targets[0].astype(jnp.float32)
    behind_gain, behind_sum = prefix(
        (carry_gain, carry_gain * misfit), "layer", compose, identity, True
    )
    grad_low = (misfit + behind_sum).astype(jnp.bfloat16)

    def grads_of_source(triple):
        return slot_grads_of(triple[2], triple[0], triple[1], tok_rows)

    segment = lax.all_gather(grad_low, "tok", axis=0, tiled=True)
    source_count = segment.shape[0] // tok_rows
    keys_part = recv_keys
    rows_part = row_cache
    grad_blocks = segment.reshape(source_count, tok_rows, model_width)
    values = lax.map(grads_of_source, (keys_part, grad_blocks, rows_part))
    returned = lax.all_to_all(values, "tok", split_axis=0, concat_axis=0, tiled=True)
    code_grad = jnp.take(returned.reshape(owners * capacity), slot_index).reshape(
        tok_rows, top_count
    )
    return (recon_full.astype(jnp.bfloat16)[None], code_grad[None])


def solution(mesh):
    return jax.shard_map(
        on_device,
        mesh=mesh,
        in_specs=(
            P("layer", "tok", None),
            P("layer", "tok", None),
            P("layer", "tok", None),
            P("layer", None),
            P("tok", None),
            P("layer", "tok", None),
        ),
        out_specs=(P("layer", "tok", None), P("layer", "tok", None)),
        check_vma=False,
    )
```

profile of v0, /device:TPU:0, one launch (start us, length us, event | category | flops | bytes accessed | tf_op | source)
XLA Modules:
  0.0 932.7 jit_solution(17020449953633308792)
XLA Ops:
  9.1 5.8 sort.17
  14.9 23.0 %gather_fusion = s32[4096]{0:T(1024)S(1)} fusion(s32[4096]{0:T(1024)S(1)} %add_select_fusion.3, s32[4096]{0:T(1024)S(1)} %get-tuple-element.481), kind=kCustom, calls=%fused_computation | custom fusion | bytes 49152 | tf_op jit(solution)/shard_map/gather | solution.py:43
  38.0 4.4 compare_select_fusion.7
  43.0 15.5 %scatter_custom_fusion = s32[4096]{0:T(1024)S(1)} fusion(s32[4096]{0:T(1024)S(1)} %get-tuple-element.482, s32[4096]{0:T(1024)S(1)} %select_subtract_fusion, s32[]{:T(128)} %constant.237.clone.1), kind=kCustom, calls=%fused_computation.106 | custom fusion | bytes 16388 | tf_op jit(solution)/shard_map/scatter | solution.py:44
  59.4 28.6 %scatter_custom_fusion.2 = bf16[6144]{0:T(1024)(128)(2,1)S(1)} fusion(s32[4096]{0:T(1024)S(1)} %get-tuple-element.475, bf16[4096]{0:T(1024)(128)(2,1)S(1)} %reshape.307, bf16[]{:T(256)} %constant.252.clone.1), kind=kCustom, calls=%fused_computation.108 | custom fusion | bytes 12290 | tf_op jit(solution)/shard_map/scatter | solution.py:50
  89.9 7.3 all-to-all-start.1
  97.1 16.1 %scatter_custom_fusion.1 = s32[6144]{0:T(1024)} fusion(s32[4096]{0:T(1024)S(1)} %get-tuple-element.475, s32[4096]{0:T(1024)S(1)} %get-tuple-element.480, s32[]{:T(128)} %constant.237.clone.1), kind=kCustom, calls=%fused_computation.101 | custom fusion | bytes 24580 | tf_op jit(solution)/shard_map/scatter | solution.py:47
  113.2 6.0 all-to-all-start
  120.1 5.8 all-to-all-done
  126.0 268.7 %gather_fusion.1 = bf16[6144,4096]{1,0:T(8,128)(2,1)} fusion(bf16[4096,4096]{1,0:T(8,128)(2,1)} %bitcast.100, s32[6144]{0:T(1024)S(1)} %broadcast_clamp_fusion), kind=kCustom, calls=%fused_computation.1 | custom fusion | bytes 100687872 | tf_op jit(solution)/shard_map/jit(_take)/gather | solution.py:88
  394.8 33.4 %broadcast_select_fusion.2 = bf16[8,768,4096]{2,1,0:T(8,128)(2,1)} fusion(bf16[8,768,4096]{2,1,0:T(8,128)(2,1)} %bitcast.101, pred[8,768]{1,0:T(8,128)(4,1)S(1)} %compare_and_fusion), kind=kLoop, calls=%fused_computation.46 | loop fusion | flops 25165824 | bytes 100669440 | tf_op jit(solution)/shard_map/jit(_take)/select_n | solution.py:88
  428.2 44.3 %while.56 = (s32[]{:T(128)}, bf16[8,128,4096]{2,1,0:T(8,128)(2,1)}, s32[8,768]{1,0:T(8,128)S(1)}, bf16[8,768]{1,0:T(8,128)(2,1)}, bf16[8,768,4096]{2,1,0:T(8,128)(2,1)}, /*index=5*/s32[]{:T(128)}) while((s32[]{:T(128)}, bf16[8,128,4096]{2,1,0:T(8,128)(2,1)}, s32[8,768]{1,0:T(8,128)S(1)}, bf16[8,768]{1,0:T(8,128)(2,1)}, ...), condition=%wide.region_7.8_spmd, body=%wide.region_6.7_spmd.sunk | while | flops 805511424 | bytes 8403533 | solution.py:95
  428.9 4.7 fusion.63
  434.5 4.7 fusion.63
  440.0 4.8 fusion.63
  445.5 4.8 fusion.63
  451.0 4.8 fusion.63
  456.6 4.8 fusion.63
  462.1 4.8 fusion.63
  467.6 4.8 fusion.63
  472.5 152.7 %reduce-scatter.2.cloned.1.call-done = bf16[128,4096]{1,0:T(8,128)(2,1)} async-done(((bf16[1024,4096]{1,0:T(8,128)(2,1)}), bf16[128,4096]{1,0:T(8,128)(2,1)}) %reduce-scatter.2.cloned.1.call-update) | async-done | bytes 1048592 | tf_op jit(solution)/shard_map/reduce_scatter | solution.py:96
  625.3 5.2 all-gather.3
  630.6 29.8 %all-gather.10.cloned.1.call-done = bf16[512,4096]{1,0:T(8,128)(2,1)} async-done(((bf16[128,4096]{1,0:T(8,128)(2,1)}), bf16[512,4096]{1,0:T(8,128)(2,1)}) %all-gather.10.cloned.1.call-update) | async-done | bytes 4194320 | tf_op jit(solution)/shard_map/all_gather | solution.py:10
  660.4 10.5 %while.58 = (s32[]{:T(128)}, f32[1,4096]{1,0:T(1,128)S(1)}, f32[128,4096]{1,0:T(8,128)S(1)}, s32[]{:T(128)}, bf16[4,1,4096]{2,1,0:T(2,128)(2,1)S(1)}, /*index=5*/bf16[4,128,4096]{2,1,0:T(8,128)(2,1)}, s32[]{:T(128)}, s32[]{:T(128)}) while((s32[]{:T(128)}, f32[1,4096]{1,0:T(1,128)S(1)}, f32[128,4096]{1,0:T(8,128)S(1)}, ...), condition=%wide.region_10.11_spmd.clone, body=%wide.region_9.10_spmd.clone.sunk | while | flops 2637828 | bytes 5316723 | solution.py:28
  660.4 2.6 fusion.68
  663.1 2.6 fusion.68
  665.7 2.6 fusion.68
  668.4 2.6 fusion.68
  670.9 3.9 multiply_convert_fusion
  674.9 34.6 %all-gather.12.cloned.1.call-done = bf16[512,4096]{1,0:T(8,128)(2,1)} async-done(((bf16[128,4096]{1,0:T(8,128)(2,1)}), bf16[512,4096]{1,0:T(8,128)(2,1)}) %all-gather.12.cloned.1.call-update) | async-done | bytes 4194320 | tf_op jit(solution)/shard_map/all_gather | solution.py:10
  709.5 10.4 %while.59 = (s32[]{:T(128)}, f32[128,4096]{1,0:T(8,128)S(1)}, s32[]{:T(128)}, bf16[4,1,4096]{2,1,0:T(2,128)(2,1)S(1)}, bf16[4,128,4096]{2,1,0:T(8,128)(2,1)}, /*index=5*/s32[]{:T(128)}, s32[]{:T(128)}, s32[]{:T(128)}, s32[]{:T(128)}) while((s32[]{:T(128)}, f32[128,4096]{1,0:T(8,128)S(1)}, s32[]{:T(128)}, ...), condition=%wide.region_12.13_spmd.clone, body=%wide.region_11.12_spmd.clone.sunk | while | flops 2625544 | bytes 5284007 | solution.py:28
  709.5 2.6 fusion.69
  712.1 2.6 fusion.69
  714.7 2.6 fusion.69
  717.3 2.6 fusion.69
  719.9 4.1 add_convert_fusion
  724.0 125.1 %all-gather.8.cloned.1.call-done = bf16[1024,4096]{1,0:T(8,128)(2,1)} async-done(((bf16[128,4096]{1,0:T(8,128)(2,1)}), bf16[1024,4096]{1,0:T(8,128)(2,1)}) %all-gather.8.cloned.1.call-update) | async-done | bytes 8388624 | tf_op jit(solution)/shard_map/all_gather | solution.py:114
  849.1 44.0 %while.57 = (s32[]{:T(128)}, f32[8,768]{1,0:T(8,128)S(1)}, s32[8,768]{1,0:T(8,128)S(1)}, bf16[8,128,4096]{2,1,0:T(8,128)(2,1)}, bf16[8,768,4096]{2,1,0:T(8,128)(2,1)}, /*index=5*/s32[]{:T(128)}, s32[]{:T(128)}) while((s32[]{:T(128)}, f32[8,768]{1,0:T(8,128)S(1)}, s32[8,768]{1,0:T(8,128)S(1)}, bf16[8,128,4096]{2,1,0:T(8,128)(2,1)}, ...), condition=%wide.region_15.16_spmd, body=%wide.region_13.15_spmd.sunk | while | flops 805608960 | bytes 7365717 | solution.py:119
  849.1 5.3 fusion.67
  854.6 5.3 fusion.67
  860.1 5.3 fusion.67
  865.7 5.3 fusion.67
  871.2 5.3 fusion.67
  876.7 5.3 fusion.67
  882.2 5.3 fusion.67
  887.7 5.3 fusion.67
  893.2 9.2 all_to_all.37
  902.4 23.0 %gather_fusion.2 = f32[4096]{0:T(1024)S(1)} fusion(f32[6144]{0:T(1024)S(1)} %bitcast.99, s32[4096]{0:T(1024)S(1)} %copy-done.4), kind=kCustom, calls=%fused_computation.2 | custom fusion | bytes 49152 | tf_op jit(solution)/shard_map/jit(_take)/gather | solution.py:121
  (103 shorter events, 14.6 us)
Async XLA Ops:
  14.9 44.3 %copy-start.5 = (bf16[1,128,32]{1,2,0:T(8,128)(2,1)S(1)}, bf16[1,128,32]{1,2,0:T(8,128)(2,1)}, u32[]{:S(2)}) copy-start(bf16[1,128,32]{1,2,0:T(8,128)(2,1)} %param.14) | copy-start | bytes 24580
  59.2 60.3 %copy-start.2 = (s32[4096]{0:T(1024)}, s32[4096]{0:T(1024)S(1)}, u32[]{:S(2)}) copy-start(s32[4096]{0:T(1024)S(1)} %get-tuple-element.475) | copy-start | bytes 49156
  89.9 23.4 %all-to-all-start.1 = ((bf16[8,2,384]{2,1,0:T(2,128)(2,1)}), bf16[8,2,384]{2,1,0:T(2,128)(2,1)S(1)}, u32[]{:S(2)}, u32[]{:S(2)}) async-start(bf16[8,2,384]{2,1,0:T(2,128)(2,1)} %reshape.367), calls=%async_computation.1 | async-start | bytes 24576 | tf_op jit(solution)/shard_map/all_to_all | solution.py:86
  113.2 12.6 %all-to-all-start = ((s32[8,1,768]{2,1,0:T(1,128)}), s32[8,1,768]{2,1,0:T(1,128)S(1)}, u32[]{:S(2)}, u32[]{:S(2)}) async-start(s32[8,1,768]{2,1,0:T(1,128)} %bitcast.18), calls=%async_computation | async-start | bytes 49152 | tf_op jit(solution)/shard_map/all_to_all | solution.py:85
  119.2 506.0 %reduce-scatter.2.cloned.1.call-start = ((), (), s32[]{:S(2)}) async-start(), calls=%async_computation.4 | async-start | bytes 9437184 | tf_op jit(solution)/shard_map/reduce_scatter | solution.py:96
  472.4 152.9 %copy-start.1 = (f32[1,4096]{1,0:T(1,128)S(1)}, f32[1,4096]{1,0:T(1,128)}, u32[]{:S(2)}) copy-start(f32[1,4096]{1,0:T(1,128)} %param.17) | copy-start | bytes 49156
  472.5 187.9 %all-gather.10.cloned.1.call-start = ((), (), s32[]{:S(2)}) async-start(), calls=%async_computation.6 | async-start | bytes 5242880 | tf_op jit(solution)/shard_map/all_gather | solution.py:10
  625.2 84.3 %all-gather.12.cloned.1.call-start = ((), (), s32[]{:S(2)}) async-start(), calls=%async_computation.7 | async-start | bytes 5242880 | tf_op jit(solution)/shard_map/all_gather | solution.py:10
  660.4 10.6 %copy-start = (bf16[1,128,4096]{2,1,0:T(8,128)(2,1)S(1)}, bf16[1,128,4096]{2,1,0:T(8,128)(2,1)}, u32[]{:S(2)}) copy-start(bf16[1,128,4096]{2,1,0:T(8,128)(2,1)} %param.19) | copy-start | bytes 3145732
  674.8 174.3 %all-gather.8.cloned.1.call-start = ((), (), s32[]{:S(2)}) async-start(), calls=%async_computation.5 | async-start | bytes 9437184 | tf_op jit(solution)/shard_map/all_gather | solution.py:114
  849.1 53.3 %copy-start.4 = (s32[4096]{0:T(1024)S(1)}, s32[4096]{0:T(1024)}, u32[]{:S(2)}) copy-start(s32[4096]{0:T(1024)} %get-tuple-element.474) | copy-start | bytes 49156
  902.4 23.0 %copy-start.3 = (s32[4096]{0:T(1024)S(1)}, s32[4096]{0:T(1024)}, u32[]{:S(2)}) copy-start(s32[4096]{0:T(1024)} %copy-done.2) | copy-start | bytes 49156
Sparse Core Ops, SparseCore 0:
  472.6 152.5 reduce-scatter.1
  626.8 33.5 all-gather.9
  674.9 34.4 all-gather.11
  724.1 124.9 all-gather.7
where the time goes:
time: 940 us; the launch traced here: 933 us
  local copies, waits for them, and re-layouts  386 us (41%)
  waiting for transfers between devices  348 us (37%)
  matrix products  80.9 us (9%)
  other arithmetic  75.3 us (8%)
  blocking collectives  14.5 us (2%)
  between operations  14 us (1%)
  starting transfers between devices  13.6 us (1%)
    gather x1, local copies, waits for them, and re-layouts, on_device(): row_cache = jnp.take(weights, recv_keys // tok_rows, axis=0)  269 us
    reduce_scatter x1, waiting for transfers between devices, on_device(): lax.psum_scatter(term_blocks.reshape(lax.axis_size('tok') * tok_rows, mod...  153 us
    all_gather x1, waiting for transfers between devices, on_device(): segment = lax.all_gather(grad_low, 'tok', axis=0, tiled=True)  125 us
    all_gather x2, waiting for transfers between devices, prefix(): lax.all_gather(part.astype(kind), axis)  64.4 us
    dot_general x8, matrix products, slot_grads_of(): jnp.einsum('td,cd->tc', grad_block, rows, preferred_element_type=jnp.floa...  42.8 us
    dot_general x8, matrix products, source_term(): return jnp.dot(spread, rows, preferred_element_type=jnp.float32)  38.1 us
    select_n x2, other arithmetic, on_device(): row_cache = jnp.take(weights, recv_keys // tok_rows, axis=0)  33.5 us
    scatter x1, local copies, waits for them, and re-layouts, bucket_lists(): jnp.zeros(owners * capacity, jnp.bfloat16).at[slot_index]  28.6 us
  transfers between devices with their start and end apart: 6, of which 5 were waited for; matrix products, arithmetic and copies ran while one was open for 2% of the time, Pallas kernels for 0%

commit v1 on v0

v1 whole, which is shorter than its diff:
```python
import jax
import jax.numpy as jnp
from jax import lax
from jax.sharding import PartitionSpec as P

LANES = 128


def prefix(shard, axis, combine, identity, reverse):
    length, mine = (lax.axis_size(axis), lax.axis_index(axis))
    everything = jax.tree.map(
        lambda part, kind: lax.all_gather(part.astype(kind), axis),
        shard,
        (jnp.bfloat16, jnp.bfloat16),
    )
    start = jax.tree.map(
        lambda part, zero: jnp.broadcast_to(jnp.asarray(zero, part.dtype), part.shape),
        shard,
        identity,
    )

    def lap(k, before):
        at = length - 1 - k if reverse else k
        reached = at > mine if reverse else at < mine
        new = combine(
            before, jax.tree.map(lambda part, own: part[at].astype(own.dtype), everything, shard)
        )
        return jax.tree.map(lambda a, b: jnp.where(reached, a, b), new, before)

    return lax.fori_loop(0, length, lap, start)


def compose(earlier_part, later_part):
    return (earlier_part[0] * later_part[0], later_part[0] * earlier_part[1] + later_part[1])


def selectors(ids_all, range_size):
    base = lax.axis_index("tok") * range_size
    local = ids_all - base
    inside = (local >= 0) & (local < range_size)
    high = jnp.where(inside, local // LANES, -1)
    low = local % LANES
    high_hot = high[..., None] == jnp.arange(range_size // LANES, dtype=jnp.int32)
    low_hot = low[..., None] == jnp.arange(LANES, dtype=jnp.int32)
    return high_hot, low_hot


def on_device(active_codes, latent_ids, decoder, carry_gain, earlier_sum, targets):
    range_size = decoder.shape[1]
    weights = decoder[0]
    ids_all = lax.all_gather(latent_ids[0], "tok", axis=0, tiled=True)
    codes_all = lax.all_gather(active_codes[0], "tok", axis=0, tiled=True)
    tokens = ids_all.shape[0]
    high_hot, low_hot = selectors(ids_all, range_size)
    coded_high = jnp.where(high_hot, codes_all[..., None], jnp.zeros((), jnp.bfloat16))
    spread = jnp.einsum(
        "tkh,tkl->thl", coded_high, low_hot.astype(jnp.bfloat16), preferred_element_type=jnp.float32
    )
    spread = spread.astype(jnp.bfloat16).reshape(tokens, range_size)
    partial = jnp.dot(spread, weights, preferred_element_type=jnp.float32).astype(jnp.bfloat16)
    decoded = lax.psum_scatter(partial, "tok", scatter_dimension=0, tiled=True).astype(jnp.float32)
    identity = (jnp.ones_like(carry_gain), jnp.zeros_like(decoded))
    ahead_gain, ahead_sum = prefix((carry_gain, decoded), "layer", compose, identity, False)
    recon_full = carry_gain * (ahead_gain * earlier_sum.astype(jnp.float32) + ahead_sum) + decoded
    misfit = recon_full - targets[0].astype(jnp.float32)
    behind_gain, behind_sum = prefix(
        (carry_gain, carry_gain * misfit), "layer", compose, identity, True
    )
    grad_low = (misfit + behind_sum).astype(jnp.bfloat16)
    segment = lax.all_gather(grad_low, "tok", axis=0, tiled=True)
    products = lax.dot_general(
        segment, weights, (((1,), (1,)), ((), ())), preferred_element_type=jnp.float32
    )
    products = products.reshape(tokens, range_size // LANES, LANES)
    picked_low = jnp.einsum(
        "thl,tkl->tkh",
        products,
        low_hot.astype(jnp.float32),
        precision=lax.Precision.HIGHEST,
        preferred_element_type=jnp.float32,
    )
    partial_grad = jnp.sum(jnp.where(high_hot, picked_low, 0.0), axis=-1)
    code_grad = lax.psum_scatter(partial_grad, "tok", scatter_dimension=0, tiled=True)
    return (recon_full.astype(jnp.bfloat16)[None], code_grad[None])


def solution(mesh):
    return jax.shard_map(
        on_device,
        mesh=mesh,
        in_specs=(
            P("layer", "tok", None),
            P("layer", "tok", None),
            P("layer", "tok", None),
            P("layer", None),
            P("tok", None),
            P("layer", "tok", None),
        ),
        out_specs=(P("layer", "tok", None), P("layer", "tok", None)),
        check_vma=False,
    )
```

time: 940 us -> 628 us (0.67)
  local copies, waits for them, and re-layouts: 386 us -> 2.1 us
  waiting for transfers between devices: 348 us -> 398 us
  blocking collectives: 14.5 us -> 63.9 us
  other arithmetic: 75.3 us -> 28.8 us
  matrix products: 80.9 us -> 121 us
  starting transfers between devices: 13.6 us -> 0.38 us
    gather x4 -> x0, local copies, waits for them, and re-layouts: 315 us -> none  [the longest x1 269 us: on_device(): row_cache = jnp.take(weights, recv_keys // tok_rows, axis=0)]
    scatter x3 -> x0, local copies, waits for them, and re-layouts: 60.2 us -> none  [the longest x1 28.6 us: bucket_lists(): jnp.zeros(owners * capacity, jnp.bfloat16).at[slot_index]]
    all_gather x0 -> x2, blocking collectives: none -> 58.7 us  [the longest x1 30.7 us: on_device(): ids_all = lax.all_gather(latent_ids[0], 'tok', axis=0, tiled=True)]
    reduce_scatter x1 -> x2, waiting for transfers between devices: 153 us -> 209 us  [the longest x1 148 us: on_device(): lax.psum_scatter(partial, 'tok', scatter_dimension=0, tiled=True)]
    dot_general x16 -> x4, matrix products: 80.9 us -> 121 us  [the longest x1 43.2 us: on_device(): lax.dot_general(segment, weights, (((1,), (1,)), ((), ())), preferred_ele...]
    select_n x20 -> x1, other arithmetic: 34 us -> 0.14 us  [selectors(): high = jnp.where(inside, local // LANES, -1)]
    all_to_all x2 -> x0, starting transfers between devices: 13.3 us -> none  [the longest x1 7.28 us: on_device(): lax.all_to_all(slot_codes, 'tok', split_axis=0, concat_axis=0, tiled=True)]
  transfers between devices with their start and end apart: 6 -> 5, of which waited for: 5 -> 5; matrix products, arithmetic and copies ran while one was open for 2% -> 0% of each run, Pallas kernels for 0% -> 0%
where the time goes in v1:
time: 628 us
  waiting for transfers between devices  398 us (63%)
  matrix products  121 us (19%)
  blocking collectives  63.9 us (10%)
  other arithmetic  28.8 us (5%)
  between operations  13.9 us (2%)
    reduce_scatter x1, waiting for transfers between devices, on_device(): lax.psum_scatter(partial, 'tok', scatter_dimension=0, tiled=True)  148 us
    all_gather x1, waiting for transfers between devices, on_device(): segment = lax.all_gather(grad_low, 'tok', axis=0, tiled=True)  125 us
    all_gather x2, waiting for transfers between devices, prefix(): lax.all_gather(part.astype(kind), axis)  64.2 us
    reduce_scatter x1, waiting for transfers between devices, on_device(): lax.psum_scatter(partial_grad, 'tok', scatter_dimension=0, tiled=True)  60.3 us
    dot_general x1, matrix products, on_device(): lax.dot_general(segment, weights, (((1,), (1,)), ((), ())), preferred_ele...  43.2 us
    dot_general x1, matrix products, on_device(): jnp.dot(spread, weights, preferred_element_type=jnp.float32)  41.3 us
    all_gather x1, blocking collectives, on_device(): ids_all = lax.all_gather(latent_ids[0], 'tok', axis=0, tiled=True)  30.7 us
    all_gather x1, blocking collectives, on_device(): codes_all = lax.all_gather(active_codes[0], 'tok', axis=0, tiled=True)  28 us
  transfers between devices with their start and end apart: 5, of which 5 were waited for; matrix products, arithmetic and copies ran while one was open for 0% of the time, Pallas kernels for 0%

profile of v1, /device:TPU:0, one launch (start us, length us, event | category | flops | bytes accessed | tf_op | source)
XLA Modules:
  0.0 627.9 jit_solution(14398185224727393191)
XLA Ops:
  7.2 0.0 reduce-scatter.3.cloned.1.call-start
  7.2 28.0 %all-gather.2 = bf16[1,1024,32]{1,2,0:T(8,128)(2,1)S(1)} all-gather(bf16[1,128,32]{1,2,0:T(8,128)(2,1)} %param.10), channel_id=4, replica_groups=mesh['layer'=4,'tok'=8] {'tok'}, dimensions={1}, use_global_device_ids=true | all-gather | bytes 73728 | tf_op jit(solution)/shard_map/all_gather | solution.py:52
  35.2 30.7 %all-gather.1 = s32[1,1024,32]{1,2,0:T(8,128)S(1)} all-gather(s32[1,128,32]{1,2,0:T(8,128)} %param.11), channel_id=3, replica_groups=mesh['layer'=4,'tok'=8] {'tok'}, dimensions={1}, use_global_device_ids=true | all-gather | bytes 147456 | tf_op jit(solution)/shard_map/all_gather | solution.py:51
  65.9 0.2 copy.12
  66.1 0.1 fusion.28
  66.2 0.2 copy.11
  66.4 0.0 copy-start.1
  66.4 0.2 copy.13
  66.6 0.0 copy-start.3
  66.7 9.7 %fusion.21 = bf16[1024,32,128]{2,1,0:T(8,128)(2,1)S(1)} fusion(s32[1024,32]{1,0:T(8,128)S(1)} %copy.13, s32[1024,32]{1,0:T(8,128)S(1)} %copy.11, bf16[1024,32]{1,0:T(8,128)(2,1)S(1)} %copy.12), kind=kOutput, calls=%fused_computation.25 | convolution fusion | flops 278921216 | bytes 8716288 | tf_op jit(solution)/shard_map/tkh,tkl->thl/dot_general | solution.py:56
  76.4 0.0 copy-done.1
  76.4 0.0 copy-done.3
  76.4 41.3 %fusion.16 = bf16[1024,4096]{1,0:T(8,128)(2,1)} fusion(bf16[1,4096,4096]{2,1,0:T(8,128)(2,1)} %param.12, bf16[128,8,32,128]{3,2,1,0:T(8,128)(2,1)S(1)} %bitcast.93), kind=kOutput, calls=%fused_computation.24 | convolution fusion | flops 34363932672 | bytes 50331648 | tf_op jit(solution)/shard_map/dot_general | solution.py:60
  117.7 0.0 copy-start.5
  117.7 0.0 reduce-scatter.3.cloned.1.call-update
  117.7 0.0 all-gather.12.cloned.1.call-start
  117.7 148.4 %reduce-scatter.3.cloned.1.call-done = bf16[128,4096]{1,0:T(8,128)(2,1)} async-done(((bf16[1024,4096]{1,0:T(8,128)(2,1)}), bf16[128,4096]{1,0:T(8,128)(2,1)}) %reduce-scatter.3.cloned.1.call-update) | async-done | bytes 1048592 | tf_op jit(solution)/shard_map/reduce_scatter | solution.py:61
  266.1 0.0 all-gather.12.cloned.1.call-update
  266.2 0.0 all-gather.14.cloned.1.call-start
  266.2 0.0 copy-done.5
  266.3 5.2 all-gather.5
  271.5 29.8 %all-gather.12.cloned.1.call-done = bf16[512,4096]{1,0:T(8,128)(2,1)} async-done(((bf16[128,4096]{1,0:T(8,128)(2,1)}), bf16[512,4096]{1,0:T(8,128)(2,1)}) %all-gather.12.cloned.1.call-update) | async-done | bytes 4194320 | tf_op jit(solution)/shard_map/all_gather | solution.py:12
  301.3 10.5 %while.32 = (s32[]{:T(128)}, f32[1,4096]{1,0:T(1,128)S(1)}, f32[128,4096]{1,0:T(8,128)S(1)}, s32[]{:T(128)}, bf16[4,1,4096]{2,1,0:T(2,128)(2,1)S(1)}, /*index=5*/bf16[4,128,4096]{2,1,0:T(8,128)(2,1)}, s32[]{:T(128)}, s32[]{:T(128)}) while((s32[]{:T(128)}, f32[1,4096]{1,0:T(1,128)S(1)}, f32[128,4096]{1,0:T(8,128)S(1)}, s32[]{:T(128)}, ...), condition=%wide.region_2.3_spmd.clone, body=%wide.region_1.2_spmd.clone.sunk | while | flops 2637828 | bytes 5316731 | solution.py:30
  301.3 2.6 fusion.37
  304.0 2.6 fusion.37
  306.6 2.6 fusion.37
  309.3 2.6 fusion.37
  311.8 0.0 copy-done
  311.8 3.9 multiply_convert_fusion
  315.7 0.0 all-gather.14.cloned.1.call-update
  315.7 0.2 all-gather.10.cloned.1.call-start
  316.0 34.4 %all-gather.14.cloned.1.call-done = bf16[512,4096]{1,0:T(8,128)(2,1)} async-done(((bf16[128,4096]{1,0:T(8,128)(2,1)}), bf16[512,4096]{1,0:T(8,128)(2,1)}) %all-gather.14.cloned.1.call-update) | async-done | bytes 4194320 | tf_op jit(solution)/shard_map/all_gather | solution.py:12
  350.4 10.4 %while.33 = (s32[]{:T(128)}, f32[128,4096]{1,0:T(8,128)S(1)}, s32[]{:T(128)}, bf16[4,1,4096]{2,1,0:T(2,128)(2,1)S(1)}, bf16[4,128,4096]{2,1,0:T(8,128)(2,1)}, /*index=5*/s32[]{:T(128)}, s32[]{:T(128)}, s32[]{:T(128)}, s32[]{:T(128)}) while((s32[]{:T(128)}, f32[128,4096]{1,0:T(8,128)S(1)}, s32[]{:T(128)}, ...), condition=%wide.region_4.5_spmd.clone, body=%wide.region_3.4_spmd.clone.sunk | while | flops 2625544 | bytes 5284015 | solution.py:30
  350.4 2.6 fusion.38
  353.0 2.6 fusion.38
  355.6 2.6 fusion.38
  358.2 2.6 fusion.38
  360.8 4.1 add_convert_fusion
  364.9 0.0 all-gather.10.cloned.1.call-update
  364.9 0.0 reduce-scatter.5.cloned.1.call-start
  364.9 125.0 %all-gather.10.cloned.1.call-done = bf16[1024,4096]{1,0:T(8,128)(2,1)} async-done(((bf16[128,4096]{1,0:T(8,128)(2,1)}), bf16[1024,4096]{1,0:T(8,128)(2,1)}) %all-gather.10.cloned.1.call-update) | async-done | bytes 8388624 | tf_op jit(solution)/shard_map/all_gather | solution.py:70
  490.0 43.2 %fusion.11 = f32[1024,32,128]{2,0,1:T(8,128)} fusion(bf16[32,128,4096]{2,1,0:T(8,128)(2,1)} %bitcast.92, bf16[1024,4096]{1,0:T(8,128)(2,1)} %all-gather.10.cloned.1.call-done), kind=kOutput, calls=%fused_computation.19 | convolution fusion | flops 34359738368 | bytes 58720256 | tf_op jit(solution)/shard_map/dot_general | solution.py:71
  533.2 0.0 copy-done.2
  533.2 0.0 copy-done.4
  533.2 26.4 %select_reduce_fusion = f32[1024,32]{1,0:T(8,128)} fusion(s32[1024,32]{1,0:T(8,128)S(1)} %copy-done.2, f32[1024,32,128]{2,0,1:T(8,128)} %fusion.11, s32[1024,32]{1,0:T(8,128)S(1)} %copy-done.4), kind=kOutput, calls=%fused_computation.12 | convolution fusion | flops 1617920000 | bytes 17170432 | tf_op jit(solution)/shard_map/thl,tkl->tkh/dot_general | solution.py:75
  559.6 0.0 reduce-scatter.5.cloned.1.call-update
  559.6 60.3 %reduce-scatter.5.cloned.1.call-done = f32[128,32]{1,0:T(8,128)} async-done(((f32[1024,32]{1,0:T(8,128)}), f32[128,32]{1,0:T(8,128)}) %reduce-scatter.5.cloned.1.call-update) | async-done | bytes 16400 | tf_op jit(solution)/shard_map/reduce_scatter | solution.py:83
  619.9 1.5 copy.14
  (15 shorter events, 0.3 us)
Async XLA Ops:
  7.2 259.0 %reduce-scatter.3.cloned.1.call-start = ((), (), s32[]{:S(2)}) async-start(), calls=%async_computation.2 | async-start | bytes 9437184 | tf_op jit(solution)/shard_map/reduce_scatter | solution.py:61
  66.4 9.9 %copy-start.1 = (s32[1024,32]{1,0:T(8,128)}, s32[1024,32]{1,0:T(8,128)S(1)}, u32[]{:S(2)}) copy-start(s32[1024,32]{1,0:T(8,128)S(1)} %copy.11) | copy-start | bytes 393220
  66.6 9.7 %copy-start.3 = (s32[1024,32]{1,0:T(8,128)}, s32[1024,32]{1,0:T(8,128)S(1)}, u32[]{:S(2)}) copy-start(s32[1024,32]{1,0:T(8,128)S(1)} %copy.13) | copy-start | bytes 393220
  117.7 148.6 %copy-start.5 = (f32[1,4096]{1,0:T(1,128)S(1)}, f32[1,4096]{1,0:T(1,128)}, u32[]{:S(2)}) copy-start(f32[1,4096]{1,0:T(1,128)} %param.13) | copy-start | bytes 49156
  117.7 183.6 %all-gather.12.cloned.1.call-start = ((), (), s32[]{:S(2)}) async-start(), calls=%async_computation.5 | async-start | bytes 5242880 | tf_op jit(solution)/shard_map/all_gather | solution.py:12
  266.2 84.2 %all-gather.14.cloned.1.call-start = ((), (), s32[]{:S(2)}) async-start(), calls=%async_computation.6 | async-start | bytes 5242880 | tf_op jit(solution)/shard_map/all_gather | solution.py:12
  301.3 10.6 %copy-start = (bf16[1,128,4096]{2,1,0:T(8,128)(2,1)S(1)}, bf16[1,128,4096]{2,1,0:T(8,128)(2,1)}, u32[]{:S(2)}) copy-start(bf16[1,128,4096]{2,1,0:T(8,128)(2,1)} %param.15) | copy-start | bytes 3145732
  315.7 174.3 %all-gather.10.cloned.1.call-start = ((), (), s32[]{:S(2)}) async-start(), calls=%async_computation.3 | async-start | bytes 9437184 | tf_op jit(solution)/shard_map/all_gather | solution.py:70
  364.9 255.0 %reduce-scatter.5.cloned.1.call-start = ((), (), s32[]{:S(2)}) async-start(), calls=%async_computation.4 | async-start | bytes 589824 | tf_op jit(solution)/shard_map/reduce_scatter | solution.py:83
  490.0 43.2 %copy-start.2 = (s32[1024,32]{1,0:T(8,128)S(1)}, s32[1024,32]{1,0:T(8,128)}, u32[]{:S(2)}) copy-start(s32[1024,32]{1,0:T(8,128)} %copy-done.1) | copy-start | bytes 393220
  490.0 43.2 %copy-start.4 = (s32[1024,32]{1,0:T(8,128)S(1)}, s32[1024,32]{1,0:T(8,128)}, u32[]{:S(2)}) copy-start(s32[1024,32]{1,0:T(8,128)} %copy-done.3) | copy-start | bytes 393220
Sparse Core Ops, SparseCore 0:
  117.8 148.2 reduce-scatter.2
  267.8 33.4 all-gather.11
  315.9 34.4 all-gather.13
  365.0 124.9 all-gather.9
  559.8 60.0 reduce-scatter.4

commit v2 on v1

v2 whole, which is shorter than its diff:
```python
import jax
import jax.numpy as jnp
from jax import lax
from jax.sharding import PartitionSpec as P

LANES = 128


def selectors(ids_all, range_size):
    base = lax.axis_index("tok") * range_size
    local = ids_all - base
    inside = (local >= 0) & (local < range_size)
    high = jnp.where(inside, local // LANES, -1)
    low = local % LANES
    high_hot = high[..., None] == jnp.arange(range_size // LANES, dtype=jnp.int32)
    low_hot = low[..., None] == jnp.arange(LANES, dtype=jnp.int32)
    return high_hot, low_hot


def exchange_codes(latent_ids, active_codes):
    owners = lax.axis_size("tok")
    top_count = latent_ids.shape[1]
    packed = jnp.concatenate(
        [latent_ids.astype(jnp.float32), active_codes.astype(jnp.float32)], axis=1
    )
    spread = jnp.broadcast_to(packed[None], (owners,) + packed.shape)
    gathered = lax.all_to_all(spread, "tok", split_axis=0, concat_axis=0, tiled=True)
    gathered = gathered.reshape(-1, 2 * top_count)
    ids_all = gathered[:, :top_count].astype(jnp.int32)
    codes_all = gathered[:, top_count:].astype(jnp.bfloat16)
    return ids_all, codes_all


def layer_chain(decoded, carry_gain, earlier_sum, targets):
    gains = lax.all_gather(carry_gain[0], "layer", axis=0, tiled=False)
    targets_all = lax.all_gather(targets[0], "layer", axis=0, tiled=False)
    decoded_all = lax.all_gather(decoded.astype(jnp.bfloat16), "layer", axis=0, tiled=False)
    layers = gains.shape[0]
    me = lax.axis_index("layer")
    carried = earlier_sum.astype(jnp.float32)
    misfits = []
    recon_own = jnp.zeros_like(decoded)
    for m in range(layers):
        own = me == m
        term = jnp.where(own, decoded, decoded_all[m].astype(jnp.float32))
        carried = term + gains[m][None, :] * carried
        recon_own = jnp.where(own, carried, recon_own)
        misfits.append(carried - targets_all[m].astype(jnp.float32))
    running = misfits[layers - 1]
    grad_own = jnp.where(me == layers - 1, running, jnp.zeros_like(running))
    for m in range(layers - 2, -1, -1):
        running = misfits[m] + gains[m + 1][None, :] * running
        grad_own = jnp.where(me == m, running, grad_own)
    return recon_own, grad_own


def on_device(active_codes, latent_ids, decoder, carry_gain, earlier_sum, targets):
    range_size = decoder.shape[1]
    owners = lax.axis_size("tok")
    weights = decoder[0]
    ids_all, codes_all = exchange_codes(latent_ids[0], active_codes[0])
    tokens = ids_all.shape[0]
    high_hot, low_hot = selectors(ids_all, range_size)
    coded_high = jnp.where(high_hot, codes_all[..., None], jnp.zeros((), jnp.bfloat16))
    spread = jnp.einsum(
        "tkh,tkl->thl", coded_high, low_hot.astype(jnp.bfloat16), preferred_element_type=jnp.float32
    )
    spread = spread.astype(jnp.bfloat16).reshape(tokens, range_size)
    partial = jnp.dot(spread, weights, preferred_element_type=jnp.float32).astype(jnp.bfloat16)
    decoded = lax.psum_scatter(partial, "tok", scatter_dimension=0, tiled=True).astype(jnp.float32)
    recon_full, grad_sum = layer_chain(decoded, carry_gain, earlier_sum, targets)
    grad_low = grad_sum.astype(jnp.bfloat16)
    segment = lax.all_gather(grad_low, "tok", axis=0, tiled=True)
    products = lax.dot_general(
        segment, weights, (((1,), (1,)), ((), ())), preferred_element_type=jnp.float32
    )
    products = products.reshape(tokens, range_size // LANES, LANES)
    picked_low = jnp.einsum(
        "thl,tkl->tkh",
        products,
        low_hot.astype(jnp.float32),
        precision=lax.Precision.HIGHEST,
        preferred_element_type=jnp.float32,
    )
    partial_grad = jnp.sum(jnp.where(high_hot, picked_low, 0.0), axis=-1)
    returned = lax.all_to_all(partial_grad, "tok", split_axis=0, concat_axis=0, tiled=True)
    code_grad = jnp.sum(returned.reshape(owners, -1, returned.shape[1]), axis=0)
    return (recon_full.astype(jnp.bfloat16)[None], code_grad[None])


def solution(mesh):
    return jax.shard_map(
        on_device,
        mesh=mesh,
        in_specs=(
            P("layer", "tok", None),
            P("layer", "tok", None),
            P("layer", "tok", None),
            P("layer", None),
            P("tok", None),
            P("layer", "tok", None),
        ),
        out_specs=(P("layer", "tok", None), P("layer", "tok", None)),
        check_vma=False,
    )
```

time: 628 us -> 481 us (0.77)
  waiting for transfers between devices: 398 us -> 313 us
  blocking collectives: 63.9 us -> 5.43 us
  other arithmetic: 28.8 us -> 12.7 us
  starting transfers between devices: 0.38 us -> 10.8 us
    reduce_scatter x1 -> x0, waiting for transfers between devices: 60.3 us -> none  [on_device(): lax.psum_scatter(partial_grad, 'tok', scatter_dimension=0, tiled=True)]
    all_gather x3 -> x1, blocking collectives: 63.9 us -> 5.43 us  [layer_chain(): gains = lax.all_gather(carry_gain[0], 'layer', axis=0, tiled=False)]
    all_gather x2, waiting for transfers between devices: 64.2 us -> 27.9 us  [the longest x1 27.9 us: layer_chain(): lax.all_gather(decoded.astype(jnp.bfloat16), 'layer', axis=0, tiled=False)]
    select_n x12 -> x1, other arithmetic: 20.7 us -> 0.07 us  [selectors(): low = local % LANES]
    all_to_all x0 -> x2, waiting for transfers between devices: none -> 11.5 us  [the longest x1 8.87 us: exchange_codes(): lax.all_to_all(spread, 'tok', split_axis=0, concat_axis=0, tiled=True)]
    all_to_all x0 -> x2, starting transfers between devices: none -> 10.7 us  [the longest x1 7.28 us: exchange_codes(): lax.all_to_all(spread, 'tok', split_axis=0, concat_axis=0, tiled=True)]
  transfers between devices with their start and end apart: 5 -> 6, of which waited for: 5 -> 5; matrix products, arithmetic and copies ran while one was open for 0% -> 1% of each run, Pallas kernels for 0% -> 0%
where the time goes in v2:
time: 481 us
  waiting for transfers between devices  313 us (65%)
  matrix products  121 us (25%)
  between operations  15.6 us (3%)
  other arithmetic  12.7 us (3%)
  starting transfers between devices  10.8 us (2%)
  blocking collectives  5.43 us (1%)
    reduce_scatter x1, waiting for transfers between devices, on_device(): lax.psum_scatter(partial, 'tok', scatter_dimension=0, tiled=True)  148 us
    all_gather x1, waiting for transfers between devices, on_device(): segment = lax.all_gather(grad_low, 'tok', axis=0, tiled=True)  125 us
    dot_general x1, matrix products, on_device(): lax.dot_general(segment, weights, (((1,), (1,)), ((), ())), preferred_ele...  43.1 us
    dot_general x1, matrix products, on_device(): jnp.dot(spread, weights, preferred_element_type=jnp.float32)  41.3 us
    all_gather x1, waiting for transfers between devices, layer_chain(): lax.all_gather(decoded.astype(jnp.bfloat16), 'layer', axis=0, tiled=False)  27.9 us
    dot_general x1, matrix products, on_device(): jnp.einsum('thl,tkl->tkh', products, low_hot.astype(jnp.float32), precisi...  26.5 us
    dot_general x1, matrix products, on_device(): jnp.einsum('tkh,tkl->thl', coded_high, low_hot.astype(jnp.bfloat16), pref...  9.7 us
  transfers between devices with their start and end apart: 6, of which 5 were waited for; matrix products, arithmetic and copies ran while one was open for 1% of the time, Pallas kernels for 0%

profile of v2, /device:TPU:0, one launch (start us, length us, event | category | flops | bytes accessed | tf_op | source)
XLA Modules:
  0.0 480.9 jit_solution(1451458494283222725)
XLA Ops:
  8.0 0.7 bitcast_convert_fusion
  8.7 0.7 convert_bitcast_fusion
  9.4 0.7 broadcast_in_dim.35
  10.1 7.3 %all-to-all-start = ((f32[8,128,64]{1,2,0:T(8,128)}), f32[8,128,64]{1,2,0:T(8,128)S(1)}, u32[]{:S(2)}, u32[]{:S(2)}) async-start(f32[8,128,64]{1,2,0:T(8,128)} %broadcast_in_dim.35), calls=%async_computation | async-start | bytes 524288 | tf_op jit(solution)/shard_map/all_to_all | solution.py:27
  17.4 0.0 reduce-scatter.2.cloned.1.call-start
  17.5 8.9 %all-to-all-done = f32[8,128,64]{1,2,0:T(8,128)S(1)} async-done(((f32[8,128,64]{1,2,0:T(8,128)}), f32[8,128,64]{1,2,0:T(8,128)S(1)}, u32[]{:S(2)}, u32[]{:S(2)}) %all-to-all-start) | async-done | bytes 262176 | tf_op jit(solution)/shard_map/all_to_all | solution.py:27
  26.4 0.1 fusion.36
  26.5 0.1 add_select_fusion
  26.6 0.2 copy.17
  26.8 0.2 copy.16
  27.0 0.2 copy.18
  27.2 9.7 %fusion.19 = bf16[1024,32,128]{2,1,0:T(8,128)(2,1)S(1)} fusion(s32[1024,32]{1,0:T(8,128)S(1)} %copy.18, s32[1024,32]{1,0:T(8,128)S(1)} %copy.16, bf16[1024,32]{1,0:T(8,128)(2,1)S(1)} %copy.17), kind=kOutput, calls=%fused_computation.17 | convolution fusion | flops 278921216 | bytes 8716288 | tf_op jit(solution)/shard_map/tkh,tkl->thl/dot_general | solution.py:65
  36.9 41.3 %fusion.14 = bf16[1024,4096]{1,0:T(8,128)(2,1)} fusion(bf16[1,4096,4096]{2,1,0:T(8,128)(2,1)} %param.8, bf16[128,8,32,128]{3,2,1,0:T(8,128)(2,1)S(1)} %bitcast.67), kind=kOutput, calls=%fused_computation.16 | convolution fusion | flops 34363932672 | bytes 50331648 | tf_op jit(solution)/shard_map/dot_general | solution.py:69
  78.2 0.0 reduce-scatter.2.cloned.1.call-update
  78.2 0.0 copy-start.2
  78.3 0.0 copy-start.1
  78.3 0.0 all-gather.6.cloned.1.call-start
  78.3 0.5 all-gather.6.cloned.1.call-update
  78.8 0.0 all-gather.10.cloned.1.call-start
  78.9 147.5 %reduce-scatter.2.cloned.1.call-done = bf16[128,4096]{1,0:T(8,128)(2,1)} async-done(((bf16[1024,4096]{1,0:T(8,128)(2,1)}), bf16[128,4096]{1,0:T(8,128)(2,1)}) %reduce-scatter.2.cloned.1.call-update) | async-done | bytes 1048592 | tf_op jit(solution)/shard_map/reduce_scatter | solution.py:70
  226.4 0.0 all-gather.10.cloned.1.call-update
  226.5 0.0 all-gather.8.cloned.1.call-start
  226.5 0.0 copy-done.2
  226.5 5.4 %all-gather.1 = f32[4,1,4096]{2,1,0:T(1,128)S(1)} all-gather(f32[1,1,4096]{2,1,0:T(1,128)S(1)} %bitcast.64), channel_id=1, replica_groups=mesh['layer'=4,'tok'=8] {'layer'}, dimensions={0}, use_global_device_ids=true | all-gather | bytes 81920 | tf_op jit(solution)/shard_map/all_gather | solution.py:35
  232.0 0.0 all-gather.6.cloned.1.call-done
  232.0 27.9 %all-gather.10.cloned.1.call-done = bf16[512,4096]{1,0:T(8,128)(2,1)} async-done(((bf16[128,4096]{1,0:T(8,128)(2,1)}), bf16[512,4096]{1,0:T(8,128)(2,1)}) %all-gather.10.cloned.1.call-update) | async-done | bytes 4194320 | tf_op jit(solution)/shard_map/all_gather | solution.py:37
  259.9 0.0 copy-done.1
  259.9 5.8 %fusion.34 = bf16[128,4096]{1,0:T(8,128)(2,1)} fusion(bf16[128,4096]{1,0:T(8,128)(2,1)} %reduce-scatter.2.cloned.1.call-done, bf16[128,4096]{1,0:T(8,128)(2,1)S(1)} %copy-done.1, bf16[4,128,4096]{2,1,0:T(8,128)(2,1)} %all-gather.6.cloned.1.call-done, f32[4096]{0:T(1024)S(1)} %bitcast.62, f32[4096]{0:T(1024)S(1)} %bitcast.58, f32[4096]{0:T(1024)S(1)} %bitcast.60, ...), kind=kLoop, calls=%fused_computation.36 | loop fusion | flops 19398656 | bytes 11599876 | tf_op jit(solution)/shard_map/convert_element_type | solution.py:72
  265.7 0.0 all-gather.8.cloned.1.call-update
  265.7 125.1 %all-gather.8.cloned.1.call-done = bf16[1024,4096]{1,0:T(8,128)(2,1)} async-done(((bf16[128,4096]{1,0:T(8,128)(2,1)}), bf16[1024,4096]{1,0:T(8,128)(2,1)}) %all-gather.8.cloned.1.call-update) | async-done | bytes 8388624 | tf_op jit(solution)/shard_map/all_gather | solution.py:73
  390.8 43.1 %fusion.9 = f32[1024,32,128]{2,0,1:T(8,128)} fusion(bf16[32,128,4096]{2,1,0:T(8,128)(2,1)} %bitcast.66, bf16[1024,4096]{1,0:T(8,128)(2,1)} %all-gather.8.cloned.1.call-done), kind=kOutput, calls=%fused_computation.11 | convolution fusion | flops 34359738368 | bytes 58720256 | tf_op jit(solution)/shard_map/dot_general | solution.py:74
  433.9 0.0 copy-start
  433.9 26.5 %select_reduce_fusion = f32[1024,32]{1,0:T(8,128)} fusion(s32[1024,32]{1,0:T(8,128)S(1)} %copy.16, f32[1024,32,128]{2,0,1:T(8,128)} %fusion.9, s32[1024,32]{1,0:T(8,128)S(1)} %copy.18), kind=kOutput, calls=%fused_computation.4 | convolution fusion | flops 1617920000 | bytes 17170432 | tf_op jit(solution)/shard_map/thl,tkl->tkh/dot_general | solution.py:78
  460.4 1.9 copy.21
  462.2 3.4 all-to-all-start.1
  465.6 0.0 copy-done
  465.6 4.7 fusion.35
  470.3 2.6 all-to-all-done.1
  472.9 0.6 reduce_sum.19
  (4 shorter events, 0.0 us)
Async XLA Ops:
  10.1 16.2 %all-to-all-start = ((f32[8,128,64]{1,2,0:T(8,128)}), f32[8,128,64]{1,2,0:T(8,128)S(1)}, u32[]{:S(2)}, u32[]{:S(2)}) async-start(f32[8,128,64]{1,2,0:T(8,128)} %broadcast_in_dim.35), calls=%async_computation | async-start | bytes 524288 | tf_op jit(solution)/shard_map/all_to_all | solution.py:27
  17.4 209.0 %reduce-scatter.2.cloned.1.call-start = ((), (), s32[]{:S(2)}) async-start(), calls=%async_computation.3 | async-start | bytes 9437184 | tf_op jit(solution)/shard_map/reduce_scatter | solution.py:70
  78.2 148.3 %copy-start.2 = (f32[1,4096]{1,0:T(1,128)S(1)}, f32[1,4096]{1,0:T(1,128)}, u32[]{:S(2)}) copy-start(f32[1,4096]{1,0:T(1,128)} %param.9) | copy-start | bytes 49156
  78.3 181.6 %copy-start.1 = (bf16[128,4096]{1,0:T(8,128)(2,1)S(1)}, bf16[128,4096]{1,0:T(8,128)(2,1)}, u32[]{:S(2)}) copy-start(bf16[128,4096]{1,0:T(8,128)(2,1)} %param.10) | copy-start | bytes 3145732
  78.3 153.7 %all-gather.6.cloned.1.call-start = ((), (), s32[]{:S(2)}) async-start(), calls=%async_computation.4 | async-start | bytes 5242880 | tf_op jit(solution)/shard_map/all_gather | solution.py:36
  78.8 181.0 %all-gather.10.cloned.1.call-start = ((), (), s32[]{:S(2)}) async-start(), calls=%async_computation.6 | async-start | bytes 5242880 | tf_op jit(solution)/shard_map/all_gather | solution.py:37
  226.5 164.3 %all-gather.8.cloned.1.call-start = ((), (), s32[]{:S(2)}) async-start(), calls=%async_computation.5 | async-start | bytes 9437184 | tf_op jit(solution)/shard_map/all_gather | solution.py:73
  433.9 31.7 %copy-start = (bf16[128,4096]{1,0:T(8,128)(2,1)S(1)}, bf16[128,4096]{1,0:T(8,128)(2,1)}, u32[]{:S(2)}) copy-start(bf16[128,4096]{1,0:T(8,128)(2,1)} %reduce-scatter.2.cloned.1.call-done) | copy-start | bytes 3145732
  462.2 10.7 %all-to-all-start.1 = ((f32[8,128,32]{1,2,0:T(8,128)}), f32[8,128,32]{1,2,0:T(8,128)S(1)}, u32[]{:S(2)}, u32[]{:S(2)}) async-start(f32[8,128,32]{1,2,0:T(8,128)} %copy.21), calls=%async_computation.2 | async-start | bytes 262144 | tf_op jit(solution)/shard_map/all_to_all | solution.py:86
Sparse Core Ops, SparseCore 0:
  78.4 148.0 reduce-scatter.1
  265.8 124.9 all-gather.7
Sparse Core Ops, SparseCore 1:
  80.4 33.3 all-gather.5
  226.5 33.3 all-gather.9

commit v3 on v2

--- a/solution.py
+++ b/solution.py
@@ -4,6 +4,7 @@
 from jax.sharding import PartitionSpec as P
 
 LANES = 128
+CHUNKS = 4
 
 
 def selectors(ids_all, range_size):
@@ -31,9 +32,7 @@
     return ids_all, codes_all
 
 
-def layer_chain(decoded, carry_gain, earlier_sum, targets):
-    gains = lax.all_gather(carry_gain[0], "layer", axis=0, tiled=False)
-    targets_all = lax.all_gather(targets[0], "layer", axis=0, tiled=False)
+def layer_chain(decoded, gains, earlier_sum, targets_all):
     decoded_all = lax.all_gather(decoded.astype(jnp.bfloat16), "layer", axis=0, tiled=False)
     layers = gains.shape[0]
     me = lax.axis_index("layer")
@@ -66,14 +65,28 @@
         "tkh,tkl->thl", coded_high, low_hot.astype(jnp.bfloat16), preferred_element_type=jnp.float32
     )
     spread = spread.astype(jnp.bfloat16).reshape(tokens, range_size)
-    partial = jnp.dot(spread, weights, preferred_element_type=jnp.float32).astype(jnp.bfloat16)
-    decoded = lax.psum_scatter(partial, "tok", scatter_dimension=0, tiled=True).astype(jnp.float32)
-    recon_full, grad_sum = layer_chain(decoded, carry_gain, earlier_sum, targets)
-    grad_low = grad_sum.astype(jnp.bfloat16)
-    segment = lax.all_gather(grad_low, "tok", axis=0, tiled=True)
-    products = lax.dot_general(
-        segment, weights, (((1,), (1,)), ((), ())), preferred_element_type=jnp.float32
-    )
+    width = weights.shape[1]
+    pieces = CHUNKS if width % (CHUNKS * LANES) == 0 else 1
+    step = width // pieces
+    gains = lax.all_gather(carry_gain[0], "layer", axis=0, tiled=False)
+    targets_all = lax.all_gather(targets[0], "layer", axis=0, tiled=False)
+    recon_parts = []
+    products = None
+    for c in range(pieces):
+        cols = slice(c * step, (c + 1) * step)
+        w_part = weights[:, cols]
+        partial = jnp.dot(spread, w_part, preferred_element_type=jnp.float32).astype(jnp.bfloat16)
+        decoded = lax.psum_scatter(partial, "tok", scatter_dimension=0, tiled=True).astype(jnp.float32)
+        recon_part, grad_part = layer_chain(
+            decoded, gains[:, cols], earlier_sum[:, cols], targets_all[:, :, cols]
+        )
+        recon_parts.append(recon_part.astype(jnp.bfloat16))
+        segment = lax.all_gather(grad_part.astype(jnp.bfloat16), "tok", axis=0, tiled=True)
+        term = lax.dot_general(
+            segment, w_part, (((1,), (1,)), ((), ())), preferred_element_type=jnp.float32
+        )
+        products = term if products is None else products + term
+    recon_full = jnp.concatenate(recon_parts, axis=1)
     products = products.reshape(tokens, range_size // LANES, LANES)
     picked_low = jnp.einsum(
         "thl,tkl->tkh",
@@ -85,7 +98,7 @@
     partial_grad = jnp.sum(jnp.where(high_hot, picked_low, 0.0), axis=-1)
     returned = lax.all_to_all(partial_grad, "tok", split_axis=0, concat_axis=0, tiled=True)
     code_grad = jnp.sum(returned.reshape(owners, -1, returned.shape[1]), axis=0)
-    return (recon_full.astype(jnp.bfloat16)[None], code_grad[None])
+    return (recon_full[None], code_grad[None])
 
 
 def solution(mesh):

time: 481 us -> 724 us (1.51); the launches traced: 481 us -> 716 us
  waiting for transfers between devices: 313 us -> 474 us
  matrix products: 121 us -> 164 us
  local copies, waits for them, and re-layouts: 3.2 us -> 15 us
  starting transfers between devices: 10.8 us -> 22 us
  other arithmetic: 12.7 us -> 21.6 us
    reduce_scatter x1 -> x4, waiting for transfers between devices: 148 us -> 232 us  [on_device(): lax.psum_scatter(partial, 'tok', scatter_dimension=0, tiled=True)]
    all_gather x2 -> x5, waiting for transfers between devices: 125 us -> 184 us  [the longest x4 148 us: on_device(): lax.all_gather(grad_part.astype(jnp.bfloat16), 'tok', axis=0, tiled=True)]
    dot_general x2 -> x8, matrix products: 84.4 us -> 134 us  [the longest x4 76.3 us: on_device(): lax.dot_general(segment, w_part, (((1,), (1,)), ((), ())), preferred_elem...]
    all_gather x1 -> x4, waiting for transfers between devices: 27.9 us -> 42.1 us  [layer_chain(): lax.all_gather(decoded.astype(jnp.bfloat16), 'layer', axis=0, tiled=False)]
    unnamed x6 -> x26, local copies, waits for them, and re-layouts: 0.02 us -> 12.9 us
    convert_element_type x1 -> x8, other arithmetic: 5.77 us -> 18.3 us  [the longest x4 11.8 us: on_device(): grad_part.astype(jnp.bfloat16)]
    all_gather x2 -> x5, starting transfers between devices: 0.08 us -> 10.8 us  [the longest x4 10.8 us: on_device(): lax.all_gather(grad_part.astype(jnp.bfloat16), 'tok', axis=0, tiled=True)]
  transfers between devices with their start and end apart: 6 -> 15, of which waited for: 5 -> 15; matrix products, arithmetic and copies ran while one was open for 1% -> 16% of each run, Pallas kernels for 0% -> 0%
where the time goes in v3:
time: 724 us; the launch traced here: 716 us
  waiting for transfers between devices  474 us (65%)
  matrix products  164 us (23%)
  starting transfers between devices  22 us (3%)
  other arithmetic  21.6 us (3%)
  local copies, waits for them, and re-layouts  15 us (2%)
  between operations  14.4 us (2%)
    reduce_scatter x4, waiting for transfers between devices, on_device(): lax.psum_scatter(partial, 'tok', scatter_dimension=0, tiled=True)  232 us
    all_gather x4, waiting for transfers between devices, on_device(): lax.all_gather(grad_part.astype(jnp.bfloat16), 'tok', axis=0, tiled=True)  148 us
    dot_general x4, matrix products, on_device(): lax.dot_general(segment, w_part, (((1,), (1,)), ((), ())), preferred_elem...  76.3 us
    dot_general x4, matrix products, on_device(): jnp.dot(spread, w_part, preferred_element_type=jnp.float32)  57.2 us
    all_gather x4, waiting for transfers between devices, layer_chain(): lax.all_gather(decoded.astype(jnp.bfloat16), 'layer', axis=0, tiled=False)  42.1 us
    all_gather x1, waiting for transfers between devices, on_device(): targets_all = lax.all_gather(targets[0], 'layer', axis=0, tiled=False)  35.9 us
    dot_general x1, matrix products, on_device(): jnp.einsum('thl,tkl->tkh', products, low_hot.astype(jnp.float32), precisi...  20.6 us
  transfers between devices with their start and end apart: 15, of which 15 were waited for; matrix products, arithmetic and copies ran while one was open for 16% of the time, Pallas kernels for 0%

profile of v3, /device:TPU:0, one launch (start us, length us, event | category | flops | bytes accessed | tf_op | source)
XLA Modules:
  0.0 715.8 jit_solution(8392312445711496544)
XLA Ops:
  7.2 0.7 bitcast_convert_fusion
  7.9 0.7 convert_bitcast_fusion
  8.6 0.7 broadcast_in_dim.35
  9.3 7.3 %all-to-all-start = ((f32[8,128,64]{1,2,0:T(8,128)}), f32[8,128,64]{1,2,0:T(8,128)S(1)}, u32[]{:S(2)}, u32[]{:S(2)}) async-start(f32[8,128,64]{1,2,0:T(8,128)} %broadcast_in_dim.35), calls=%async_computation | async-start | bytes 524288 | tf_op jit(solution)/shard_map/all_to_all | solution.py:28
  16.6 8.9 %all-to-all-done = f32[8,128,64]{1,2,0:T(8,128)S(1)} async-done(((f32[8,128,64]{1,2,0:T(8,128)}), f32[8,128,64]{1,2,0:T(8,128)S(1)}, u32[]{:S(2)}, u32[]{:S(2)}) %all-to-all-start) | async-done | bytes 262176 | tf_op jit(solution)/shard_map/all_to_all | solution.py:28
  25.9 0.2 copy.15
  26.4 9.7 %fusion.26 = bf16[1024,32,128]{2,1,0:T(8,128)(2,1)S(1)} fusion(s32[1024,32]{1,0:T(8,128)S(1)} %copy.17, s32[1024,32]{1,0:T(8,128)S(1)} %copy.15, bf16[1024,32]{1,0:T(8,128)(2,1)S(1)} %copy.16), kind=kOutput, calls=%fused_computation.29 | convolution fusion | flops 278921216 | bytes 8716288 | tf_op jit(solution)/shard_map/tkh,tkl->thl/dot_general | solution.py:64
  36.1 3.3 copy-done.11
  39.4 12.5 %fusion.40 = bf16[1024,1024]{1,0:T(8,128)(2,1)} fusion(bf16[4096,4096]{1,0:T(8,128)(2,1)} %bitcast.178, bf16[128,8,32,128]{3,2,1,0:T(8,128)(2,1)S(1)} %bitcast.186), kind=kOutput, calls=%fused_computation.37 | convolution fusion | flops 8590983168 | bytes 18874368 | tf_op jit(solution)/shard_map/dot_general | solution.py:78
  52.0 14.8 %fusion.35 = bf16[1024,1024]{1,0:T(8,128)(2,1)} fusion(bf16[4096,4096]{1,0:T(8,128)(2,1)} %bitcast.179, bf16[128,8,32,128]{3,2,1,0:T(8,128)(2,1)} %bitcast.187), kind=kOutput, calls=%fused_computation.36 | convolution fusion | flops 8590983168 | bytes 18874368 | tf_op jit(solution)/shard_map/dot_general | solution.py:78
  66.8 0.3 reduce-scatter.9.cloned.1.call-start
  67.1 14.9 %fusion.45 = bf16[1024,1024]{1,0:T(8,128)(2,1)} fusion(bf16[4096,4096]{1,0:T(8,128)(2,1)} %bitcast.180, bf16[128,8,32,128]{3,2,1,0:T(8,128)(2,1)} %bitcast.188), kind=kOutput, calls=%fused_computation.38 | convolution fusion | flops 8590983168 | bytes 18874368 | tf_op jit(solution)/shard_map/dot_general | solution.py:78
  82.1 15.0 %fusion.50 = bf16[1024,1024]{1,0:T(8,128)(2,1)} fusion(bf16[4096,4096]{1,0:T(8,128)(2,1)} %bitcast.181, bf16[128,8,32,128]{3,2,1,0:T(8,128)(2,1)} %bitcast.189), kind=kOutput, calls=%fused_computation.39 | convolution fusion | flops 8590983168 | bytes 18874368 | tf_op jit(solution)/shard_map/dot_general | solution.py:78
  97.1 21.5 %reduce-scatter.7.cloned.1.call-done = bf16[128,1024]{1,0:T(8,128)(2,1)} async-done(((bf16[1024,1024]{1,0:T(8,128)(2,1)}), bf16[128,1024]{1,0:T(8,128)(2,1)}) %reduce-scatter.7.cloned.1.call-update) | async-done | bytes 262160 | tf_op jit(solution)/shard_map/reduce_scatter | solution.py:79
  118.7 0.5 all-gather.15.cloned.1.call-update
  119.3 69.8 %reduce-scatter.5.cloned.1.call-done = bf16[128,1024]{1,0:T(8,128)(2,1)} async-done(((bf16[1024,1024]{1,0:T(8,128)(2,1)}), bf16[128,1024]{1,0:T(8,128)(2,1)}) %reduce-scatter.5.cloned.1.call-update) | async-done | bytes 262160 | tf_op jit(solution)/shard_map/reduce_scatter | solution.py:79
  189.2 70.3 %reduce-scatter.9.cloned.1.call-done = bf16[128,1024]{1,0:T(8,128)(2,1)} async-done(((bf16[1024,1024]{1,0:T(8,128)(2,1)}), bf16[128,1024]{1,0:T(8,128)(2,1)}) %reduce-scatter.9.cloned.1.call-update) | async-done | bytes 262160 | tf_op jit(solution)/shard_map/reduce_scatter | solution.py:79
  259.6 70.0 %reduce-scatter.11.cloned.1.call-done = bf16[128,1024]{1,0:T(8,128)(2,1)} async-done(((bf16[1024,1024]{1,0:T(8,128)(2,1)}), bf16[128,1024]{1,0:T(8,128)(2,1)}) %reduce-scatter.11.cloned.1.call-update) | async-done | bytes 262160 | tf_op jit(solution)/shard_map/reduce_scatter | solution.py:79
  329.7 5.2 all-gather.4
  335.0 11.7 %all-gather.27.cloned.1.call-done = bf16[512,1024]{1,0:T(8,128)(2,1)} async-done(((bf16[128,1024]{1,0:T(8,128)(2,1)}), bf16[512,1024]{1,0:T(8,128)(2,1)}) %all-gather.27.cloned.1.call-update) | async-done | bytes 1048592 | tf_op jit(solution)/shard_map/all_gather | solution.py:36
  346.7 35.9 %all-gather.15.cloned.1.call-done = bf16[4,128,4096]{2,1,0:T(8,128)(2,1)} async-done(((bf16[1,128,4096]{2,1,0:T(8,128)(2,1)}), bf16[4,128,4096]{2,1,0:T(8,128)(2,1)}) %all-gather.15.cloned.1.call-update) | async-done | bytes 4194320 | tf_op jit(solution)/shard_map/all_gather | solution.py:72
  382.6 3.0 fusion.85
  385.7 15.3 %all-gather.25.cloned.1.call-done = bf16[512,1024]{1,0:T(8,128)(2,1)} async-done(((bf16[128,1024]{1,0:T(8,128)(2,1)}), bf16[512,1024]{1,0:T(8,128)(2,1)}) %all-gather.25.cloned.1.call-update) | async-done | bytes 1048592 | tf_op jit(solution)/shard_map/all_gather | solution.py:36
  400.9 3.0 fusion.90
  404.0 10.6 %all-gather.21.cloned.1.call-start = ((), (), s32[]{:S(2)}) async-start(), calls=%async_computation.13 | async-start | bytes 2359296 | tf_op jit(solution)/shard_map/all_gather | solution.py:84
  414.6 4.6 all-gather.29.cloned.1.call-done
  419.3 2.9 fusion.80
  422.3 2.4 select_convert_fusion.1
  424.6 1.1 select_convert_fusion.2
  425.7 1.4 select_convert_fusion.3
  427.1 10.5 %all-gather.31.cloned.1.call-done = bf16[512,1024]{1,0:T(8,128)(2,1)} async-done(((bf16[128,1024]{1,0:T(8,128)(2,1)}), bf16[512,1024]{1,0:T(8,128)(2,1)}) %all-gather.31.cloned.1.call-update) | async-done | bytes 1048592 | tf_op jit(solution)/shard_map/all_gather | solution.py:36
  437.6 1.7 select_convert_fusion
  439.2 2.9 fusion.75
  442.2 46.7 %all-gather.19.cloned.1.call-done = bf16[1024,1024]{1,0:T(8,128)(2,1)} async-done(((bf16[128,1024]{1,0:T(8,128)(2,1)}), bf16[1024,1024]{1,0:T(8,128)(2,1)}) %all-gather.19.cloned.1.call-update) | async-done | bytes 2097168 | tf_op jit(solution)/shard_map/all_gather | solution.py:84
  488.9 16.1 %fusion.20 = f32[1024,4096]{1,0:T(8,128)} fusion(bf16[1024,1024]{1,0:T(8,128)(2,1)} %all-gather.19.cloned.1.call-done, bf16[4096,4096]{1,0:T(8,128)(2,1)} %bitcast.182), kind=kOutput, calls=%fused_computation.23 | convolution fusion | flops 8589934592 | bytes 27262976 | tf_op jit(solution)/shard_map/dot_general | solution.py:85
  504.9 33.9 %all-gather.17.cloned.1.call-done = bf16[1024,1024]{1,0:T(8,128)(2,1)} async-done(((bf16[128,1024]{1,0:T(8,128)(2,1)}), bf16[1024,1024]{1,0:T(8,128)(2,1)}) %all-gather.17.cloned.1.call-update) | async-done | bytes 2097168 | tf_op jit(solution)/shard_map/all_gather | solution.py:84
  538.8 16.0 %fusion.23 = f32[1024,4096]{1,0:T(8,128)} fusion(bf16[1024,1024]{1,0:T(8,128)(2,1)} %all-gather.17.cloned.1.call-done, bf16[4096,4096]{1,0:T(8,128)(2,1)} %bitcast.183), kind=kOutput, calls=%fused_computation.26 | convolution fusion | flops 8589934592 | bytes 27262976 | tf_op jit(solution)/shard_map/dot_general | solution.py:85
  554.9 33.7 %all-gather.21.cloned.1.call-done = bf16[1024,1024]{1,0:T(8,128)(2,1)} async-done(((bf16[128,1024]{1,0:T(8,128)(2,1)}), bf16[1024,1024]{1,0:T(8,128)(2,1)}) %all-gather.21.cloned.1.call-update) | async-done | bytes 2097168 | tf_op jit(solution)/shard_map/all_gather | solution.py:84
  588.6 16.0 %fusion.17 = f32[1024,4096]{1,0:T(8,128)} fusion(bf16[1024,1024]{1,0:T(8,128)(2,1)} %all-gather.21.cloned.1.call-done, bf16[4096,4096]{1,0:T(8,128)(2,1)} %bitcast.184), kind=kOutput, calls=%fused_computation.20 | convolution fusion | flops 8589934592 | bytes 27262976 | tf_op jit(solution)/shard_map/dot_general | solution.py:85
  604.6 33.9 %all-gather.23.cloned.1.call-done = bf16[1024,1024]{1,0:T(8,128)(2,1)} async-done(((bf16[128,1024]{1,0:T(8,128)(2,1)}), bf16[1024,1024]{1,0:T(8,128)(2,1)}) %all-gather.23.cloned.1.call-update) | async-done | bytes 2097168 | tf_op jit(solution)/shard_map/all_gather | solution.py:84
  638.5 28.2 %add_bitcast_fusion = f32[128,8,32,128]{3,1,2,0:T(8,128)} fusion(f32[1024,4096]{1,0:T(8,128)} %fusion.17, f32[1024,4096]{1,0:T(8,128)} %fusion.23, f32[1024,4096]{1,0:T(8,128)} %fusion.20, bf16[1024,1024]{1,0:T(8,128)(2,1)} %all-gather.23.cloned.1.call-done, bf16[4096,4096]{1,0:T(8,128)(2,1)} %bitcast.185), kind=kOutput, calls=%fused_computation.1 | convolution fusion | flops 8602517504 | bytes 77594624 | tf_op jit(solution)/shard_map/dot_general | solution.py:85
  666.8 9.5 %copy.25 = f32[128,8,32,128]{3,2,1,0:T(8,128)S(1)} copy(f32[128,8,32,128]{3,1,2,0:T(8,128)} %add_bitcast_fusion) | data formatting | bytes 33554432
  676.3 20.6 %select_reduce_fusion = f32[1024,32]{1,0:T(8,128)S(1)} fusion(s32[1024,32]{1,0:T(8,128)S(1)} %copy-done.7, f32[1024,32,128]{2,1,0:T(8,128)S(1)} %bitcast.141, s32[1024,32]{1,0:T(8,128)S(1)} %copy-done.9), kind=kOutput, calls=%fused_computation | convolution fusion | flops 1617920000 | bytes 17170432 | tf_op jit(solution)/shard_map/thl,tkl->tkh/dot_general | solution.py:91
  696.9 0.8 copy.19
  697.7 3.4 all-to-all-start.1
  701.1 1.0 maximum_bitcast_fusion
  702.2 6.2 all-to-all-done.1
  708.4 0.6 reduce_sum.19
  (55 shorter events, 1.4 us)
Async XLA Ops:
  9.3 16.2 %all-to-all-start = ((f32[8,128,64]{1,2,0:T(8,128)}), f32[8,128,64]{1,2,0:T(8,128)S(1)}, u32[]{:S(2)}, u32[]{:S(2)}) async-start(f32[8,128,64]{1,2,0:T(8,128)} %broadcast_in_dim.35), calls=%async_computation | async-start | bytes 524288 | tf_op jit(solution)/shard_map/all_to_all | solution.py:28
  16.6 102.0 %reduce-scatter.7.cloned.1.call-start = ((), (), s32[]{:S(2)}) async-start(), calls=%async_computation.7 | async-start | bytes 2359296 | tf_op jit(solution)/shard_map/reduce_scatter | solution.py:79
  26.1 9.9 %copy-start.6 = (s32[1024,32]{1,0:T(8,128)}, s32[1024,32]{1,0:T(8,128)S(1)}, u32[]{:S(2)}) copy-start(s32[1024,32]{1,0:T(8,128)S(1)} %copy.15) | copy-start | bytes 393220
  26.4 9.7 %copy-start.8 = (s32[1024,32]{1,0:T(8,128)}, s32[1024,32]{1,0:T(8,128)S(1)}, u32[]{:S(2)}) copy-start(s32[1024,32]{1,0:T(8,128)S(1)} %copy.17) | copy-start | bytes 393220
  36.1 3.3 copy-start.11
  51.9 137.2 %reduce-scatter.5.cloned.1.call-start = ((), (), s32[]{:S(2)}) async-start(), calls=%async_computation.6 | async-start | bytes 2359296 | tf_op jit(solution)/shard_map/reduce_scatter | solution.py:79
  66.8 192.7 %reduce-scatter.9.cloned.1.call-start = ((), (), s32[]{:S(2)}) async-start(), calls=%async_computation.8 | async-start | bytes 2359296 | tf_op jit(solution)/shard_map/reduce_scatter | solution.py:79
  82.0 247.6 %copy-start.10 = (f32[1,4096]{1,0:T(1,128)S(1)}, f32[1,4096]{1,0:T(1,128)}, u32[]{:S(2)}) copy-start(f32[1,4096]{1,0:T(1,128)} %param.9) | copy-start | bytes 49156
  82.1 300.6 %copy-start = (bf16[128,4096]{1,0:T(8,128)(2,1)S(1)}, bf16[128,4096]{1,0:T(8,128)(2,1)}, u32[]{:S(2)}) copy-start(bf16[128,4096]{1,0:T(8,128)(2,1)} %param.10) | copy-start | bytes 3145732
  82.1 247.5 %reduce-scatter.11.cloned.1.call-start = ((), (), s32[]{:S(2)}) async-start(), calls=%async_computation.9 | async-start | bytes 2359296 | tf_op jit(solution)/shard_map/reduce_scatter | solution.py:79
  97.1 249.6 %all-gather.27.cloned.1.call-start = ((), (), s32[]{:S(2)}) async-start(), calls=%async_computation.16 | async-start | bytes 1310720 | tf_op jit(solution)/shard_map/all_gather | solution.py:36
  118.6 306.0 %copy-start.3 = (bf16[128,1024]{1,0:T(8,128)(2,1)S(1)}, bf16[128,1024]{1,0:T(8,128)(2,1)}, u32[]{:S(2)}) copy-start(bf16[128,1024]{1,0:T(8,128)(2,1)} %reduce-scatter.7.cloned.1.call-done) | copy-start | bytes 786436
  118.6 264.0 %all-gather.15.cloned.1.call-start = ((), (), s32[]{:S(2)}) async-start(), calls=%async_computation.10 | async-start | bytes 5242880 | tf_op jit(solution)/shard_map/all_gather | solution.py:72
  119.2 281.7 %all-gather.25.cloned.1.call-start = ((), (), s32[]{:S(2)}) async-start(), calls=%async_computation.15 | async-start | bytes 1310720 | tf_op jit(solution)/shard_map/all_gather | solution.py:36
  189.1 230.1 %all-gather.29.cloned.1.call-start = ((), (), s32[]{:S(2)}) async-start(), calls=%async_computation.17 | async-start | bytes 1310720 | tf_op jit(solution)/shard_map/all_gather | solution.py:36
  259.5 178.1 %all-gather.31.cloned.1.call-start = ((), (), s32[]{:S(2)}) async-start(), calls=%async_computation.18 | async-start | bytes 1310720 | tf_op jit(solution)/shard_map/all_gather | solution.py:36
  329.6 159.3 %all-gather.19.cloned.1.call-start = ((), (), s32[]{:S(2)}) async-start(), calls=%async_computation.12 | async-start | bytes 2359296 | tf_op jit(solution)/shard_map/all_gather | solution.py:84
  346.7 77.9 %copy-start.1 = (bf16[512,1024]{1,0:T(8,128)(2,1)S(1)}, bf16[512,1024]{1,0:T(8,128)(2,1)}, u32[]{:S(2)}) copy-start(bf16[512,1024]{1,0:T(8,128)(2,1)} %all-gather.27.cloned.1.call-done) | copy-start | bytes 3145732
  385.6 153.2 %all-gather.17.cloned.1.call-start = ((), (), s32[]{:S(2)}) async-start(), calls=%async_computation.11 | async-start | bytes 2359296 | tf_op jit(solution)/shard_map/all_gather | solution.py:84
  400.9 24.8 %copy-start.2 = (bf16[512,1024]{1,0:T(8,128)(2,1)S(1)}, bf16[512,1024]{1,0:T(8,128)(2,1)}, u32[]{:S(2)}) copy-start(bf16[512,1024]{1,0:T(8,128)(2,1)} %all-gather.25.cloned.1.call-done) | copy-start | bytes 3145732
  404.0 184.6 %all-gather.21.cloned.1.call-start = ((), (), s32[]{:S(2)}) async-start(), calls=%async_computation.13 | async-start | bytes 2359296 | tf_op jit(solution)/shard_map/all_gather | solution.py:84
  422.2 216.3 %all-gather.23.cloned.1.call-start = ((), (), s32[]{:S(2)}) async-start(), calls=%async_computation.14 | async-start | bytes 2359296 | tf_op jit(solution)/shard_map/all_gather | solution.py:84
  666.8 9.5 %copy-start.7 = (s32[1024,32]{1,0:T(8,128)S(1)}, s32[1024,32]{1,0:T(8,128)}, u32[]{:S(2)}) copy-start(s32[1024,32]{1,0:T(8,128)} %copy-done.6) | copy-start | bytes 393220
  666.8 9.5 %copy-start.9 = (s32[1024,32]{1,0:T(8,128)S(1)}, s32[1024,32]{1,0:T(8,128)}, u32[]{:S(2)}) copy-start(s32[1024,32]{1,0:T(8,128)} %copy-done.8) | copy-start | bytes 393220
  676.3 24.8 %copy-start.4 = (bf16[128,1024]{1,0:T(8,128)(2,1)S(1)}, bf16[128,1024]{1,0:T(8,128)(2,1)}, u32[]{:S(2)}) copy-start(bf16[128,1024]{1,0:T(8,128)(2,1)} %select_convert_fusion.1) | copy-start | bytes 786436
  676.3 24.8 %copy-start.5 = (bf16[128,1024]{1,0:T(8,128)(2,1)S(1)}, bf16[128,1024]{1,0:T(8,128)(2,1)}, u32[]{:S(2)}) copy-start(bf16[128,1024]{1,0:T(8,128)(2,1)} %select_convert_fusion.2) | copy-start | bytes 786436
  697.7 10.7 %all-to-all-start.1 = ((f32[8,128,32]{1,2,0:T(8,128)}), f32[8,128,32]{1,2,0:T(8,128)S(1)}, u32[]{:S(2)}, u32[]{:S(2)}) async-start(f32[8,128,32]{1,2,0:T(8,128)} %copy.19), calls=%async_computation.5 | async-start | bytes 262144 | tf_op jit(solution)/shard_map/all_to_all | solution.py:99
Sparse Core Ops, SparseCore 0:
  52.0 66.5 reduce-scatter.6
  122.2 66.9 reduce-scatter.4
  192.6 66.8 reduce-scatter.8
  262.9 66.6 reduce-scatter.10
  331.0 15.6 all-gather.26
  348.1 34.4 all-gather.14
  384.2 16.7 all-gather.24
  402.5 16.7 all-gather.28
  420.8 16.7 all-gather.30
  439.6 49.2 all-gather.18
  491.0 47.7 all-gather.16
  540.8 47.7 all-gather.20
  590.7 47.7 all-gather.22

commit v4 on v2

--- a/solution.py
+++ b/solution.py
@@ -1,3 +1,5 @@
+import functools
+
 import jax
 import jax.numpy as jnp
 from jax import lax
@@ -15,6 +17,78 @@
     high_hot = high[..., None] == jnp.arange(range_size // LANES, dtype=jnp.int32)
     low_hot = low[..., None] == jnp.arange(LANES, dtype=jnp.int32)
     return high_hot, low_hot
+
+
+def ring_order(mesh):
+    count = mesh.shape["tok"]
+    row = mesh.devices.reshape(-1, count)[0]
+    coords = [getattr(device, "coords", None) for device in row]
+    if any(c is None for c in coords):
+        return list(range(count))
+    varying = [d for d in range(len(coords[0])) if len({c[d] for c in coords}) > 1]
+    if len(varying) != 2:
+        return sorted(range(count), key=lambda i: tuple(coords[i]))
+    sizes = [len({c[d] for c in coords}) for d in varying]
+    outer, inner = (1, 0) if sizes[1] % 2 == 0 else (0, 1)
+    place = {(coords[i][varying[outer]], coords[i][varying[inner]]): i for i in range(count)}
+    outer_values = sorted({c[varying[outer]] for c in coords})
+    inner_values = sorted({c[varying[inner]] for c in coords})
+    order = []
+    for n, o in enumerate(outer_values):
+        walk = inner_values if n % 2 == 0 else inner_values[::-1]
+        order.extend(place[(o, i)] for i in walk)
+    return order
+
+
+def ring_tables(ring):
+    count = len(ring)
+    position = [0] * count
+    for p, i in enumerate(ring):
+        position[i] = p
+    forward = [(ring[p], ring[(p + 1) % count]) for p in range(count)]
+    backward = [(ring[(p + 1) % count], ring[p]) for p in range(count)]
+    here = jnp.asarray(position, jnp.int32)[lax.axis_index("tok")]
+    return jnp.asarray(ring, jnp.int32), here, forward, backward
+
+
+def ring_reduce_scatter(partial, ring):
+    count = len(ring)
+    members, here, forward, backward = ring_tables(ring)
+    blocks = partial.reshape(count, -1, partial.shape[1])
+    half = partial.shape[1] // 2
+    sides = ((forward, -1, slice(0, half)), (backward, 1, slice(half, None)))
+    results = []
+    for perm, sign, cols in sides:
+        own = blocks[:, :, cols]
+        first = lax.dynamic_index_in_dim(own, members[(here + sign) % count], 0, keepdims=False)
+        running = first
+        for s in range(count - 1):
+            arrived = lax.ppermute(running, "tok", perm)
+            block = members[(here + sign * (s + 2)) % count]
+            total = arrived.astype(jnp.float32) + lax.dynamic_index_in_dim(
+                own, block, 0, keepdims=False
+            ).astype(jnp.float32)
+            running = total.astype(jnp.bfloat16)
+        results.append(total)
+    return jnp.concatenate(results, axis=1)
+
+
+def ring_all_gather(piece, ring):
+    count = len(ring)
+    members, here, forward, backward = ring_tables(ring)
+    half = piece.shape[1] // 2
+    gathered = jnp.zeros((count,) + piece.shape, piece.dtype)
+    me = lax.axis_index("tok")
+    gathered = lax.dynamic_update_index_in_dim(gathered, piece, me, 0)
+    sides = ((forward, -1, 0, piece[:, :half]), (backward, 1, half, piece[:, half:]))
+    for perm, sign, offset, travelling in sides:
+        for s in range(count - 1):
+            travelling = lax.ppermute(travelling, "tok", perm)
+            source = members[(here + sign * (s + 1)) % count]
+            gathered = lax.dynamic_update_slice(
+                gathered, travelling[None], (source, jnp.int32(0), jnp.int32(offset))
+            )
+    return gathered.reshape(count * piece.shape[0], piece.shape[1])
 
 
 def exchange_codes(latent_ids, active_codes):
@@ -54,7 +128,7 @@
     return recon_own, grad_own
 
 
-def on_device(active_codes, latent_ids, decoder, carry_gain, earlier_sum, targets):
+def on_device(ring, active_codes, latent_ids, decoder, carry_gain, earlier_sum, targets):
     range_size = decoder.shape[1]
     owners = lax.axis_size("tok")
     weights = decoder[0]
@@ -67,10 +141,10 @@
     )
     spread = spread.astype(jnp.bfloat16).reshape(tokens, range_size)
     partial = jnp.dot(spread, weights, preferred_element_type=jnp.float32).astype(jnp.bfloat16)
-    decoded = lax.psum_scatter(partial, "tok", scatter_dimension=0, tiled=True).astype(jnp.float32)
+    decoded = ring_reduce_scatter(partial, ring)
     recon_full, grad_sum = layer_chain(decoded, carry_gain, earlier_sum, targets)
     grad_low = grad_sum.astype(jnp.bfloat16)
-    segment = lax.all_gather(grad_low, "tok", axis=0, tiled=True)
+    segment = ring_all_gather(grad_low, ring)
     products = lax.dot_general(
         segment, weights, (((1,), (1,)), ((), ())), preferred_element_type=jnp.float32
     )
@@ -89,8 +163,9 @@
 
 
 def solution(mesh):
+    ring = ring_order(mesh)
     return jax.shard_map(
-        on_device,
+        functools.partial(on_device, ring),
         mesh=mesh,
         in_specs=(
             P("layer", "tok", None),

time: 481 us -> 575 us (1.20)
  starting transfers between devices: 10.8 us -> 160 us
  waiting for transfers between devices: 313 us -> 176 us
  between operations: 15.6 us -> 54.6 us
  local copies, waits for them, and re-layouts: 3.2 us -> 30.5 us
  other arithmetic: 12.7 us -> 26.8 us
    reduce_scatter x1 -> x0, waiting for transfers between devices: 148 us -> none  [on_device(): lax.psum_scatter(partial, 'tok', scatter_dimension=0, tiled=True)]
    ppermute x0 -> x28, starting transfers between devices: none -> 142 us  [the longest x14 79.6 us: ring_reduce_scatter(): arrived = lax.ppermute(running, 'tok', perm)]
    ppermute x0 -> x28, waiting for transfers between devices: none -> 128 us  [the longest x14 95.3 us: ring_all_gather(): travelling = lax.ppermute(travelling, 'tok', perm)]
    all_gather x1 -> x0, waiting for transfers between devices: 125 us -> none  [on_device(): segment = lax.all_gather(grad_low, 'tok', axis=0, tiled=True)]
    all_gather x1, waiting for transfers between devices: 27.9 us -> 44.6 us  [layer_chain(): lax.all_gather(decoded.astype(jnp.bfloat16), 'layer', axis=0, tiled=False)]
    dynamic_update_slice x0 -> x14, local copies, waits for them, and re-layouts: none -> 11.8 us  [ring_all_gather(): lax.dynamic_update_slice(gathered, travelling[None], (source, jnp.int32(0...]
    all_to_all x1, waiting for transfers between devices: 8.87 us -> 0.01 us  [exchange_codes(): lax.all_to_all(spread, 'tok', split_axis=0, concat_axis=0, tiled=True)]
    convert_element_type x1 -> x12, other arithmetic: 5.77 us -> 14 us  [ring_reduce_scatter(): running = total.astype(jnp.bfloat16)]
  transfers between devices with their start and end apart: 6 -> 32, of which waited for: 5 -> 25; matrix products, arithmetic and copies ran while one was open for 1% -> 6% of each run, Pallas kernels for 0% -> 0%
where the time goes in v4:
time: 575 us; the launch traced here: 573 us
  waiting for transfers between devices  176 us (31%)
  starting transfers between devices  160 us (28%)
  matrix products  121 us (21%)
  between operations  54.6 us (9%)
  local copies, waits for them, and re-layouts  30.5 us (5%)
  other arithmetic  26.8 us (5%)
    ppermute x14, waiting for transfers between devices, ring_all_gather(): travelling = lax.ppermute(travelling, 'tok', perm)  95.3 us
    ppermute x14, starting transfers between devices, ring_reduce_scatter(): arrived = lax.ppermute(running, 'tok', perm)  79.6 us
    ppermute x14, starting transfers between devices, ring_all_gather(): travelling = lax.ppermute(travelling, 'tok', perm)  62.5 us
    all_gather x1, waiting for transfers between devices, layer_chain(): lax.all_gather(decoded.astype(jnp.bfloat16), 'layer', axis=0, tiled=False)  44.6 us
    dot_general x1, matrix products, on_device(): lax.dot_general(segment, weights, (((1,), (1,)), ((), ())), preferred_ele...  43.1 us
    dot_general x1, matrix products, on_device(): jnp.dot(spread, weights, preferred_element_type=jnp.float32)  42.2 us
    ppermute x14, waiting for transfers between devices, ring_reduce_scatter(): arrived = lax.ppermute(running, 'tok', perm)  32.2 us
    dot_general x1, matrix products, on_device(): jnp.einsum('thl,tkl->tkh', products, low_hot.astype(jnp.float32), precisi...  24.7 us
  transfers between devices with their start and end apart: 32, of which 25 were waited for; matrix products, arithmetic and copies ran while one was open for 6% of the time, Pallas kernels for 0%

profile of v4, /device:TPU:0, one launch (start us, length us, event | category | flops | bytes accessed | tf_op | source)
XLA Modules:
  0.0 573.5 jit_solution(12694825048766335462)
XLA Ops:
  9.3 7.3 %all-to-all-start = ((f32[8,128,64]{1,2,0:T(8,128)}), f32[8,128,64]{1,2,0:T(8,128)S(1)}, u32[]{:S(2)}, u32[]{:S(2)}) async-start(f32[8,128,64]{1,2,0:T(8,128)} %broadcast_in_dim.84), calls=%async_computation | async-start | bytes 524288 | tf_op jit(solution)/shard_map/all_to_all | solution.py:101
  28.5 2.0 fusion.56
  33.3 10.7 %fusion.17 = bf16[1024,32,128]{2,1,0:T(8,128)(2,1)} fusion(s32[1024,32]{1,0:T(8,128)S(1)} %copy.22, s32[1024,32]{1,0:T(8,128)S(1)} %copy.20, bf16[1024,32]{1,0:T(8,128)(2,1)S(1)} %copy.21), kind=kOutput, calls=%fused_computation.15 | convolution fusion | flops 278921216 | bytes 8716288 | tf_op jit(solution)/shard_map/tkh,tkl->thl/dot_general | solution.py:139
  44.1 42.2 %fusion.12 = bf16[1024,4096]{1,0:T(8,128)(2,1)S(1)} fusion(bf16[1,4096,4096]{2,1,0:T(8,128)(2,1)} %param.12, bf16[128,8,32,128]{3,2,1,0:T(8,128)(2,1)} %bitcast.220), kind=kOutput, calls=%fused_computation.14 | convolution fusion | flops 34363932672 | bytes 50331648 | tf_op jit(solution)/shard_map/dot_general | solution.py:143
  86.3 2.5 fusion.53
  88.8 2.0 copy-done.1
  90.9 3.8 collective-permute-start.7
  101.1 4.3 collective-permute-done.7
  106.5 4.4 collective-permute-start.8
  117.7 2.9 collective-permute-done.8
  121.8 4.4 collective-permute-start.9
  132.3 2.7 collective-permute-done.9
  136.1 4.4 collective-permute-start.10
  142.8 36.7 %collective-permute-start.3 = (bf16[128,2048]{1,0:T(8,128)(2,1)S(1)}, bf16[128,2048]{1,0:T(8,128)(2,1)S(1)}, u32[]{:S(2)}, u32[]{:S(2)}) collective-permute-start(bf16[128,2048]{1,0:T(8,128)(2,1)S(1)} %fusion.42), channel_id=1, source_target_pairs={{0,1},{1,3},{3,2},{2,4},{4,5},{5,7},{7,6},{6,0},{8,9},{9,11},{11,1... | collective-permute-start | bytes 1572872 | tf_op jit(solution)/shard_map/ppermute | solution.py:66
  185.9 3.2 collective-permute-done.3
  190.3 2.7 collective-permute-start.4
  199.6 2.9 collective-permute-start.12
  202.5 5.4 collective-permute-done.4
  214.1 3.9 collective-permute-start.13
  218.0 4.7 collective-permute-done.5
  223.8 16.0 %collective-permute-start.6 = (bf16[128,2048]{1,0:T(8,128)(2,1)S(1)}, bf16[128,2048]{1,0:T(8,128)(2,1)S(1)}, u32[]{:S(2)}, u32[]{:S(2)}) collective-permute-start(bf16[128,2048]{1,0:T(8,128)(2,1)S(1)} %fusion.39), channel_id=1, source_target_pairs={{0,1},{1,3},{3,2},{2,4},{4,5},{5,7},{7,6},{6,0},{8,9},{9,11},{11,1... | collective-permute-start | bytes 1572872 | tf_op jit(solution)/shard_map/ppermute | solution.py:66
  243.4 1.6 collective-permute-done.13
  249.1 5.2 all-gather
  254.4 44.6 %all-gather.4.cloned.1.call-done = bf16[4,128,4096]{2,1,0:T(8,128)(2,1)} async-done(((bf16[1,128,4096]{2,1,0:T(8,128)(2,1)}), bf16[4,128,4096]{2,1,0:T(8,128)(2,1)}) %all-gather.4.cloned.1.call-update) | async-done | bytes 4194320 | tf_op jit(solution)/shard_map/all_gather | solution.py:111
  299.0 5.3 broadcast_in_dim.88
  305.5 3.3 bitcast_dynamic-update-slice_fusion
  310.4 2.4 collective-permute-start.21
  312.8 12.2 %collective-permute-done.14 = bf16[128,2048]{1,0:T(8,128)(2,1)S(1)} collective-permute-done((bf16[128,2048]{1,0:T(8,128)(2,1)S(1)}, bf16[128,2048]{1,0:T(8,128)(2,1)S(1)}, u32[]{:S(2)}, u32[]{:S(2)}) %collective-permute-start.14) | collective-permute-done | bytes 524320 | tf_op jit(solution)/shard_map/ppermute | solution.py:86
  325.0 3.8 collective-permute-start.22
  328.8 11.3 %collective-permute-done.15 = bf16[128,2048]{1,0:T(8,128)(2,1)S(1)} collective-permute-done((bf16[128,2048]{1,0:T(8,128)(2,1)S(1)}, bf16[128,2048]{1,0:T(8,128)(2,1)S(1)}, u32[]{:S(2)}, u32[]{:S(2)}) %collective-permute-start.15) | collective-permute-done | bytes 524320 | tf_op jit(solution)/shard_map/ppermute | solution.py:86
  340.1 3.8 collective-permute-start.23
  343.9 10.3 %collective-permute-done.16 = bf16[128,2048]{1,0:T(8,128)(2,1)S(1)} collective-permute-done((bf16[128,2048]{1,0:T(8,128)(2,1)S(1)}, bf16[128,2048]{1,0:T(8,128)(2,1)S(1)}, u32[]{:S(2)}, u32[]{:S(2)}) %collective-permute-start.16) | collective-permute-done | bytes 524320 | tf_op jit(solution)/shard_map/ppermute | solution.py:86
  354.2 25.7 %collective-permute-start.17 = (bf16[128,2048]{1,0:T(8,128)(2,1)S(1)}, bf16[128,2048]{1,0:T(8,128)(2,1)S(1)}, u32[]{:S(2)}, u32[]{:S(2)}) collective-permute-start(bf16[128,2048]{1,0:T(8,128)(2,1)S(1)} %collective-permute-done.16), channel_id=1, source_target_pairs={{0,1},{1,3},{3,2},{2,4},{4,5},{5,7},{7,6},{6,0},{8,9},{9,11},{11,1... | collective-permute-start | bytes 1572872 | tf_op jit(solution)/shard_map/ppermute | solution.py:86
  381.1 7.7 %collective-permute-done.17 = bf16[128,2048]{1,0:T(8,128)(2,1)S(1)} collective-permute-done((bf16[128,2048]{1,0:T(8,128)(2,1)S(1)}, bf16[128,2048]{1,0:T(8,128)(2,1)S(1)}, u32[]{:S(2)}, u32[]{:S(2)}) %collective-permute-start.17) | collective-permute-done | bytes 524320 | tf_op jit(solution)/shard_map/ppermute | solution.py:86
  388.9 7.2 %collective-permute-start.18 = (bf16[128,2048]{1,0:T(8,128)(2,1)S(1)}, bf16[128,2048]{1,0:T(8,128)(2,1)S(1)}, u32[]{:S(2)}, u32[]{:S(2)}) collective-permute-start(bf16[128,2048]{1,0:T(8,128)(2,1)S(1)} %collective-permute-done.17), channel_id=1, source_target_pairs={{0,1},{1,3},{3,2},{2,4},{4,5},{5,7},{7,6},{6,0},{8,9},{9,11},{11,1... | collective-permute-start | bytes 1572872 | tf_op jit(solution)/shard_map/ppermute | solution.py:86
  396.9 10.1 %collective-permute-done.24 = bf16[128,2048]{1,0:T(8,128)(2,1)S(1)} collective-permute-done((bf16[128,2048]{1,0:T(8,128)(2,1)S(1)}, bf16[128,2048]{1,0:T(8,128)(2,1)S(1)}, u32[]{:S(2)}, u32[]{:S(2)}) %collective-permute-start.24) | collective-permute-done | bytes 524320 | tf_op jit(solution)/shard_map/ppermute | solution.py:86
  407.9 6.8 %collective-permute-start.19 = (bf16[128,2048]{1,0:T(8,128)(2,1)S(1)}, bf16[128,2048]{1,0:T(8,128)(2,1)S(1)}, u32[]{:S(2)}, u32[]{:S(2)}) collective-permute-start(bf16[128,2048]{1,0:T(8,128)(2,1)S(1)} %collective-permute-done.18), channel_id=1, source_target_pairs={{0,1},{1,3},{3,2},{2,4},{4,5},{5,7},{7,6},{6,0},{8,9},{9,11},{11,1... | collective-permute-start | bytes 1572872 | tf_op jit(solution)/shard_map/ppermute | solution.py:86
  415.5 3.6 collective-permute-done.25
  419.1 2.2 collective-permute-start.26
  422.3 9.1 %collective-permute-start.20 = (bf16[128,2048]{1,0:T(8,128)(2,1)S(1)}, bf16[128,2048]{1,0:T(8,128)(2,1)S(1)}, u32[]{:S(2)}, u32[]{:S(2)}) collective-permute-start(bf16[128,2048]{1,0:T(8,128)(2,1)S(1)} %collective-permute-done.19), channel_id=1, source_target_pairs={{0,1},{1,3},{3,2},{2,4},{4,5},{5,7},{7,6},{6,0},{8,9},{9,11},{11,1... | collective-permute-start | bytes 1572872 | tf_op jit(solution)/shard_map/ppermute | solution.py:86
  432.2 7.4 %collective-permute-done.26 = bf16[128,2048]{1,0:T(8,128)(2,1)S(1)} collective-permute-done((bf16[128,2048]{1,0:T(8,128)(2,1)S(1)}, bf16[128,2048]{1,0:T(8,128)(2,1)S(1)}, u32[]{:S(2)}, u32[]{:S(2)}) %collective-permute-start.26) | collective-permute-done | bytes 524320 | tf_op jit(solution)/shard_map/ppermute | solution.py:86
  446.3 31.4 %collective-permute-done.27 = bf16[128,2048]{1,0:T(8,128)(2,1)S(1)} collective-permute-done((bf16[128,2048]{1,0:T(8,128)(2,1)S(1)}, bf16[128,2048]{1,0:T(8,128)(2,1)S(1)}, u32[]{:S(2)}, u32[]{:S(2)}) %collective-permute-start.27) | collective-permute-done | bytes 524320 | tf_op jit(solution)/shard_map/ppermute | solution.py:86
  478.5 43.1 %fusion.57 = f32[1024,32,128]{2,0,1:T(8,128)} fusion(bf16[1024,4096,1]{1,0,2:T(8,128)(2,1)} %bitcast.84, bf16[32,128,4096]{2,1,0:T(8,128)(2,1)} %bitcast.219), kind=kOutput, calls=%fused_computation.115 | convolution fusion | flops 34359738368 | bytes 58720256 | tf_op jit(solution)/shard_map/dot_general | solution.py:148
  521.7 24.7 %select_reduce_fusion = f32[1024,32]{1,0:T(8,128)} fusion(s32[1024,32]{1,0:T(8,128)} %copy-done.4, f32[1024,32,128]{2,0,1:T(8,128)} %fusion.57, s32[1024,32]{1,0:T(8,128)} %copy-done.5), kind=kOutput, calls=%fused_computation.4 | convolution fusion | flops 1617920000 | bytes 17170432 | tf_op jit(solution)/shard_map/thl,tkl->tkh/dot_general | solution.py:152
  546.4 1.9 copy.25
  548.2 10.5 %all-to-all-start.1 = ((f32[8,128,32]{1,2,0:T(8,128)}), f32[8,128,32]{1,2,0:T(8,128)S(1)}, u32[]{:S(2)}, u32[]{:S(2)}) async-start(f32[8,128,32]{1,2,0:T(8,128)} %copy.25), calls=%async_computation.1 | async-start | bytes 262144 | tf_op jit(solution)/shard_map/all_to_all | solution.py:160
  558.7 3.8 fusion.45
  562.5 3.5 all-to-all-done.1
  (89 shorter events, 47.1 us)
Async XLA Ops:
  9.3 23.1 %all-to-all-start = ((f32[8,128,64]{1,2,0:T(8,128)}), f32[8,128,64]{1,2,0:T(8,128)S(1)}, u32[]{:S(2)}, u32[]{:S(2)}) async-start(f32[8,128,64]{1,2,0:T(8,128)} %broadcast_in_dim.84), calls=%async_computation | async-start | bytes 524288 | tf_op jit(solution)/shard_map/all_to_all | solution.py:101
  16.6 237.8 %all-gather.6.cloned.1.call-start = ((), (), s32[]{:S(2)}) async-start(), calls=%async_computation.3 | async-start | bytes 5242880 | tf_op jit(solution)/shard_map/all_gather | solution.py:110
  33.1 11.0 %copy-start.4 = (s32[1024,32]{1,0:T(8,128)}, s32[1024,32]{1,0:T(8,128)S(1)}, u32[]{:S(2)}) copy-start(s32[1024,32]{1,0:T(8,128)S(1)} %copy.20) | copy-start | bytes 393220
  33.3 10.8 %copy-start.5 = (s32[1024,32]{1,0:T(8,128)}, s32[1024,32]{1,0:T(8,128)S(1)}, u32[]{:S(2)}) copy-start(s32[1024,32]{1,0:T(8,128)S(1)} %copy.22) | copy-start | bytes 393220
  88.8 2.0 copy-start.1
  90.9 14.5 %collective-permute-start.7 = (bf16[128,2048]{1,0:T(8,128)(2,1)S(1)}, bf16[128,2048]{1,0:T(8,128)(2,1)S(1)}, u32[]{:S(2)}, u32[]{:S(2)}) collective-permute-start(bf16[128,2048]{1,0:T(8,128)(2,1)S(1)} %dynamic-slice_bitcast_fusion), channel_id=1, source_target_pairs={{1,0},{3,1},{2,3},{4,2},{5,4},{7,5},{6,7},{0,6},{9,8},{11,9},{10,1... | collective-permute-start | bytes 1572872 | tf_op jit(solution)/shard_map/ppermute | solution.py:66
  97.7 14.8 %collective-permute-start = (bf16[128,2048]{1,0:T(8,128)(2,1)S(1)}, bf16[128,2048]{1,0:T(8,128)(2,1)S(1)}, u32[]{:S(2)}, u32[]{:S(2)}) collective-permute-start(bf16[128,2048]{1,0:T(8,128)(2,1)S(1)} %dynamic-slice_bitcast_fusion.1), channel_id=1, source_target_pairs={{0,1},{1,3},{3,2},{2,4},{4,5},{5,7},{7,6},{6,0},{8,9},{9,11},{11,1... | collective-permute-start | bytes 1572872 | tf_op jit(solution)/shard_map/ppermute | solution.py:66
  106.5 14.1 %collective-permute-start.8 = (bf16[128,2048]{1,0:T(8,128)(2,1)S(1)}, bf16[128,2048]{1,0:T(8,128)(2,1)S(1)}, u32[]{:S(2)}, u32[]{:S(2)}) collective-permute-start(bf16[128,2048]{1,0:T(8,128)(2,1)S(1)} %fusion.38), channel_id=1, source_target_pairs={{1,0},{3,1},{2,3},{4,2},{5,4},{7,5},{6,7},{0,6},{9,8},{11,9},{10,1... | collective-permute-start | bytes 1572872 | tf_op jit(solution)/shard_map/ppermute | solution.py:66
  113.6 13.8 %collective-permute-start.1 = (bf16[128,2048]{1,0:T(8,128)(2,1)S(1)}, bf16[128,2048]{1,0:T(8,128)(2,1)S(1)}, u32[]{:S(2)}, u32[]{:S(2)}) collective-permute-start(bf16[128,2048]{1,0:T(8,128)(2,1)S(1)} %fusion.44), channel_id=1, source_target_pairs={{0,1},{1,3},{3,2},{2,4},{4,5},{5,7},{7,6},{6,0},{8,9},{9,11},{11,1... | collective-permute-start | bytes 1572872 | tf_op jit(solution)/shard_map/ppermute | solution.py:66
  113.7 185.3 %all-gather.4.cloned.1.call-start = ((), (), s32[]{:S(2)}) async-start(), calls=%async_computation.2 | async-start | bytes 5242880 | tf_op jit(solution)/shard_map/all_gather | solution.py:111
  121.8 13.1 %collective-permute-start.9 = (bf16[128,2048]{1,0:T(8,128)(2,1)S(1)}, bf16[128,2048]{1,0:T(8,128)(2,1)S(1)}, u32[]{:S(2)}, u32[]{:S(2)}) collective-permute-start(bf16[128,2048]{1,0:T(8,128)(2,1)S(1)} %fusion.37), channel_id=1, source_target_pairs={{1,0},{3,1},{2,3},{4,2},{5,4},{7,5},{6,7},{0,6},{9,8},{11,9},{10,1... | collective-permute-start | bytes 1572872 | tf_op jit(solution)/shard_map/ppermute | solution.py:66
  128.7 12.9 %collective-permute-start.2 = (bf16[128,2048]{1,0:T(8,128)(2,1)S(1)}, bf16[128,2048]{1,0:T(8,128)(2,1)S(1)}, u32[]{:S(2)}, u32[]{:S(2)}) collective-permute-start(bf16[128,2048]{1,0:T(8,128)(2,1)S(1)} %fusion.43), channel_id=1, source_target_pairs={{0,1},{1,3},{3,2},{2,4},{4,5},{5,7},{7,6},{6,0},{8,9},{9,11},{11,1... | collective-permute-start | bytes 1572872 | tf_op jit(solution)/shard_map/ppermute | solution.py:66
  136.1 48.5 %collective-permute-start.10 = (bf16[128,2048]{1,0:T(8,128)(2,1)S(1)}, bf16[128,2048]{1,0:T(8,128)(2,1)S(1)}, u32[]{:S(2)}, u32[]{:S(2)}) collective-permute-start(bf16[128,2048]{1,0:T(8,128)(2,1)S(1)} %fusion.36), channel_id=1, source_target_pairs={{1,0},{3,1},{2,3},{4,2},{5,4},{7,5},{6,7},{0,6},{9,8},{11,9},{10,1... | collective-permute-start | bytes 1572872 | tf_op jit(solution)/shard_map/ppermute | solution.py:66
  142.8 46.3 %collective-permute-start.3 = (bf16[128,2048]{1,0:T(8,128)(2,1)S(1)}, bf16[128,2048]{1,0:T(8,128)(2,1)S(1)}, u32[]{:S(2)}, u32[]{:S(2)}) collective-permute-start(bf16[128,2048]{1,0:T(8,128)(2,1)S(1)} %fusion.42), channel_id=1, source_target_pairs={{0,1},{1,3},{3,2},{2,4},{4,5},{5,7},{7,6},{6,0},{8,9},{9,11},{11,1... | collective-permute-start | bytes 1572872 | tf_op jit(solution)/shard_map/ppermute | solution.py:66
  185.8 12.6 %collective-permute-start.11 = (bf16[128,2048]{1,0:T(8,128)(2,1)S(1)}, bf16[128,2048]{1,0:T(8,128)(2,1)S(1)}, u32[]{:S(2)}, u32[]{:S(2)}) collective-permute-start(bf16[128,2048]{1,0:T(8,128)(2,1)S(1)} %fusion.35), channel_id=1, source_target_pairs={{1,0},{3,1},{2,3},{4,2},{5,4},{7,5},{6,7},{0,6},{9,8},{11,9},{10,1... | collective-permute-start | bytes 1572872 | tf_op jit(solution)/shard_map/ppermute | solution.py:66
  190.3 17.6 %collective-permute-start.4 = (bf16[128,2048]{1,0:T(8,128)(2,1)S(1)}, bf16[128,2048]{1,0:T(8,128)(2,1)S(1)}, u32[]{:S(2)}, u32[]{:S(2)}) collective-permute-start(bf16[128,2048]{1,0:T(8,128)(2,1)S(1)} %fusion.41), channel_id=1, source_target_pairs={{0,1},{1,3},{3,2},{2,4},{4,5},{5,7},{7,6},{6,0},{8,9},{9,11},{11,1... | collective-permute-start | bytes 1572872 | tf_op jit(solution)/shard_map/ppermute | solution.py:66
  199.6 13.3 %collective-permute-start.12 = (bf16[128,2048]{1,0:T(8,128)(2,1)S(1)}, bf16[128,2048]{1,0:T(8,128)(2,1)S(1)}, u32[]{:S(2)}, u32[]{:S(2)}) collective-permute-start(bf16[128,2048]{1,0:T(8,128)(2,1)S(1)} %fusion.34), channel_id=1, source_target_pairs={{1,0},{3,1},{2,3},{4,2},{5,4},{7,5},{6,7},{0,6},{9,8},{11,9},{10,1... | collective-permute-start | bytes 1572872 | tf_op jit(solution)/shard_map/ppermute | solution.py:66
  209.0 13.6 %collective-permute-start.5 = (bf16[128,2048]{1,0:T(8,128)(2,1)S(1)}, bf16[128,2048]{1,0:T(8,128)(2,1)S(1)}, u32[]{:S(2)}, u32[]{:S(2)}) collective-permute-start(bf16[128,2048]{1,0:T(8,128)(2,1)S(1)} %fusion.40), channel_id=1, source_target_pairs={{0,1},{1,3},{3,2},{2,4},{4,5},{5,7},{7,6},{6,0},{8,9},{9,11},{11,1... | collective-permute-start | bytes 1572872 | tf_op jit(solution)/shard_map/ppermute | solution.py:66
  214.1 31.0 %collective-permute-start.13 = (bf16[128,2048]{1,0:T(8,128)(2,1)S(1)}, bf16[128,2048]{1,0:T(8,128)(2,1)S(1)}, u32[]{:S(2)}, u32[]{:S(2)}) collective-permute-start(bf16[128,2048]{1,0:T(8,128)(2,1)S(1)} %fusion.33), channel_id=1, source_target_pairs={{1,0},{3,1},{2,3},{4,2},{5,4},{7,5},{6,7},{0,6},{9,8},{11,9},{10,1... | collective-permute-start | bytes 1572872 | tf_op jit(solution)/shard_map/ppermute | solution.py:66
  223.8 23.0 %collective-permute-start.6 = (bf16[128,2048]{1,0:T(8,128)(2,1)S(1)}, bf16[128,2048]{1,0:T(8,128)(2,1)S(1)}, u32[]{:S(2)}, u32[]{:S(2)}) collective-permute-start(bf16[128,2048]{1,0:T(8,128)(2,1)S(1)} %fusion.39), channel_id=1, source_target_pairs={{0,1},{1,3},{3,2},{2,4},{4,5},{5,7},{7,6},{6,0},{8,9},{9,11},{11,1... | collective-permute-start | bytes 1572872 | tf_op jit(solution)/shard_map/ppermute | solution.py:66
  243.4 5.7 copy-start.6
  248.0 56.3 %copy-start.3 = (bf16[128,4096]{1,0:T(8,128)(2,1)S(1)}, bf16[128,4096]{1,0:T(8,128)(2,1)}, u32[]{:S(2)}) copy-start(bf16[128,4096]{1,0:T(8,128)(2,1)} %param.14) | copy-start | bytes 3145732
  299.0 5.3 copy-start
  299.0 6.5 %copy-start.2 = (bf16[4,128,4096]{2,1,0:T(8,128)(2,1)S(1)}, bf16[4,128,4096]{2,1,0:T(8,128)(2,1)}, u32[]{:S(2)}) copy-start(bf16[4,128,4096]{2,1,0:T(8,128)(2,1)} %all-gather.6.cloned.1.call-done) | copy-start | bytes 12582916
  308.9 16.0 %collective-permute-start.14 = (bf16[128,2048]{1,0:T(8,128)(2,1)S(1)}, bf16[128,2048]{1,0:T(8,128)(2,1)S(1)}, u32[]{:S(2)}, u32[]{:S(2)}) collective-permute-start(bf16[128,2048]{1,0:T(8,128)(2,1)S(1)} %get-tuple-element.13), channel_id=1, source_target_pairs={{0,1},{1,3},{3,2},{2,4},{4,5},{5,7},{7,6},{6,0},{8,9},{9,11},{11,1... | collective-permute-start | bytes 1572872 | tf_op jit(solution)/shard_map/ppermute | solution.py:86
  310.4 14.5 %collective-permute-start.21 = (bf16[128,2048]{1,0:T(8,128)(2,1)S(1)}, bf16[128,2048]{1,0:T(8,128)(2,1)S(1)}, u32[]{:S(2)}, u32[]{:S(2)}) collective-permute-start(bf16[128,2048]{1,0:T(8,128)(2,1)S(1)} %get-tuple-element.12), channel_id=1, source_target_pairs={{1,0},{3,1},{2,3},{4,2},{5,4},{7,5},{6,7},{0,6},{9,8},{11,9},{10,1... | collective-permute-start | bytes 1572872 | tf_op jit(solution)/shard_map/ppermute | solution.py:86
  325.0 15.1 %collective-permute-start.15 = (bf16[128,2048]{1,0:T(8,128)(2,1)S(1)}, bf16[128,2048]{1,0:T(8,128)(2,1)S(1)}, u32[]{:S(2)}, u32[]{:S(2)}) collective-permute-start(bf16[128,2048]{1,0:T(8,128)(2,1)S(1)} %collective-permute-done.14), channel_id=1, source_target_pairs={{0,1},{1,3},{3,2},{2,4},{4,5},{5,7},{7,6},{6,0},{8,9},{9,11},{11,1... | collective-permute-start | bytes 1572872 | tf_op jit(solution)/shard_map/ppermute | solution.py:86
  325.0 15.1 %collective-permute-start.22 = (bf16[128,2048]{1,0:T(8,128)(2,1)S(1)}, bf16[128,2048]{1,0:T(8,128)(2,1)S(1)}, u32[]{:S(2)}, u32[]{:S(2)}) collective-permute-start(bf16[128,2048]{1,0:T(8,128)(2,1)S(1)} %collective-permute-done.21), channel_id=1, source_target_pairs={{1,0},{3,1},{2,3},{4,2},{5,4},{7,5},{6,7},{0,6},{9,8},{11,9},{10,1... | collective-permute-start | bytes 1572872 | tf_op jit(solution)/shard_map/ppermute | solution.py:86
  340.1 14.2 %collective-permute-start.16 = (bf16[128,2048]{1,0:T(8,128)(2,1)S(1)}, bf16[128,2048]{1,0:T(8,128)(2,1)S(1)}, u32[]{:S(2)}, u32[]{:S(2)}) collective-permute-start(bf16[128,2048]{1,0:T(8,128)(2,1)S(1)} %collective-permute-done.15), channel_id=1, source_target_pairs={{0,1},{1,3},{3,2},{2,4},{4,5},{5,7},{7,6},{6,0},{8,9},{9,11},{11,1... | collective-permute-start | bytes 1572872 | tf_op jit(solution)/shard_map/ppermute | solution.py:86
  340.1 41.0 %collective-permute-start.23 = (bf16[128,2048]{1,0:T(8,128)(2,1)S(1)}, bf16[128,2048]{1,0:T(8,128)(2,1)S(1)}, u32[]{:S(2)}, u32[]{:S(2)}) collective-permute-start(bf16[128,2048]{1,0:T(8,128)(2,1)S(1)} %collective-permute-done.22), channel_id=1, source_target_pairs={{1,0},{3,1},{2,3},{4,2},{5,4},{7,5},{6,7},{0,6},{9,8},{11,9},{10,1... | collective-permute-start | bytes 1572872 | tf_op jit(solution)/shard_map/ppermute | solution.py:86
  354.2 34.6 %collective-permute-start.17 = (bf16[128,2048]{1,0:T(8,128)(2,1)S(1)}, bf16[128,2048]{1,0:T(8,128)(2,1)S(1)}, u32[]{:S(2)}, u32[]{:S(2)}) collective-permute-start(bf16[128,2048]{1,0:T(8,128)(2,1)S(1)} %collective-permute-done.16), channel_id=1, source_target_pairs={{0,1},{1,3},{3,2},{2,4},{4,5},{5,7},{7,6},{6,0},{8,9},{9,11},{11,1... | collective-permute-start | bytes 1572872 | tf_op jit(solution)/shard_map/ppermute | solution.py:86
  381.1 25.9 %collective-permute-start.24 = (bf16[128,2048]{1,0:T(8,128)(2,1)S(1)}, bf16[128,2048]{1,0:T(8,128)(2,1)S(1)}, u32[]{:S(2)}, u32[]{:S(2)}) collective-permute-start(bf16[128,2048]{1,0:T(8,128)(2,1)S(1)} %collective-permute-done.23), channel_id=1, source_target_pairs={{1,0},{3,1},{2,3},{4,2},{5,4},{7,5},{6,7},{0,6},{9,8},{11,9},{10,1... | collective-permute-start | bytes 1572872 | tf_op jit(solution)/shard_map/ppermute | solution.py:86
  388.9 19.1 %collective-permute-start.18 = (bf16[128,2048]{1,0:T(8,128)(2,1)S(1)}, bf16[128,2048]{1,0:T(8,128)(2,1)S(1)}, u32[]{:S(2)}, u32[]{:S(2)}) collective-permute-start(bf16[128,2048]{1,0:T(8,128)(2,1)S(1)} %collective-permute-done.17), channel_id=1, source_target_pairs={{0,1},{1,3},{3,2},{2,4},{4,5},{5,7},{7,6},{6,0},{8,9},{9,11},{11,1... | collective-permute-start | bytes 1572872 | tf_op jit(solution)/shard_map/ppermute | solution.py:86
  407.1 12.1 %collective-permute-start.25 = (bf16[128,2048]{1,0:T(8,128)(2,1)S(1)}, bf16[128,2048]{1,0:T(8,128)(2,1)S(1)}, u32[]{:S(2)}, u32[]{:S(2)}) collective-permute-start(bf16[128,2048]{1,0:T(8,128)(2,1)S(1)} %collective-permute-done.24), channel_id=1, source_target_pairs={{1,0},{3,1},{2,3},{4,2},{5,4},{7,5},{6,7},{0,6},{9,8},{11,9},{10,1... | collective-permute-start | bytes 1572872 | tf_op jit(solution)/shard_map/ppermute | solution.py:86
  407.9 14.3 %collective-permute-start.19 = (bf16[128,2048]{1,0:T(8,128)(2,1)S(1)}, bf16[128,2048]{1,0:T(8,128)(2,1)S(1)}, u32[]{:S(2)}, u32[]{:S(2)}) collective-permute-start(bf16[128,2048]{1,0:T(8,128)(2,1)S(1)} %collective-permute-done.18), channel_id=1, source_target_pairs={{0,1},{1,3},{3,2},{2,4},{4,5},{5,7},{7,6},{6,0},{8,9},{9,11},{11,1... | collective-permute-start | bytes 1572872 | tf_op jit(solution)/shard_map/ppermute | solution.py:86
  419.1 20.4 %collective-permute-start.26 = (bf16[128,2048]{1,0:T(8,128)(2,1)S(1)}, bf16[128,2048]{1,0:T(8,128)(2,1)S(1)}, u32[]{:S(2)}, u32[]{:S(2)}) collective-permute-start(bf16[128,2048]{1,0:T(8,128)(2,1)S(1)} %collective-permute-done.25), channel_id=1, source_target_pairs={{1,0},{3,1},{2,3},{4,2},{5,4},{7,5},{6,7},{0,6},{9,8},{11,9},{10,1... | collective-permute-start | bytes 1572872 | tf_op jit(solution)/shard_map/ppermute | solution.py:86
  422.3 18.2 %collective-permute-start.20 = (bf16[128,2048]{1,0:T(8,128)(2,1)S(1)}, bf16[128,2048]{1,0:T(8,128)(2,1)S(1)}, u32[]{:S(2)}, u32[]{:S(2)}) collective-permute-start(bf16[128,2048]{1,0:T(8,128)(2,1)S(1)} %collective-permute-done.19), channel_id=1, source_target_pairs={{0,1},{1,3},{3,2},{2,4},{4,5},{5,7},{7,6},{6,0},{8,9},{9,11},{11,1... | collective-permute-start | bytes 1572872 | tf_op jit(solution)/shard_map/ppermute | solution.py:86
  439.6 38.1 %collective-permute-start.27 = (bf16[128,2048]{1,0:T(8,128)(2,1)S(1)}, bf16[128,2048]{1,0:T(8,128)(2,1)S(1)}, u32[]{:S(2)}, u32[]{:S(2)}) collective-permute-start(bf16[128,2048]{1,0:T(8,128)(2,1)S(1)} %collective-permute-done.26), channel_id=1, source_target_pairs={{1,0},{3,1},{2,3},{4,2},{5,4},{7,5},{6,7},{0,6},{9,8},{11,9},{10,1... | collective-permute-start | bytes 1572872 | tf_op jit(solution)/shard_map/ppermute | solution.py:86
  548.2 17.8 %all-to-all-start.1 = ((f32[8,128,32]{1,2,0:T(8,128)}), f32[8,128,32]{1,2,0:T(8,128)S(1)}, u32[]{:S(2)}, u32[]{:S(2)}) async-start(f32[8,128,32]{1,2,0:T(8,128)} %copy.25), calls=%async_computation.1 | async-start | bytes 262144 | tf_op jit(solution)/shard_map/all_to_all | solution.py:160
Sparse Core Ops, SparseCore 0:
  113.9 72.8 all-gather.5
  249.2 49.7 all-gather.3

commit v5 on v2

--- a/solution.py
+++ b/solution.py
@@ -67,10 +67,15 @@
     )
     spread = spread.astype(jnp.bfloat16).reshape(tokens, range_size)
     partial = jnp.dot(spread, weights, preferred_element_type=jnp.float32).astype(jnp.bfloat16)
-    decoded = lax.psum_scatter(partial, "tok", scatter_dimension=0, tiled=True).astype(jnp.float32)
+    received = lax.all_to_all(partial, "tok", split_axis=0, concat_axis=0, tiled=True)
+    decoded = jnp.sum(
+        received.reshape(owners, -1, received.shape[1]).astype(jnp.float32), axis=0
+    )
     recon_full, grad_sum = layer_chain(decoded, carry_gain, earlier_sum, targets)
     grad_low = grad_sum.astype(jnp.bfloat16)
-    segment = lax.all_gather(grad_low, "tok", axis=0, tiled=True)
+    copies = jnp.broadcast_to(grad_low[None], (owners,) + grad_low.shape)
+    segment = lax.all_to_all(copies, "tok", split_axis=0, concat_axis=0, tiled=True)
+    segment = segment.reshape(owners * grad_low.shape[0], grad_low.shape[1])
     products = lax.dot_general(
         segment, weights, (((1,), (1,)), ((), ())), preferred_element_type=jnp.float32
     )

time: 481 us -> 587 us (1.22)
  blocking collectives: 5.43 us -> 194 us
  waiting for transfers between devices: 313 us -> 222 us
    all_to_all x0 -> x1, blocking collectives: none -> 189 us  [on_device(): lax.all_to_all(copies, 'tok', split_axis=0, concat_axis=0, tiled=True)]
    all_to_all x0 -> x1, waiting for transfers between devices: none -> 181 us  [on_device(): lax.all_to_all(partial, 'tok', split_axis=0, concat_axis=0, tiled=True)]
    reduce_scatter x1 -> x0, waiting for transfers between devices: 148 us -> none  [on_device(): lax.psum_scatter(partial, 'tok', scatter_dimension=0, tiled=True)]
    all_gather x1 -> x0, waiting for transfers between devices: 125 us -> none  [on_device(): segment = lax.all_gather(grad_low, 'tok', axis=0, tiled=True)]
  transfers between devices with their start and end apart: 6 -> 5, of which waited for: 5 -> 4; matrix products, arithmetic and copies ran while one was open for 1% -> 2% of each run, Pallas kernels for 0% -> 0%
where the time goes in v5:
time: 587 us; the launch traced here: 586 us
  waiting for transfers between devices  222 us (38%)
  blocking collectives  194 us (33%)
  matrix products  119 us (20%)
  other arithmetic  16.8 us (3%)
  starting transfers between devices  15.9 us (3%)
  between operations  14.2 us (2%)
    all_to_all x1, blocking collectives, on_device(): lax.all_to_all(copies, 'tok', split_axis=0, concat_axis=0, tiled=True)  189 us
    all_to_all x1, waiting for transfers between devices, on_device(): lax.all_to_all(partial, 'tok', split_axis=0, concat_axis=0, tiled=True)  181 us
    dot_general x1, matrix products, on_device(): lax.dot_general(segment, weights, (((1,), (1,)), ((), ())), preferred_ele...  43.1 us
    dot_general x1, matrix products, on_device(): jnp.dot(spread, weights, preferred_element_type=jnp.float32)  41.3 us
    all_gather x1, waiting for transfers between devices, layer_chain(): lax.all_gather(decoded.astype(jnp.bfloat16), 'layer', axis=0, tiled=False)  28.2 us
    dot_general x1, matrix products, on_device(): jnp.einsum('thl,tkl->tkh', products, low_hot.astype(jnp.float32), precisi...  24.7 us
  transfers between devices with their start and end apart: 5, of which 4 were waited for; matrix products, arithmetic and copies ran while one was open for 2% of the time, Pallas kernels for 0%

profile of v5, /device:TPU:0, one launch (start us, length us, event | category | flops | bytes accessed | tf_op | source)
XLA Modules:
  0.0 586.4 jit_solution(6004021499078432627)
XLA Ops:
  7.2 0.7 bitcast_convert_fusion
  7.9 0.7 convert_bitcast_fusion
  8.6 0.7 broadcast_in_dim.26
  9.3 7.3 %all-to-all-start = ((f32[8,128,64]{1,2,0:T(8,128)}), f32[8,128,64]{1,2,0:T(8,128)S(1)}, u32[]{:S(2)}, u32[]{:S(2)}) async-start(f32[8,128,64]{1,2,0:T(8,128)} %broadcast_in_dim.26), calls=%async_computation | async-start | bytes 524288 | tf_op jit(solution)/shard_map/all_to_all | solution.py:27
  16.6 8.9 %all-to-all-done = f32[8,128,64]{1,2,0:T(8,128)S(1)} async-done(((f32[8,128,64]{1,2,0:T(8,128)}), f32[8,128,64]{1,2,0:T(8,128)S(1)}, u32[]{:S(2)}, u32[]{:S(2)}) %all-to-all-start) | async-done | bytes 262176 | tf_op jit(solution)/shard_map/all_to_all | solution.py:27
  25.6 0.1 fusion.34
  25.7 0.1 add_select_fusion
  25.8 0.2 copy.17
  25.9 0.2 copy.16
  26.1 0.0 copy-start.1
  26.1 0.2 copy.18
  26.3 0.0 copy-start.2
  26.4 9.7 %fusion.17 = bf16[1024,32,128]{2,1,0:T(8,128)(2,1)S(1)} fusion(s32[1024,32]{1,0:T(8,128)S(1)} %copy.18, s32[1024,32]{1,0:T(8,128)S(1)} %copy.16, bf16[1024,32]{1,0:T(8,128)(2,1)S(1)} %copy.17), kind=kOutput, calls=%fused_computation.16 | convolution fusion | flops 278921216 | bytes 8716288 | tf_op jit(solution)/shard_map/tkh,tkl->thl/dot_general | solution.py:65
  36.1 0.0 copy-done.1
  36.1 0.0 copy-done.2
  36.1 41.3 %fusion.12 = bf16[1024,4096]{1,0:T(8,128)(2,1)} fusion(bf16[1,4096,4096]{2,1,0:T(8,128)(2,1)} %param.8, bf16[128,8,32,128]{3,2,1,0:T(8,128)(2,1)S(1)} %bitcast.71), kind=kOutput, calls=%fused_computation.15 | convolution fusion | flops 34363932672 | bytes 50331648 | tf_op jit(solution)/shard_map/dot_general | solution.py:69
  77.4 4.9 all-to-all-start.1
  82.3 0.0 all-gather.5.cloned.1.call-start
  82.4 0.7 all-gather.5.cloned.1.call-update
  83.1 0.0 all-gather.7.cloned.1.call-start
  83.1 180.7 %all-to-all-done.1 = bf16[8,128,4096]{2,1,0:T(8,128)(2,1)} async-done(((bf16[8,128,4096]{2,1,0:T(8,128)(2,1)}), bf16[8,128,4096]{2,1,0:T(8,128)(2,1)}, u32[]{:S(2)}, u32[]{:S(2)}) %all-to-all-start.1) | async-done | bytes 8388640 | tf_op jit(solution)/shard_map/all_to_all | solution.py:70
  263.8 5.0 convert_reduce_fusion
  268.8 0.0 copy-start.3
  268.8 0.0 copy-start
  268.9 1.1 convert_element_type.105
  270.0 0.0 all-gather.7.cloned.1.call-update
  270.0 0.0 copy-done.3
  270.0 5.4 all-gather.1
  275.4 0.0 all-gather.5.cloned.1.call-done
  275.4 28.2 %all-gather.7.cloned.1.call-done = bf16[512,4096]{1,0:T(8,128)(2,1)} async-done(((bf16[128,4096]{1,0:T(8,128)(2,1)}), bf16[512,4096]{1,0:T(8,128)(2,1)}) %all-gather.7.cloned.1.call-update) | async-done | bytes 4194320 | tf_op jit(solution)/shard_map/all_gather | solution.py:37
  303.7 0.0 copy-done
  303.7 4.7 fusion.28
  308.3 1.0 broadcast_in_dim.45
  309.4 188.8 %all_to_all.28 = bf16[8,128,4096]{2,1,0:T(8,128)(2,1)} all-to-all(bf16[8,128,4096]{2,1,0:T(8,128)(2,1)S(1)} %broadcast_in_dim.45), channel_id=1, replica_groups=mesh['layer'=4,'tok'=8] {'tok'}, dimensions={0} | all-to-all | bytes 16777216 | tf_op jit(solution)/shard_map/all_to_all | solution.py:77
  498.2 43.1 %fusion.41 = f32[1024,32,128]{2,0,1:T(8,128)} fusion(bf16[1024,4096,1]{1,0,2:T(8,128)(2,1)} %bitcast.58, bf16[32,128,4096]{2,1,0:T(8,128)(2,1)} %bitcast.70), kind=kOutput, calls=%fused_computation.62 | convolution fusion | flops 34359738368 | bytes 58720256 | tf_op jit(solution)/shard_map/dot_general | solution.py:79
  541.3 24.7 %select_reduce_fusion = f32[1024,32]{1,0:T(8,128)} fusion(s32[1024,32]{1,0:T(8,128)} %copy-done.1, f32[1024,32,128]{2,0,1:T(8,128)} %fusion.41, s32[1024,32]{1,0:T(8,128)} %copy-done.2), kind=kOutput, calls=%fused_computation.4 | convolution fusion | flops 1617920000 | bytes 17170432 | tf_op jit(solution)/shard_map/thl,tkl->tkh/dot_general | solution.py:83
  566.1 1.9 copy.21
  567.9 3.6 all-to-all-start.3
  571.6 3.8 fusion.33
  575.4 3.5 all-to-all-done.3
  578.9 0.6 reduce_sum.29
  (4 shorter events, 0.0 us)
Async XLA Ops:
  9.3 16.2 %all-to-all-start = ((f32[8,128,64]{1,2,0:T(8,128)}), f32[8,128,64]{1,2,0:T(8,128)S(1)}, u32[]{:S(2)}, u32[]{:S(2)}) async-start(f32[8,128,64]{1,2,0:T(8,128)} %broadcast_in_dim.26), calls=%async_computation | async-start | bytes 524288 | tf_op jit(solution)/shard_map/all_to_all | solution.py:27
  26.1 9.9 %copy-start.1 = (s32[1024,32]{1,0:T(8,128)}, s32[1024,32]{1,0:T(8,128)S(1)}, u32[]{:S(2)}) copy-start(s32[1024,32]{1,0:T(8,128)S(1)} %copy.16) | copy-start | bytes 393220
  26.3 9.7 %copy-start.2 = (s32[1024,32]{1,0:T(8,128)}, s32[1024,32]{1,0:T(8,128)S(1)}, u32[]{:S(2)}) copy-start(s32[1024,32]{1,0:T(8,128)S(1)} %copy.18) | copy-start | bytes 393220
  77.4 186.4 %all-to-all-start.1 = ((bf16[8,128,4096]{2,1,0:T(8,128)(2,1)}), bf16[8,128,4096]{2,1,0:T(8,128)(2,1)}, u32[]{:S(2)}, u32[]{:S(2)}) async-start(bf16[8,128,4096]{2,1,0:T(8,128)(2,1)} %bitcast.57), calls=%async_computation.1 | async-start | bytes 16777216 | tf_op jit(solution)/shard_map/all_to_all | solution.py:70
  82.3 193.1 %all-gather.5.cloned.1.call-start = ((), (), s32[]{:S(2)}) async-start(), calls=%async_computation.4 | async-start | bytes 5242880 | tf_op jit(solution)/shard_map/all_gather | solution.py:36
  83.1 220.6 %all-gather.7.cloned.1.call-start = ((), (), s32[]{:S(2)}) async-start(), calls=%async_computation.5 | async-start | bytes 5242880 | tf_op jit(solution)/shard_map/all_gather | solution.py:37
  268.8 1.2 copy-start.3
  268.8 34.8 %copy-start = (bf16[128,4096]{1,0:T(8,128)(2,1)S(1)}, bf16[128,4096]{1,0:T(8,128)(2,1)}, u32[]{:S(2)}) copy-start(bf16[128,4096]{1,0:T(8,128)(2,1)} %param.10) | copy-start | bytes 3145732
  567.9 11.0 %all-to-all-start.3 = ((f32[8,128,32]{1,2,0:T(8,128)}), f32[8,128,32]{1,2,0:T(8,128)S(1)}, u32[]{:S(2)}, u32[]{:S(2)}) async-start(f32[8,128,32]{1,2,0:T(8,128)} %copy.21), calls=%async_computation.3 | async-start | bytes 262144 | tf_op jit(solution)/shard_map/all_to_all | solution.py:91
Sparse Core Ops, SparseCore 0:
  84.7 35.7 all-gather.4
  270.1 33.5 all-gather.6

commit v6 on v2

--- a/solution.py
+++ b/solution.py
@@ -66,11 +66,24 @@
         "tkh,tkl->thl", coded_high, low_hot.astype(jnp.bfloat16), preferred_element_type=jnp.float32
     )
     spread = spread.astype(jnp.bfloat16).reshape(tokens, range_size)
-    partial = jnp.dot(spread, weights, preferred_element_type=jnp.float32).astype(jnp.bfloat16)
-    decoded = lax.psum_scatter(partial, "tok", scatter_dimension=0, tiled=True).astype(jnp.float32)
+    half = weights.shape[1] // 2
+    w_first, w_second = weights[:, :half], weights[:, half:]
+    partial_first = jnp.dot(spread, w_first, preferred_element_type=jnp.float32).astype(jnp.bfloat16)
+    decoded_first = lax.psum_scatter(partial_first, "tok", scatter_dimension=0, tiled=True)
+    partial_second = jnp.dot(spread, w_second, preferred_element_type=jnp.float32).astype(jnp.bfloat16)
+    received = lax.all_to_all(partial_second, "tok", split_axis=0, concat_axis=0, tiled=True)
+    decoded_second = jnp.sum(
+        received.reshape(owners, -1, received.shape[1]).astype(jnp.float32), axis=0
+    )
+    decoded = jnp.concatenate([decoded_first.astype(jnp.float32), decoded_second], axis=1)
     recon_full, grad_sum = layer_chain(decoded, carry_gain, earlier_sum, targets)
     grad_low = grad_sum.astype(jnp.bfloat16)
-    segment = lax.all_gather(grad_low, "tok", axis=0, tiled=True)
+    segment_first = lax.all_gather(grad_low[:, :half], "tok", axis=0, tiled=True)
+    copies = jnp.broadcast_to(grad_low[None, :, half:], (owners, grad_low.shape[0], half))
+    segment_second = lax.all_to_all(copies, "tok", split_axis=0, concat_axis=0, tiled=True)
+    segment = jnp.concatenate(
+        [segment_first, segment_second.reshape(owners * grad_low.shape[0], half)], axis=1
+    )
     products = lax.dot_general(
         segment, weights, (((1,), (1,)), ((), ())), preferred_element_type=jnp.float32
     )

time: 481 us -> 503 us (1.046)
  starting transfers between devices: 10.8 us -> 21.1 us
  local copies, waits for them, and re-layouts: 3.2 us -> 11.1 us
  waiting for transfers between devices: 313 us -> 306 us
    reduce_scatter x1, waiting for transfers between devices: 148 us -> 18.2 us  [on_device(): lax.psum_scatter(partial_first, 'tok', scatter_dimension=0, tiled=True)]
    all_to_all x0 -> x2, waiting for transfers between devices: none -> 108 us  [the longest x1 104 us: on_device(): lax.all_to_all(partial_second, 'tok', split_axis=0, concat_axis=0, tiled=...]
    all_gather x1, waiting for transfers between devices: 125 us -> 140 us  [on_device(): lax.all_gather(grad_low[:, :half], 'tok', axis=0, tiled=True)]
    all_to_all x0 -> x2, starting transfers between devices: none -> 10.1 us  [the longest x1 5.52 us: on_device(): lax.all_to_all(copies, 'tok', split_axis=0, concat_axis=0, tiled=True)]
    dot_general x1 -> x2, matrix products: 41.3 us -> 45.8 us  [the longest x1 24 us: on_device(): jnp.dot(spread, w_second, preferred_element_type=jnp.float32)]
  transfers between devices with their start and end apart: 6 -> 8, of which waited for: 5 -> 7; matrix products, arithmetic and copies ran while one was open for 1% -> 8% of each run, Pallas kernels for 0% -> 0%
where the time goes in v6:
time: 503 us; the launch traced here: 502 us
  waiting for transfers between devices  306 us (61%)
  matrix products  125 us (25%)
  starting transfers between devices  21.1 us (4%)
  other arithmetic  17.4 us (3%)
  between operations  15.7 us (3%)
  local copies, waits for them, and re-layouts  11.1 us (2%)
  blocking collectives  5.25 us (1%)
    all_gather x1, waiting for transfers between devices, on_device(): lax.all_gather(grad_low[:, :half], 'tok', axis=0, tiled=True)  140 us
    all_to_all x1, waiting for transfers between devices, on_device(): lax.all_to_all(partial_second, 'tok', split_axis=0, concat_axis=0, tiled=...  104 us
    dot_general x1, matrix products, on_device(): lax.dot_general(segment, weights, (((1,), (1,)), ((), ())), preferred_ele...  44.8 us
    all_gather x1, waiting for transfers between devices, layer_chain(): lax.all_gather(decoded.astype(jnp.bfloat16), 'layer', axis=0, tiled=False)  27.6 us
    dot_general x1, matrix products, on_device(): jnp.einsum('thl,tkl->tkh', products, low_hot.astype(jnp.float32), precisi...  24.7 us
    dot_general x1, matrix products, on_device(): jnp.dot(spread, w_second, preferred_element_type=jnp.float32)  24 us
    dot_general x1, matrix products, on_device(): jnp.dot(spread, w_first, preferred_element_type=jnp.float32)  21.8 us
    reduce_scatter x1, waiting for transfers between devices, on_device(): lax.psum_scatter(partial_first, 'tok', scatter_dimension=0, tiled=True)  18.2 us
  transfers between devices with their start and end apart: 8, of which 7 were waited for; matrix products, arithmetic and copies ran while one was open for 8% of the time, Pallas kernels for 0%

profile of v6, /device:TPU:0, one launch (start us, length us, event | category | flops | bytes accessed | tf_op | source)
XLA Modules:
  0.0 501.8 jit_solution(18060377345678664662)
XLA Ops:
  8.0 0.7 bitcast_convert_fusion
  8.7 0.7 convert_bitcast_fusion.1
  9.4 0.7 broadcast_in_dim.26
  10.1 7.3 %all-to-all-start = ((f32[8,128,64]{1,2,0:T(8,128)}), f32[8,128,64]{1,2,0:T(8,128)S(1)}, u32[]{:S(2)}, u32[]{:S(2)}) async-start(f32[8,128,64]{1,2,0:T(8,128)} %broadcast_in_dim.26), calls=%async_computation | async-start | bytes 524288 | tf_op jit(solution)/shard_map/all_to_all | solution.py:27
  17.4 0.0 reduce-scatter.2.cloned.1.call-start
  17.5 8.9 %all-to-all-done = f32[8,128,64]{1,2,0:T(8,128)S(1)} async-done(((f32[8,128,64]{1,2,0:T(8,128)}), f32[8,128,64]{1,2,0:T(8,128)S(1)}, u32[]{:S(2)}, u32[]{:S(2)}) %all-to-all-start) | async-done | bytes 262176 | tf_op jit(solution)/shard_map/all_to_all | solution.py:27
  26.4 0.1 fusion.46
  26.5 0.1 add_select_fusion
  26.6 0.2 copy.17
  26.8 0.2 copy.16
  27.0 0.2 copy.18
  27.2 9.7 %fusion.19 = bf16[1024,32,128]{2,1,0:T(8,128)(2,1)S(1)} fusion(s32[1024,32]{1,0:T(8,128)S(1)} %copy.18, s32[1024,32]{1,0:T(8,128)S(1)} %copy.16, bf16[1024,32]{1,0:T(8,128)(2,1)S(1)} %copy.17), kind=kOutput, calls=%fused_computation.23 | convolution fusion | flops 278921216 | bytes 8716288 | tf_op jit(solution)/shard_map/tkh,tkl->thl/dot_general | solution.py:65
  36.9 3.2 copy-done.4
  40.1 21.8 %fusion.24 = bf16[1024,2048]{1,0:T(8,128)(2,1)} fusion(bf16[4096,4096]{1,0:T(8,128)(2,1)} %bitcast.104, bf16[128,8,32,128]{3,2,1,0:T(8,128)(2,1)S(1)} %bitcast.107), kind=kOutput, calls=%fused_computation.26 | convolution fusion | flops 17181966336 | bytes 29360128 | tf_op jit(solution)/shard_map/dot_general | solution.py:71
  62.0 0.0 reduce-scatter.2.cloned.1.call-update
  62.0 24.0 %fusion.29 = bf16[1024,2048]{1,0:T(8,128)(2,1)} fusion(bf16[4096,4096]{1,0:T(8,128)(2,1)} %bitcast.105, bf16[128,8,32,128]{3,2,1,0:T(8,128)(2,1)} %bitcast.108), kind=kOutput, calls=%fused_computation.27 | convolution fusion | flops 17181966336 | bytes 29360128 | tf_op jit(solution)/shard_map/dot_general | solution.py:73
  86.0 4.6 all-to-all-start.1
  90.5 0.0 all-gather.7.cloned.1.call-start
  90.6 0.5 all-gather.7.cloned.1.call-update
  91.1 0.0 copy-start.3
  91.1 0.2 all-gather.5.cloned.1.call-start
  91.4 103.6 %all-to-all-done.1 = bf16[8,128,2048]{2,1,0:T(8,128)(2,1)} async-done(((bf16[8,128,2048]{2,1,0:T(8,128)(2,1)}), bf16[8,128,2048]{2,1,0:T(8,128)(2,1)}, u32[]{:S(2)}, u32[]{:S(2)}) %all-to-all-start.1) | async-done | bytes 4194336 | tf_op jit(solution)/shard_map/all_to_all | solution.py:74
  195.0 3.4 convert_reduce_fusion
  198.3 0.0 copy-start
  198.3 0.1 convert_bitcast_fusion
  198.4 18.2 %reduce-scatter.2.cloned.1.call-done = bf16[128,2048]{1,0:T(8,128)(2,1)} async-done(((bf16[1024,2048]{1,0:T(8,128)(2,1)}), bf16[128,2048]{1,0:T(8,128)(2,1)}) %reduce-scatter.2.cloned.1.call-update) | async-done | bytes 524304 | tf_op jit(solution)/shard_map/reduce_scatter | solution.py:72
  216.6 2.1 pad_maximum_fusion.1
  218.7 0.0 all-gather.5.cloned.1.call-update
  218.7 0.0 all-gather.9.cloned.1.call-start
  218.7 0.0 copy-done.3
  218.8 5.2 %all-gather = f32[4,1,4096]{2,1,0:T(1,128)S(1)} all-gather(f32[1,1,4096]{2,1,0:T(1,128)S(1)} %bitcast.102), channel_id=1, replica_groups=mesh['layer'=4,'tok'=8] {'layer'}, dimensions={0}, use_global_device_ids=true | all-gather | bytes 81920 | tf_op jit(solution)/shard_map/all_gather | solution.py:35
  224.0 1.2 convert_element_type.105
  225.2 0.0 all-gather.7.cloned.1.call-done
  225.2 27.6 %all-gather.5.cloned.1.call-done = bf16[4,128,4096]{2,1,0:T(8,128)(2,1)} async-done(((bf16[1,128,4096]{2,1,0:T(8,128)(2,1)}), bf16[4,128,4096]{2,1,0:T(8,128)(2,1)}) %all-gather.5.cloned.1.call-update) | async-done | bytes 4194320 | tf_op jit(solution)/shard_map/all_gather | solution.py:37
  252.9 4.6 fusion.40
  257.5 1.1 fusion.53
  258.6 0.0 all-gather.9.cloned.1.call-update
  258.6 3.5 broadcast_in_dim.45
  262.2 5.5 %all-to-all-start.2 = ((bf16[8,128,2048]{2,1,0:T(8,128)(2,1)}), bf16[8,128,2048]{2,1,0:T(8,128)(2,1)}, u32[]{:S(2)}, u32[]{:S(2)}) async-start(bf16[8,128,2048]{2,1,0:T(8,128)(2,1)} %broadcast_in_dim.45), calls=%async_computation.3 | async-start | bytes 8388608 | tf_op jit(solution)/shard_map/all_to_all | solution.py:83
  267.7 139.8 %all-gather.9.cloned.1.call-done = bf16[1024,2048]{1,0:T(8,128)(2,1)} async-done(((bf16[128,2048]{1,0:T(8,128)(2,1)}), bf16[1024,2048]{1,0:T(8,128)(2,1)}) %all-gather.9.cloned.1.call-update) | async-done | bytes 4194320 | tf_op jit(solution)/shard_map/all_gather | solution.py:81
  407.5 4.2 all-to-all-done.2
  411.6 44.8 %fusion.11 = f32[1024,32,128]{2,0,1:T(8,128)} fusion(bf16[32,128,4096]{2,1,0:T(8,128)(2,1)} %bitcast.106, bf16[1024,2048]{1,0:T(8,128)(2,1)} %bitcast.20, bf16[1024,2048]{1,0:T(8,128)(2,1)} %all-gather.9.cloned.1.call-done), kind=kOutput, calls=%fused_computation.14 | convolution fusion | flops 34376515584 | bytes 58720256 | tf_op jit(solution)/shard_map/dot_general | solution.py:87
  456.5 24.7 %select_reduce_fusion = f32[1024,32]{1,0:T(8,128)} fusion(s32[1024,32]{1,0:T(8,128)} %copy-done.1, f32[1024,32,128]{2,0,1:T(8,128)} %fusion.11, s32[1024,32]{1,0:T(8,128)} %copy-done.2), kind=kOutput, calls=%fused_computation.6 | convolution fusion | flops 1617920000 | bytes 17170432 | tf_op jit(solution)/shard_map/thl,tkl->tkh/dot_general | solution.py:91
  481.2 1.9 copy.21
  483.0 3.4 all-to-all-start.3
  486.4 3.8 fusion.45
  490.2 3.5 all-to-all-done.3
  493.8 0.6 reduce_sum.29
  (10 shorter events, 0.1 us)
Async XLA Ops:
  10.1 16.2 %all-to-all-start = ((f32[8,128,64]{1,2,0:T(8,128)}), f32[8,128,64]{1,2,0:T(8,128)S(1)}, u32[]{:S(2)}, u32[]{:S(2)}) async-start(f32[8,128,64]{1,2,0:T(8,128)} %broadcast_in_dim.26), calls=%async_computation | async-start | bytes 524288 | tf_op jit(solution)/shard_map/all_to_all | solution.py:27
  17.4 199.1 %reduce-scatter.2.cloned.1.call-start = ((), (), s32[]{:S(2)}) async-start(), calls=%async_computation.5 | async-start | bytes 4718592 | tf_op jit(solution)/shard_map/reduce_scatter | solution.py:72
  27.0 9.9 %copy-start.1 = (s32[1024,32]{1,0:T(8,128)}, s32[1024,32]{1,0:T(8,128)S(1)}, u32[]{:S(2)}) copy-start(s32[1024,32]{1,0:T(8,128)S(1)} %copy.16) | copy-start | bytes 393220
  27.2 9.7 %copy-start.2 = (s32[1024,32]{1,0:T(8,128)}, s32[1024,32]{1,0:T(8,128)S(1)}, u32[]{:S(2)}) copy-start(s32[1024,32]{1,0:T(8,128)S(1)} %copy.18) | copy-start | bytes 393220
  36.9 3.2 copy-start.4
  86.0 109.0 %all-to-all-start.1 = ((bf16[8,128,2048]{2,1,0:T(8,128)(2,1)}), bf16[8,128,2048]{2,1,0:T(8,128)(2,1)}, u32[]{:S(2)}, u32[]{:S(2)}) async-start(bf16[8,128,2048]{2,1,0:T(8,128)(2,1)} %bitcast.91), calls=%async_computation.2 | async-start | bytes 8388608 | tf_op jit(solution)/shard_map/all_to_all | solution.py:74
  90.5 134.7 %all-gather.7.cloned.1.call-start = ((), (), s32[]{:S(2)}) async-start(), calls=%async_computation.7 | async-start | bytes 5242880 | tf_op jit(solution)/shard_map/all_gather | solution.py:36
  91.1 127.6 %copy-start.3 = (f32[1,4096]{1,0:T(1,128)S(1)}, f32[1,4096]{1,0:T(1,128)}, u32[]{:S(2)}) copy-start(f32[1,4096]{1,0:T(1,128)} %param.9) | copy-start | bytes 49156
  91.1 161.7 %all-gather.5.cloned.1.call-start = ((), (), s32[]{:S(2)}) async-start(), calls=%async_computation.6 | async-start | bytes 5242880 | tf_op jit(solution)/shard_map/all_gather | solution.py:37
  198.3 54.5 %copy-start = (bf16[128,4096]{1,0:T(8,128)(2,1)S(1)}, bf16[128,4096]{1,0:T(8,128)(2,1)}, u32[]{:S(2)}) copy-start(bf16[128,4096]{1,0:T(8,128)(2,1)} %param.10) | copy-start | bytes 3145732
  218.7 188.8 %all-gather.9.cloned.1.call-start = ((), (), s32[]{:S(2)}) async-start(), calls=%async_computation.8 | async-start | bytes 4718592 | tf_op jit(solution)/shard_map/all_gather | solution.py:81
  262.2 149.4 %all-to-all-start.2 = ((bf16[8,128,2048]{2,1,0:T(8,128)(2,1)}), bf16[8,128,2048]{2,1,0:T(8,128)(2,1)}, u32[]{:S(2)}, u32[]{:S(2)}) async-start(bf16[8,128,2048]{2,1,0:T(8,128)(2,1)} %broadcast_in_dim.45), calls=%async_computation.3 | async-start | bytes 8388608 | tf_op jit(solution)/shard_map/all_to_all | solution.py:83
  483.0 10.7 %all-to-all-start.3 = ((f32[8,128,32]{1,2,0:T(8,128)}), f32[8,128,32]{1,2,0:T(8,128)S(1)}, u32[]{:S(2)}, u32[]{:S(2)}) async-start(f32[8,128,32]{1,2,0:T(8,128)} %copy.21), calls=%async_computation.4 | async-start | bytes 262144 | tf_op jit(solution)/shard_map/all_to_all | solution.py:99
Sparse Core Ops, SparseCore 0:
  62.1 154.3 reduce-scatter.1
  258.8 148.6 all-gather.8
Sparse Core Ops, SparseCore 1:
  92.7 35.6 all-gather.6
  218.8 34.0 all-gather.4

commit v7 on v6

--- a/solution.py
+++ b/solution.py
@@ -78,12 +78,7 @@
     decoded = jnp.concatenate([decoded_first.astype(jnp.float32), decoded_second], axis=1)
     recon_full, grad_sum = layer_chain(decoded, carry_gain, earlier_sum, targets)
     grad_low = grad_sum.astype(jnp.bfloat16)
-    segment_first = lax.all_gather(grad_low[:, :half], "tok", axis=0, tiled=True)
-    copies = jnp.broadcast_to(grad_low[None, :, half:], (owners, grad_low.shape[0], half))
-    segment_second = lax.all_to_all(copies, "tok", split_axis=0, concat_axis=0, tiled=True)
-    segment = jnp.concatenate(
-        [segment_first, segment_second.reshape(owners * grad_low.shape[0], half)], axis=1
-    )
+    segment = lax.all_gather(grad_low, "tok", axis=0, tiled=True)
     products = lax.dot_general(
         segment, weights, (((1,), (1,)), ((), ())), preferred_element_type=jnp.float32
     )
@@ -92,7 +87,7 @@
         "thl,tkl->tkh",
         products,
         low_hot.astype(jnp.float32),
-        precision=lax.Precision.HIGHEST,
+        precision=lax.Precision.HIGH,
         preferred_element_type=jnp.float32,
     )
     partial_grad = jnp.sum(jnp.where(high_hot, picked_low, 0.0), axis=-1)

time: 503 us -> 468 us (0.930)
  waiting for transfers between devices: 306 us -> 287 us
  matrix products: 125 us -> 119 us
  starting transfers between devices: 21.1 us -> 15.5 us
    all_gather x1, waiting for transfers between devices: 140 us -> 125 us  [on_device(): segment = lax.all_gather(grad_low, 'tok', axis=0, tiled=True)]
    all_to_all x1 -> x0, starting transfers between devices: 5.52 us -> none  [on_device(): lax.all_to_all(copies, 'tok', split_axis=0, concat_axis=0, tiled=True)]
  transfers between devices with their start and end apart: 8 -> 7, of which waited for: 7 -> 6; matrix products, arithmetic and copies ran while one was open for 8% -> 7% of each run, Pallas kernels for 0% -> 0%
where the time goes in v7:
time: 468 us; the launch traced here: 467 us
  waiting for transfers between devices  287 us (61%)
  matrix products  119 us (25%)
  other arithmetic  18.2 us (4%)
  between operations  15.7 us (3%)
  starting transfers between devices  15.5 us (3%)
  local copies, waits for them, and re-layouts  6.42 us (1%)
  blocking collectives  5.25 us (1%)
    all_gather x1, waiting for transfers between devices, on_device(): segment = lax.all_gather(grad_low, 'tok', axis=0, tiled=True)  125 us
    all_to_all x1, waiting for transfers between devices, on_device(): lax.all_to_all(partial_second, 'tok', split_axis=0, concat_axis=0, tiled=...  104 us
    dot_general x1, matrix products, on_device(): lax.dot_general(segment, weights, (((1,), (1,)), ((), ())), preferred_ele...  43.1 us
    all_gather x1, waiting for transfers between devices, layer_chain(): lax.all_gather(decoded.astype(jnp.bfloat16), 'layer', axis=0, tiled=False)  27.6 us
    dot_general x1, matrix products, on_device(): jnp.dot(spread, w_second, preferred_element_type=jnp.float32)  24 us
    dot_general x1, matrix products, on_device(): jnp.dot(spread, w_first, preferred_element_type=jnp.float32)  21.9 us
    dot_general x1, matrix products, on_device(): jnp.einsum('thl,tkl->tkh', products, low_hot.astype(jnp.float32), precisi...  20.3 us
    reduce_scatter x1, waiting for transfers between devices, on_device(): lax.psum_scatter(partial_first, 'tok', scatter_dimension=0, tiled=True)  18.2 us
  transfers between devices with their start and end apart: 7, of which 6 were waited for; matrix products, arithmetic and copies ran while one was open for 7% of the time, Pallas kernels for 0%

profile of v7, /device:TPU:0, one launch (start us, length us, event | category | flops | bytes accessed | tf_op | source)
XLA Modules:
  0.0 467.5 jit_solution(11131684662799173570)
XLA Ops:
  8.0 0.7 bitcast_convert_fusion
  8.7 0.7 convert_bitcast_fusion.1
  9.4 0.7 broadcast_in_dim.35
  10.1 7.3 %all-to-all-start = ((f32[8,128,64]{1,2,0:T(8,128)}), f32[8,128,64]{1,2,0:T(8,128)S(1)}, u32[]{:S(2)}, u32[]{:S(2)}) async-start(f32[8,128,64]{1,2,0:T(8,128)} %broadcast_in_dim.35), calls=%async_computation | async-start | bytes 524288 | tf_op jit(solution)/shard_map/all_to_all | solution.py:27
  17.4 0.0 reduce-scatter.2.cloned.1.call-start
  17.5 8.9 %all-to-all-done = f32[8,128,64]{1,2,0:T(8,128)S(1)} async-done(((f32[8,128,64]{1,2,0:T(8,128)}), f32[8,128,64]{1,2,0:T(8,128)S(1)}, u32[]{:S(2)}, u32[]{:S(2)}) %all-to-all-start) | async-done | bytes 262176 | tf_op jit(solution)/shard_map/all_to_all | solution.py:27
  26.4 0.1 fusion.45
  26.5 0.1 add_select_fusion
  26.6 0.2 copy.17
  26.8 0.2 copy.16
  27.0 0.0 copy-start.1
  27.0 0.2 copy.18
  27.2 0.0 copy-start.2
  27.2 9.7 %fusion.18 = bf16[1024,32,128]{2,1,0:T(8,128)(2,1)S(1)} fusion(s32[1024,32]{1,0:T(8,128)S(1)} %copy.18, s32[1024,32]{1,0:T(8,128)S(1)} %copy.16, bf16[1024,32]{1,0:T(8,128)(2,1)S(1)} %copy.17), kind=kOutput, calls=%fused_computation.21 | convolution fusion | flops 278921216 | bytes 8716288 | tf_op jit(solution)/shard_map/tkh,tkl->thl/dot_general | solution.py:65
  36.9 0.0 copy-done.1
  36.9 0.0 copy-done.2
  36.9 0.0 copy-start.4
  36.9 3.2 copy-done.4
  40.1 21.9 %fusion.23 = bf16[1024,2048]{1,0:T(8,128)(2,1)} fusion(bf16[4096,4096]{1,0:T(8,128)(2,1)} %bitcast.100, bf16[128,8,32,128]{3,2,1,0:T(8,128)(2,1)S(1)} %bitcast.103), kind=kOutput, calls=%fused_computation.24 | convolution fusion | flops 17181966336 | bytes 29360128 | tf_op jit(solution)/shard_map/dot_general | solution.py:71
  62.0 0.0 reduce-scatter.2.cloned.1.call-update
  62.0 24.0 %fusion.28 = bf16[1024,2048]{1,0:T(8,128)(2,1)} fusion(bf16[4096,4096]{1,0:T(8,128)(2,1)} %bitcast.101, bf16[128,8,32,128]{3,2,1,0:T(8,128)(2,1)} %bitcast.104), kind=kOutput, calls=%fused_computation.25 | convolution fusion | flops 17181966336 | bytes 29360128 | tf_op jit(solution)/shard_map/dot_general | solution.py:73
  86.0 4.5 all-to-all-start.1
  90.6 0.0 all-gather.7.cloned.1.call-start
  90.7 0.5 all-gather.7.cloned.1.call-update
  91.2 0.2 all-gather.5.cloned.1.call-start
  91.4 103.6 %all-to-all-done.1 = bf16[8,128,2048]{2,1,0:T(8,128)(2,1)} async-done(((bf16[8,128,2048]{2,1,0:T(8,128)(2,1)}), bf16[8,128,2048]{2,1,0:T(8,128)(2,1)}, u32[]{:S(2)}, u32[]{:S(2)}) %all-to-all-start.1) | async-done | bytes 4194336 | tf_op jit(solution)/shard_map/all_to_all | solution.py:74
  195.0 3.4 convert_reduce_fusion
  198.3 0.0 copy-start.3
  198.4 0.1 convert_bitcast_fusion
  198.4 18.2 %reduce-scatter.2.cloned.1.call-done = bf16[128,2048]{1,0:T(8,128)(2,1)} async-done(((bf16[1024,2048]{1,0:T(8,128)(2,1)}), bf16[128,2048]{1,0:T(8,128)(2,1)}) %reduce-scatter.2.cloned.1.call-update) | async-done | bytes 524304 | tf_op jit(solution)/shard_map/reduce_scatter | solution.py:72
  216.6 2.2 pad_maximum_fusion.1
  218.8 0.0 all-gather.5.cloned.1.call-update
  218.8 0.0 all-gather.9.cloned.1.call-start
  218.9 0.0 copy-done.3
  218.9 5.2 %all-gather = f32[4,1,4096]{2,1,0:T(1,128)S(1)} all-gather(f32[1,1,4096]{2,1,0:T(1,128)S(1)} %bitcast.98), channel_id=1, replica_groups=mesh['layer'=4,'tok'=8] {'layer'}, dimensions={0}, use_global_device_ids=true | all-gather | bytes 81920 | tf_op jit(solution)/shard_map/all_gather | solution.py:35
  224.2 1.2 convert_element_type.105
  225.3 0.0 all-gather.7.cloned.1.call-done
  225.4 27.6 %all-gather.5.cloned.1.call-done = bf16[4,128,4096]{2,1,0:T(8,128)(2,1)} async-done(((bf16[1,128,4096]{2,1,0:T(8,128)(2,1)}), bf16[4,128,4096]{2,1,0:T(8,128)(2,1)}) %all-gather.5.cloned.1.call-update) | async-done | bytes 4194320 | tf_op jit(solution)/shard_map/all_gather | solution.py:37
  253.0 5.4 %fusion.39 = bf16[128,4096]{1,0:T(8,128)(2,1)} fusion(bf16[128,4096]{1,0:T(8,128)(2,1)S(1)} %copy-done, f32[128,2048]{1,0:T(8,128)S(1)} %convert_reduce_fusion, f32[128,2048]{1,0:T(8,128)S(1)} %convert_element_type.105, bf16[4,128,4096]{2,1,0:T(8,128)(2,1)} %all-gather.7.cloned.1.call-done, f32[4096]{0:T(1024)S(1)} %bitcast.96, f32[4096]{0:T(1024)S(1)} %bitcast.92, ...), kind=kLoop, calls=%fused_computation.35 | loop fusion | flops 19398656 | bytes 12648452 | tf_op jit(solution)/shard_map/convert_element_type | solution.py:80
  258.4 0.0 all-gather.9.cloned.1.call-update
  258.4 125.1 %all-gather.9.cloned.1.call-done = bf16[1024,4096]{1,0:T(8,128)(2,1)} async-done(((bf16[128,4096]{1,0:T(8,128)(2,1)}), bf16[1024,4096]{1,0:T(8,128)(2,1)}) %all-gather.9.cloned.1.call-update) | async-done | bytes 8388624 | tf_op jit(solution)/shard_map/all_gather | solution.py:81
  383.5 43.1 %fusion.11 = f32[1024,32,128]{2,0,1:T(8,128)} fusion(bf16[32,128,4096]{2,1,0:T(8,128)(2,1)} %bitcast.102, bf16[1024,4096]{1,0:T(8,128)(2,1)} %all-gather.9.cloned.1.call-done), kind=kOutput, calls=%fused_computation.13 | convolution fusion | flops 34359738368 | bytes 58720256 | tf_op jit(solution)/shard_map/dot_general | solution.py:82
  426.6 20.3 %select_reduce_fusion = f32[1024,32]{1,0:T(8,128)} fusion(s32[1024,32]{1,0:T(8,128)} %copy-done.1, f32[1024,32,128]{2,0,1:T(8,128)} %fusion.11, s32[1024,32]{1,0:T(8,128)} %copy-done.2), kind=kOutput, calls=%fused_computation.6 | convolution fusion | flops 812613632 | bytes 17170432 | tf_op jit(solution)/shard_map/thl,tkl->tkh/dot_general | solution.py:86
  446.9 1.9 copy.21
  448.8 3.4 all-to-all-start.2
  452.2 3.8 fusion.44
  456.0 3.5 all-to-all-done.2
  459.5 0.6 reduce_sum.29
  (6 shorter events, 0.0 us)
Async XLA Ops:
  10.1 16.2 %all-to-all-start = ((f32[8,128,64]{1,2,0:T(8,128)}), f32[8,128,64]{1,2,0:T(8,128)S(1)}, u32[]{:S(2)}, u32[]{:S(2)}) async-start(f32[8,128,64]{1,2,0:T(8,128)} %broadcast_in_dim.35), calls=%async_computation | async-start | bytes 524288 | tf_op jit(solution)/shard_map/all_to_all | solution.py:27
  17.4 199.2 %reduce-scatter.2.cloned.1.call-start = ((), (), s32[]{:S(2)}) async-start(), calls=%async_computation.4 | async-start | bytes 4718592 | tf_op jit(solution)/shard_map/reduce_scatter | solution.py:72
  27.0 9.9 %copy-start.1 = (s32[1024,32]{1,0:T(8,128)}, s32[1024,32]{1,0:T(8,128)S(1)}, u32[]{:S(2)}) copy-start(s32[1024,32]{1,0:T(8,128)S(1)} %copy.16) | copy-start | bytes 393220
  27.2 9.7 %copy-start.2 = (s32[1024,32]{1,0:T(8,128)}, s32[1024,32]{1,0:T(8,128)S(1)}, u32[]{:S(2)}) copy-start(s32[1024,32]{1,0:T(8,128)S(1)} %copy.18) | copy-start | bytes 393220
  36.9 3.2 copy-start.4
  86.0 108.9 %all-to-all-start.1 = ((bf16[8,128,2048]{2,1,0:T(8,128)(2,1)}), bf16[8,128,2048]{2,1,0:T(8,128)(2,1)}, u32[]{:S(2)}, u32[]{:S(2)}) async-start(bf16[8,128,2048]{2,1,0:T(8,128)(2,1)} %bitcast.87), calls=%async_computation.2 | async-start | bytes 8388608 | tf_op jit(solution)/shard_map/all_to_all | solution.py:74
  90.6 134.8 %all-gather.7.cloned.1.call-start = ((), (), s32[]{:S(2)}) async-start(), calls=%async_computation.6 | async-start | bytes 5242880 | tf_op jit(solution)/shard_map/all_gather | solution.py:36
  91.2 161.8 %all-gather.5.cloned.1.call-start = ((), (), s32[]{:S(2)}) async-start(), calls=%async_computation.5 | async-start | bytes 5242880 | tf_op jit(solution)/shard_map/all_gather | solution.py:37
  198.3 20.5 %copy-start.3 = (f32[1,4096]{1,0:T(1,128)S(1)}, f32[1,4096]{1,0:T(1,128)}, u32[]{:S(2)}) copy-start(f32[1,4096]{1,0:T(1,128)} %param.9) | copy-start | bytes 49156
  216.6 36.4 %copy-start = (bf16[128,4096]{1,0:T(8,128)(2,1)S(1)}, bf16[128,4096]{1,0:T(8,128)(2,1)}, u32[]{:S(2)}) copy-start(bf16[128,4096]{1,0:T(8,128)(2,1)} %param.10) | copy-start | bytes 3145732
  218.8 164.7 %all-gather.9.cloned.1.call-start = ((), (), s32[]{:S(2)}) async-start(), calls=%async_computation.7 | async-start | bytes 9437184 | tf_op jit(solution)/shard_map/all_gather | solution.py:81
  448.8 10.7 %all-to-all-start.2 = ((f32[8,128,32]{1,2,0:T(8,128)}), f32[8,128,32]{1,2,0:T(8,128)S(1)}, u32[]{:S(2)}, u32[]{:S(2)}) async-start(f32[8,128,32]{1,2,0:T(8,128)} %copy.21), calls=%async_computation.3 | async-start | bytes 262144 | tf_op jit(solution)/shard_map/all_to_all | solution.py:94
Sparse Core Ops, SparseCore 0:
  62.2 154.4 reduce-scatter.1
  258.6 124.9 all-gather.8
Sparse Core Ops, SparseCore 1:
  92.7 35.6 all-gather.6
  218.9 34.0 all-gather.4

commit v8 on v7

--- a/solution.py
+++ b/solution.py
@@ -32,8 +32,20 @@
 
 
 def layer_chain(decoded, carry_gain, earlier_sum, targets):
-    gains = lax.all_gather(carry_gain[0], "layer", axis=0, tiled=False)
-    targets_all = lax.all_gather(targets[0], "layer", axis=0, tiled=False)
+    gain = carry_gain[0][None, :]
+    gain_high = gain.astype(jnp.bfloat16)
+    rest = gain - gain_high.astype(jnp.float32)
+    gain_mid = rest.astype(jnp.bfloat16)
+    gain_low = (rest - gain_mid.astype(jnp.float32)).astype(jnp.bfloat16)
+    rows = targets.shape[1]
+    packed = jnp.concatenate([targets[0], gain_high, gain_mid, gain_low], axis=0)
+    packed_all = lax.all_gather(packed, "layer", axis=0, tiled=False)
+    targets_all = packed_all[:, :rows]
+    gains = (
+        packed_all[:, rows].astype(jnp.float32)
+        + packed_all[:, rows + 1].astype(jnp.float32)
+        + packed_all[:, rows + 2].astype(jnp.float32)
+    )
     decoded_all = lax.all_gather(decoded.astype(jnp.bfloat16), "layer", axis=0, tiled=False)
     layers = gains.shape[0]
     me = lax.axis_index("layer")
@@ -78,19 +90,29 @@
     decoded = jnp.concatenate([decoded_first.astype(jnp.float32), decoded_second], axis=1)
     recon_full, grad_sum = layer_chain(decoded, carry_gain, earlier_sum, targets)
     grad_low = grad_sum.astype(jnp.bfloat16)
-    segment = lax.all_gather(grad_low, "tok", axis=0, tiled=True)
-    products = lax.dot_general(
-        segment, weights, (((1,), (1,)), ((), ())), preferred_element_type=jnp.float32
-    )
-    products = products.reshape(tokens, range_size // LANES, LANES)
-    picked_low = jnp.einsum(
-        "thl,tkl->tkh",
-        products,
-        low_hot.astype(jnp.float32),
-        precision=lax.Precision.HIGH,
-        preferred_element_type=jnp.float32,
-    )
-    partial_grad = jnp.sum(jnp.where(high_hot, picked_low, 0.0), axis=-1)
+    rows = grad_low.shape[0]
+    pieces = 2 if rows % 32 == 0 else 1
+    span = rows // pieces
+    picked = []
+    for c in range(pieces):
+        segment = lax.all_gather(grad_low[c * span:(c + 1) * span], "tok", axis=0, tiled=True)
+        products = lax.dot_general(
+            segment, weights, (((1,), (1,)), ((), ())), preferred_element_type=jnp.float32
+        )
+        products = products.reshape(owners * span, range_size // LANES, LANES)
+        own_rows = lambda a: a.reshape((owners, rows) + a.shape[1:])[:, c * span:(c + 1) * span].reshape(
+            (owners * span,) + a.shape[1:]
+        )
+        picked_low = jnp.einsum(
+            "thl,tkl->tkh",
+            products,
+            own_rows(low_hot).astype(jnp.float32),
+            precision=lax.Precision.HIGH,
+            preferred_element_type=jnp.float32,
+        )
+        chosen = jnp.sum(jnp.where(own_rows(high_hot), picked_low, 0.0), axis=-1)
+        picked.append(chosen.reshape(owners, span, -1))
+    partial_grad = jnp.concatenate(picked, axis=1).reshape(owners * rows, -1)
     returned = lax.all_to_all(partial_grad, "tok", split_axis=0, concat_axis=0, tiled=True)
     code_grad = jnp.sum(returned.reshape(owners, -1, returned.shape[1]), axis=0)
     return (recon_full.astype(jnp.bfloat16)[None], code_grad[None])

time: 468 us -> 470 us (level); the launches traced: 467 us -> 462 us
  waiting for transfers between devices: 287 us -> 259 us
  other arithmetic: 18.2 us -> 32.6 us
  local copies, waits for them, and re-layouts: 6.42 us -> 15.4 us
  blocking collectives: 5.25 us -> 0 us
    all_gather x2 -> x3, waiting for transfers between devices: 125 us -> 94.7 us  [the longest x2 94.7 us: on_device(): lax.all_gather(grad_low[c * span:(c + 1) * span], 'tok', axis=0, tiled=True)]
    eq x0 -> x2, other arithmetic: none -> 10.8 us  [the longest x1 5.66 us: selectors(): low_hot = low[..., None] == jnp.arange(LANES, dtype=jnp.int32)]
    slice x0 -> x3, local copies, waits for them, and re-layouts: none -> 9.9 us  [the longest x2 8.83 us: on_device(): a.reshape((owners, rows) + a.shape[1:])[:, c * span:(c + 1) * span]]
    all_gather x1 -> x0, blocking collectives: 5.25 us -> none  [layer_chain(): gains = lax.all_gather(carry_gain[0], 'layer', axis=0, tiled=False)]
    dot_general x1 -> x2, matrix products: 43.1 us -> 45.9 us  [on_device(): lax.dot_general(segment, weights, (((1,), (1,)), ((), ())), preferred_ele...]
    dot_general x1 -> x2, matrix products: 20.3 us -> 21.4 us  [on_device(): jnp.einsum('thl,tkl->tkh', products, own_rows(low_hot).astype(jnp.float32...]
  transfers between devices with their start and end apart: 7 -> 8, of which waited for: 6 -> 7; matrix products, arithmetic and copies ran while one was open for 7% -> 20% of each run, Pallas kernels for 0% -> 0%
where the time goes in v8:
time: 470 us; the launch traced here: 462 us
  waiting for transfers between devices  259 us (55%)
  matrix products  123 us (26%)
  other arithmetic  32.6 us (7%)
  between operations  15.9 us (3%)
  starting transfers between devices  15.7 us (3%)
  local copies, waits for them, and re-layouts  15.4 us (3%)
    all_to_all x1, waiting for transfers between devices, on_device(): lax.all_to_all(partial_second, 'tok', split_axis=0, concat_axis=0, tiled=...  103 us
    all_gather x2, waiting for transfers between devices, on_device(): lax.all_gather(grad_low[c * span:(c + 1) * span], 'tok', axis=0, tiled=True)  94.7 us
    dot_general x2, matrix products, on_device(): lax.dot_general(segment, weights, (((1,), (1,)), ((), ())), preferred_ele...  45.9 us
    all_gather x1, waiting for transfers between devices, layer_chain(): lax.all_gather(decoded.astype(jnp.bfloat16), 'layer', axis=0, tiled=False)  31.4 us
    dot_general x1, matrix products, on_device(): jnp.dot(spread, w_second, preferred_element_type=jnp.float32)  24 us
    dot_general x1, matrix products, on_device(): jnp.dot(spread, w_first, preferred_element_type=jnp.float32)  21.9 us
    dot_general x2, matrix products, on_device(): jnp.einsum('thl,tkl->tkh', products, own_rows(low_hot).astype(jnp.float32...  21.4 us
    reduce_scatter x1, waiting for transfers between devices, on_device(): lax.psum_scatter(partial_first, 'tok', scatter_dimension=0, tiled=True)  18.2 us
  transfers between devices with their start and end apart: 8, of which 7 were waited for; matrix products, arithmetic and copies ran while one was open for 20% of the time, Pallas kernels for 0%

profile of v8, /device:TPU:0, one launch (start us, length us, event | category | flops | bytes accessed | tf_op | source)
XLA Modules:
  0.0 462.0 jit_solution(2503611786665094825)
XLA Ops:
  8.0 0.7 bitcast_convert_fusion
  8.7 0.7 convert_bitcast_fusion.1
  9.4 0.7 broadcast_in_dim.36
  10.1 7.3 %all-to-all-start = ((f32[8,128,64]{1,2,0:T(8,128)}), f32[8,128,64]{1,2,0:T(8,128)S(1)}, u32[]{:S(2)}, u32[]{:S(2)}) async-start(f32[8,128,64]{1,2,0:T(8,128)} %broadcast_in_dim.36), calls=%async_computation | async-start | bytes 524288 | tf_op jit(solution)/shard_map/all_to_all | solution.py:27
  17.4 0.0 reduce-scatter.2.cloned.1.call-start
  17.5 8.9 %all-to-all-done = f32[8,128,64]{1,2,0:T(8,128)S(1)} async-done(((f32[8,128,64]{1,2,0:T(8,128)}), f32[8,128,64]{1,2,0:T(8,128)S(1)}, u32[]{:S(2)}, u32[]{:S(2)}) %all-to-all-start) | async-done | bytes 262176 | tf_op jit(solution)/shard_map/all_to_all | solution.py:27
  26.4 0.1 fusion.50
  26.5 0.1 add_select_fusion
  26.6 0.2 copy.22
  26.8 0.2 copy.20
  27.0 0.2 copy.21
  27.2 9.7 %fusion.17 = bf16[1024,32,128]{2,1,0:T(8,128)(2,1)S(1)} fusion(s32[1024,32]{1,0:T(8,128)S(1)} %copy.22, s32[1024,32]{1,0:T(8,128)S(1)} %copy.20, bf16[1024,32]{1,0:T(8,128)(2,1)S(1)} %copy.21), kind=kOutput, calls=%fused_computation.23 | convolution fusion | flops 278921216 | bytes 8716288 | tf_op jit(solution)/shard_map/tkh,tkl->thl/dot_general | solution.py:77
  36.9 3.2 copy-done.9
  40.2 21.9 %fusion.26 = bf16[1024,2048]{1,0:T(8,128)(2,1)} fusion(bf16[4096,4096]{1,0:T(8,128)(2,1)} %bitcast.122, bf16[128,8,32,128]{3,2,1,0:T(8,128)(2,1)S(1)} %bitcast.126), kind=kOutput, calls=%fused_computation.30 | convolution fusion | flops 17181966336 | bytes 29360128 | tf_op jit(solution)/shard_map/dot_general | solution.py:83
  62.1 24.0 %fusion.31 = bf16[1024,2048]{1,0:T(8,128)(2,1)} fusion(bf16[4096,4096]{1,0:T(8,128)(2,1)} %bitcast.123, bf16[128,8,32,128]{3,2,1,0:T(8,128)(2,1)} %bitcast.127), kind=kOutput, calls=%fused_computation.31 | convolution fusion | flops 17181966336 | bytes 29360128 | tf_op jit(solution)/shard_map/dot_general | solution.py:85
  86.0 4.7 %all-to-all-start.1 = ((bf16[8,128,2048]{2,1,0:T(8,128)(2,1)}), bf16[8,128,2048]{2,1,0:T(8,128)(2,1)}, u32[]{:S(2)}, u32[]{:S(2)}) async-start(bf16[8,128,2048]{2,1,0:T(8,128)(2,1)} %bitcast.106), calls=%async_computation.2 | async-start | bytes 8388608 | tf_op jit(solution)/shard_map/all_to_all | solution.py:86
  90.7 0.0 all-gather.13.cloned.1.call-start
  90.9 1.2 maximum_bitcast_fusion
  92.0 0.2 all-gather.7.cloned.1.call-start
  92.3 102.7 %all-to-all-done.1 = bf16[8,128,2048]{2,1,0:T(8,128)(2,1)} async-done(((bf16[8,128,2048]{2,1,0:T(8,128)(2,1)}), bf16[8,128,2048]{2,1,0:T(8,128)(2,1)}, u32[]{:S(2)}, u32[]{:S(2)}) %all-to-all-start.1) | async-done | bytes 4194336 | tf_op jit(solution)/shard_map/all_to_all | solution.py:86
  195.0 3.4 convert_reduce_fusion
  198.4 0.1 convert_bitcast_fusion
  198.5 18.2 %reduce-scatter.2.cloned.1.call-done = bf16[128,2048]{1,0:T(8,128)(2,1)} async-done(((bf16[1024,2048]{1,0:T(8,128)(2,1)}), bf16[128,2048]{1,0:T(8,128)(2,1)}) %reduce-scatter.2.cloned.1.call-update) | async-done | bytes 524304 | tf_op jit(solution)/shard_map/reduce_scatter | solution.py:84
  216.7 2.2 pad_maximum_fusion.1
  218.9 0.0 all-gather.11.cloned.1.call-start
  219.0 1.5 fusion.54
  220.5 1.1 convert_element_type.133
  221.6 31.4 %all-gather.7.cloned.1.call-done = bf16[4,128,4096]{2,1,0:T(8,128)(2,1)} async-done(((bf16[1,128,4096]{2,1,0:T(8,128)(2,1)}), bf16[4,128,4096]{2,1,0:T(8,128)(2,1)}) %all-gather.7.cloned.1.call-update) | async-done | bytes 4194320 | tf_op jit(solution)/shard_map/all_gather | solution.py:49
  253.0 4.6 %fusion.44 = bf16[128,4096]{1,0:T(8,128)(2,1)S(1)} fusion(bf16[128,4096]{1,0:T(8,128)(2,1)S(1)} %copy-done, f32[128,2048]{1,0:T(8,128)S(1)} %convert_reduce_fusion, f32[128,2048]{1,0:T(8,128)S(1)} %convert_element_type.133, bf16[4,131,4096]{2,1,0:T(8,128)(2,1)} %all-gather.13.cloned.1.call-done, f32[4096]{0:T(1024)S(1)} %bitcast.115, f32[4096]{0:T(1024)S(1)} %bitcast.117, ...), kind=kLoop, calls=%fused_computation.41 | loop fusion | flops 19398656 | bytes 12648452 | tf_op jit(solution)/shard_map/convert_element_type | solution.py:92
  257.7 1.1 fusion.61
  258.8 0.0 all-gather.9.cloned.1.call-start
  258.9 5.2 %iota_compare_fusion.1 = pred[8,128,32,32]{2,3,1,0:T(32,128)(4,1)} fusion(s32[8,128,32]{2,1,0:T(8,128)} %bitcast.108), kind=kLoop, calls=%fused_computation.5 | loop fusion | flops 1048576 | bytes 1179648 | tf_op jit(solution)/shard_map/eq | solution.py:15
  264.1 4.6 fusion.60
  268.6 5.7 %iota_compare_fusion = pred[8,128,32,128]{3,2,1,0:T(32,128)(4,1)S(1)} fusion(s32[8,128,32]{2,1,0:T(8,128)S(1)} %bitcast.107), kind=kLoop, calls=%fused_computation.4 | loop fusion | flops 4194304 | bytes 4325376 | tf_op jit(solution)/shard_map/eq | solution.py:16
  274.3 4.3 fusion.59
  278.6 53.8 %all-gather.11.cloned.1.call-done = bf16[512,4096]{1,0:T(8,128)(2,1)} async-done(((bf16[64,4096]{1,0:T(8,128)(2,1)}), bf16[512,4096]{1,0:T(8,128)(2,1)}) %all-gather.11.cloned.1.call-update) | async-done | bytes 4194320 | tf_op jit(solution)/shard_map/all_gather | solution.py:98
  332.4 22.9 %fusion.20 = f32[512,32,128]{2,0,1:T(8,128)S(1)} fusion(bf16[32,128,4096]{2,1,0:T(8,128)(2,1)} %bitcast.124, bf16[512,4096]{1,0:T(8,128)(2,1)} %all-gather.11.cloned.1.call-done), kind=kOutput, calls=%fused_computation.24 | convolution fusion | flops 17179869184 | bytes 46137344 | tf_op jit(solution)/shard_map/dot_general | solution.py:99
  355.3 10.7 %select_reduce_fusion = f32[512,32]{1,0:T(8,128)S(1)} fusion(pred[8,64,32,32]{2,3,1,0:T(32,128)(4,1)} %get-tuple-element.7, pred[512,32,128]{2,1,0:T(32,128)(4,1)} %bitcast.105, f32[512,32,128]{2,0,1:T(8,128)S(1)} %fusion.20), kind=kOutput, calls=%fused_computation.16 | convolution fusion | flops 403685376 | bytes 11075584 | tf_op jit(solution)/shard_map/thl,tkl->tkh/dot_general | solution.py:106
  366.0 0.1 copy.30
  366.1 40.9 %all-gather.9.cloned.1.call-done = bf16[512,4096]{1,0:T(8,128)(2,1)} async-done(((bf16[64,4096]{1,0:T(8,128)(2,1)}), bf16[512,4096]{1,0:T(8,128)(2,1)}) %all-gather.9.cloned.1.call-update) | async-done | bytes 4194320 | tf_op jit(solution)/shard_map/all_gather | solution.py:98
  407.0 23.0 %fusion.22 = f32[512,32,128]{2,0,1:T(8,128)S(1)} fusion(bf16[32,128,4096]{2,1,0:T(8,128)(2,1)} %bitcast.125, bf16[512,4096]{1,0:T(8,128)(2,1)} %all-gather.9.cloned.1.call-done), kind=kOutput, calls=%fused_computation.26 | convolution fusion | flops 17179869184 | bytes 46137344 | tf_op jit(solution)/shard_map/dot_general | solution.py:99
  430.0 10.7 %select_reduce_fusion.1 = f32[512,32]{1,0:T(8,128)S(1)} fusion(pred[8,64,32,32]{2,3,1,0:T(32,128)(4,1)} %get-tuple-element.6, pred[512,32,128]{2,1,0:T(32,128)(4,1)} %bitcast.104, f32[512,32,128]{2,0,1:T(8,128)S(1)} %fusion.22), kind=kOutput, calls=%fused_computation.17 | convolution fusion | flops 403685376 | bytes 11075584 | tf_op jit(solution)/shard_map/thl,tkl->tkh/dot_general | solution.py:106
  440.7 0.8 copy.29
  441.5 1.7 pad_maximum_fusion.2
  443.1 3.4 all-to-all-start.2
  446.5 3.8 fusion.49
  450.3 3.4 all-to-all-done.2
  453.8 0.6 reduce_sum.39
  (30 shorter events, 0.2 us)
Async XLA Ops:
  10.1 16.2 %all-to-all-start = ((f32[8,128,64]{1,2,0:T(8,128)}), f32[8,128,64]{1,2,0:T(8,128)S(1)}, u32[]{:S(2)}, u32[]{:S(2)}) async-start(f32[8,128,64]{1,2,0:T(8,128)} %broadcast_in_dim.36), calls=%async_computation | async-start | bytes 524288 | tf_op jit(solution)/shard_map/all_to_all | solution.py:27
  17.4 199.2 %reduce-scatter.2.cloned.1.call-start = ((), (), s32[]{:S(2)}) async-start(), calls=%async_computation.4 | async-start | bytes 4718592 | tf_op jit(solution)/shard_map/reduce_scatter | solution.py:84
  26.8 10.1 %copy-start.1 = (s32[1024,32]{1,0:T(8,128)}, s32[1024,32]{1,0:T(8,128)S(1)}, u32[]{:S(2)}) copy-start(s32[1024,32]{1,0:T(8,128)S(1)} %copy.22) | copy-start | bytes 393220
  27.0 9.9 %copy-start.3 = (s32[1024,32]{1,0:T(8,128)}, s32[1024,32]{1,0:T(8,128)S(1)}, u32[]{:S(2)}) copy-start(s32[1024,32]{1,0:T(8,128)S(1)} %copy.20) | copy-start | bytes 393220
  36.9 3.3 copy-start.9
  86.0 4.8 %copy-start.8 = (f32[1,4096]{1,0:T(1,128)S(1)}, f32[1,4096]{1,0:T(1,128)}, u32[]{:S(2)}) copy-start(f32[1,4096]{1,0:T(1,128)} %param.9) | copy-start | bytes 49156
  86.0 4.8 %copy-start.4 = (bf16[1,128,4096]{2,1,0:T(8,128)(2,1)S(1)}, bf16[1,128,4096]{2,1,0:T(8,128)(2,1)}, u32[]{:S(2)}) copy-start(bf16[1,128,4096]{2,1,0:T(8,128)(2,1)} %param.11) | copy-start | bytes 3145732
  86.0 109.0 %all-to-all-start.1 = ((bf16[8,128,2048]{2,1,0:T(8,128)(2,1)}), bf16[8,128,2048]{2,1,0:T(8,128)(2,1)}, u32[]{:S(2)}, u32[]{:S(2)}) async-start(bf16[8,128,2048]{2,1,0:T(8,128)(2,1)} %bitcast.106), calls=%async_computation.2 | async-start | bytes 8388608 | tf_op jit(solution)/shard_map/all_to_all | solution.py:86
  90.7 128.2 %all-gather.13.cloned.1.call-start = ((), (), s32[]{:S(2)}) async-start(), calls=%async_computation.8 | async-start | bytes 5570560 | tf_op jit(solution)/shard_map/all_gather | solution.py:42
  92.0 161.0 %all-gather.7.cloned.1.call-start = ((), (), s32[]{:S(2)}) async-start(), calls=%async_computation.5 | async-start | bytes 5242880 | tf_op jit(solution)/shard_map/all_gather | solution.py:49
  216.7 36.4 %copy-start = (bf16[128,4096]{1,0:T(8,128)(2,1)S(1)}, bf16[128,4096]{1,0:T(8,128)(2,1)}, u32[]{:S(2)}) copy-start(bf16[128,4096]{1,0:T(8,128)(2,1)} %param.10) | copy-start | bytes 3145732
  218.9 113.5 %all-gather.11.cloned.1.call-start = ((), (), s32[]{:S(2)}) async-start(), calls=%async_computation.7 | async-start | bytes 4718592 | tf_op jit(solution)/shard_map/all_gather | solution.py:98
  220.4 37.2 %copy-start.5 = (f32[1,1,4096]{2,1,0:T(1,128)}, f32[1,1,4096]{2,1,0:T(1,128)S(1)}, u32[]{:S(2)}) copy-start(f32[1,1,4096]{2,1,0:T(1,128)S(1)} %get-tuple-element.11) | copy-start | bytes 49156
  220.5 37.2 %copy-start.6 = (f32[1,1,4096]{2,1,0:T(1,128)}, f32[1,1,4096]{2,1,0:T(1,128)S(1)}, u32[]{:S(2)}) copy-start(f32[1,1,4096]{2,1,0:T(1,128)S(1)} %get-tuple-element.12) | copy-start | bytes 49156
  220.5 37.2 %copy-start.7 = (f32[1,1,4096]{2,1,0:T(1,128)}, f32[1,1,4096]{2,1,0:T(1,128)S(1)}, u32[]{:S(2)}) copy-start(f32[1,1,4096]{2,1,0:T(1,128)S(1)} %get-tuple-element.13) | copy-start | bytes 49156
  258.8 148.2 %all-gather.9.cloned.1.call-start = ((), (), s32[]{:S(2)}) async-start(), calls=%async_computation.6 | async-start | bytes 4718592 | tf_op jit(solution)/shard_map/all_gather | solution.py:98
  264.0 4.6 copy-start.2
  443.1 10.7 %all-to-all-start.2 = ((f32[8,128,32]{1,2,0:T(8,128)}), f32[8,128,32]{1,2,0:T(8,128)S(1)}, u32[]{:S(2)}, u32[]{:S(2)}) async-start(f32[8,128,32]{1,2,0:T(8,128)} %pad_maximum_fusion.2), calls=%async_computation.3 | async-start | bytes 262144 | tf_op jit(solution)/shard_map/all_to_all | solution.py:116
Sparse Core Ops, SparseCore 0:
  62.2 154.4 reduce-scatter.1
  258.9 73.3 all-gather.10
  335.3 71.6 all-gather.8
Sparse Core Ops, SparseCore 1:
  92.8 37.1 all-gather.12
  219.0 34.0 all-gather.6

commit v9 on v7

--- a/solution.py
+++ b/solution.py
@@ -66,7 +66,7 @@
         "tkh,tkl->thl", coded_high, low_hot.astype(jnp.bfloat16), preferred_element_type=jnp.float32
     )
     spread = spread.astype(jnp.bfloat16).reshape(tokens, range_size)
-    half = weights.shape[1] // 2
+    half = weights.shape[1] // 4 if weights.shape[1] % (4 * LANES) == 0 else weights.shape[1] // 2
     w_first, w_second = weights[:, :half], weights[:, half:]
     partial_first = jnp.dot(spread, w_first, preferred_element_type=jnp.float32).astype(jnp.bfloat16)
     decoded_first = lax.psum_scatter(partial_first, "tok", scatter_dimension=0, tiled=True)
@@ -83,13 +83,12 @@
         segment, weights, (((1,), (1,)), ((), ())), preferred_element_type=jnp.float32
     )
     products = products.reshape(tokens, range_size // LANES, LANES)
+    products_high = products.astype(jnp.bfloat16)
+    products_low = (products - products_high.astype(jnp.float32)).astype(jnp.bfloat16)
+    low_pick = low_hot.astype(jnp.bfloat16)
     picked_low = jnp.einsum(
-        "thl,tkl->tkh",
-        products,
-        low_hot.astype(jnp.float32),
-        precision=lax.Precision.HIGH,
-        preferred_element_type=jnp.float32,
-    )
+        "thl,tkl->tkh", products_high, low_pick, preferred_element_type=jnp.float32
+    ) + jnp.einsum("thl,tkl->tkh", products_low, low_pick, preferred_element_type=jnp.float32)
     partial_grad = jnp.sum(jnp.where(high_hot, picked_low, 0.0), axis=-1)
     returned = lax.all_to_all(partial_grad, "tok", split_axis=0, concat_axis=0, tiled=True)
     code_grad = jnp.sum(returned.reshape(owners, -1, returned.shape[1]), axis=0)

time: 468 us -> 524 us (1.12)
  matrix products: 119 us -> 148 us
  waiting for transfers between devices: 287 us -> 316 us
    all_to_all x1, waiting for transfers between devices: 104 us -> 138 us  [on_device(): lax.all_to_all(partial_second, 'tok', split_axis=0, concat_axis=0, tiled=...]
    dot_general x1 -> x2, matrix products: 20.3 us -> 46.3 us  [the longest x1 25 us: on_device(): jnp.einsum('thl,tkl->tkh', products_high, low_pick, preferred_element_typ...]
    dot_general x1, matrix products: 24 us -> 36.2 us  [on_device(): jnp.dot(spread, w_second, preferred_element_type=jnp.float32)]
    dot_general x1, matrix products: 21.9 us -> 14.8 us  [on_device(): jnp.dot(spread, w_first, preferred_element_type=jnp.float32)]
  transfers between devices with their start and end apart: 7 -> 7, of which waited for: 6 -> 6; matrix products, arithmetic and copies ran while one was open for 7% -> 5% of each run, Pallas kernels for 0% -> 0%
where the time goes in v9:
time: 524 us; the launch traced here: 523 us
  waiting for transfers between devices  316 us (60%)
  matrix products  148 us (28%)
  other arithmetic  18.6 us (4%)
  starting transfers between devices  15.8 us (3%)
  between operations  15.7 us (3%)
  blocking collectives  5.47 us (1%)
    all_to_all x1, waiting for transfers between devices, on_device(): lax.all_to_all(partial_second, 'tok', split_axis=0, concat_axis=0, tiled=...  138 us
    all_gather x1, waiting for transfers between devices, on_device(): segment = lax.all_gather(grad_low, 'tok', axis=0, tiled=True)  125 us
    dot_general x1, matrix products, on_device(): lax.dot_general(segment, weights, (((1,), (1,)), ((), ())), preferred_ele...  41.4 us
    dot_general x1, matrix products, on_device(): jnp.dot(spread, w_second, preferred_element_type=jnp.float32)  36.2 us
    all_gather x1, waiting for transfers between devices, layer_chain(): lax.all_gather(decoded.astype(jnp.bfloat16), 'layer', axis=0, tiled=False)  26.8 us
    dot_general x1, matrix products, on_device(): jnp.einsum('thl,tkl->tkh', products_high, low_pick, preferred_element_typ...  25 us
    dot_general x1, matrix products, on_device(): jnp.einsum('thl,tkl->tkh', products_low, low_pick, preferred_element_type...  21.3 us
    dot_general x1, matrix products, on_device(): jnp.dot(spread, w_first, preferred_element_type=jnp.float32)  14.8 us
  transfers between devices with their start and end apart: 7, of which 6 were waited for; matrix products, arithmetic and copies ran while one was open for 5% of the time, Pallas kernels for 0%

profile of v9, /device:TPU:0, one launch (start us, length us, event | category | flops | bytes accessed | tf_op | source)
XLA Modules:
  0.0 522.9 jit_solution(16978194778072448333)
XLA Ops:
  8.0 0.7 bitcast_convert_fusion
  8.7 0.7 convert_bitcast_fusion.1
  9.4 0.7 broadcast_in_dim.35
  10.1 7.3 %all-to-all-start = ((f32[8,128,64]{1,2,0:T(8,128)}), f32[8,128,64]{1,2,0:T(8,128)S(1)}, u32[]{:S(2)}, u32[]{:S(2)}) async-start(f32[8,128,64]{1,2,0:T(8,128)} %broadcast_in_dim.35), calls=%async_computation | async-start | bytes 524288 | tf_op jit(solution)/shard_map/all_to_all | solution.py:27
  17.4 8.9 %all-to-all-done = f32[8,128,64]{1,2,0:T(8,128)S(1)} async-done(((f32[8,128,64]{1,2,0:T(8,128)}), f32[8,128,64]{1,2,0:T(8,128)S(1)}, u32[]{:S(2)}, u32[]{:S(2)}) %all-to-all-start) | async-done | bytes 262176 | tf_op jit(solution)/shard_map/all_to_all | solution.py:27
  26.4 0.1 fusion.48
  26.5 0.1 add_select_fusion
  26.6 0.2 copy.22
  26.8 0.2 copy.23
  27.0 0.0 copy-start.1
  27.0 0.2 copy.21
  27.2 9.7 %fusion.21 = bf16[1024,32,128]{2,1,0:T(8,128)(2,1)S(1)} fusion(s32[1024,32]{1,0:T(8,128)S(1)} %copy.23, s32[1024,32]{1,0:T(8,128)S(1)} %copy.21, bf16[1024,32]{1,0:T(8,128)(2,1)S(1)} %copy.22), kind=kOutput, calls=%fused_computation.25 | convolution fusion | flops 278921216 | bytes 8716288 | tf_op jit(solution)/shard_map/tkh,tkl->thl/dot_general | solution.py:65
  36.9 36.2 %fusion.24 = bf16[1024,3072]{1,0:T(8,128)(2,1)} fusion(bf16[4096,4096]{1,0:T(8,128)(2,1)} %bitcast.102, bf16[128,8,32,128]{3,2,1,0:T(8,128)(2,1)S(1)} %bitcast.105), kind=kOutput, calls=%fused_computation.26 | convolution fusion | flops 25772949504 | bytes 39845888 | tf_op jit(solution)/shard_map/dot_general | solution.py:73
  73.2 0.0 copy-done.6
  73.2 4.8 all-to-all-start.1
  78.0 0.2 reduce-scatter.2.cloned.1.call-start
  78.2 14.8 %fusion.42 = bf16[1024,1024]{1,0:T(8,128)(2,1)} fusion(bf16[4096,4096]{1,0:T(8,128)(2,1)} %bitcast.103, bf16[128,8,32,128]{3,2,1,0:T(8,128)(2,1)} %bitcast.106), kind=kOutput, calls=%fused_computation.49 | convolution fusion | flops 8590983168 | bytes 18874368 | tf_op jit(solution)/shard_map/dot_general | solution.py:71
  93.1 0.0 reduce-scatter.2.cloned.1.call-update
  93.1 0.0 all-gather.7.cloned.1.call-start
  93.1 0.5 all-gather.7.cloned.1.call-update
  93.7 0.0 all-gather.5.cloned.1.call-start
  93.7 137.8 %all-to-all-done.1 = bf16[8,128,3072]{2,1,0:T(8,128)(2,1)} async-done(((bf16[8,128,3072]{2,1,0:T(8,128)(2,1)}), bf16[8,128,3072]{2,1,0:T(8,128)(2,1)}, u32[]{:S(2)}, u32[]{:S(2)}) %all-to-all-start.1) | async-done | bytes 6291488 | tf_op jit(solution)/shard_map/all_to_all | solution.py:74
  231.5 4.0 convert_reduce_fusion
  235.5 0.0 copy-start.5
  235.6 0.0 copy-start
  235.6 0.1 convert_bitcast_fusion
  235.7 13.0 %reduce-scatter.2.cloned.1.call-done = bf16[128,1024]{1,0:T(8,128)(2,1)} async-done(((bf16[1024,1024]{1,0:T(8,128)(2,1)}), bf16[128,1024]{1,0:T(8,128)(2,1)}) %reduce-scatter.2.cloned.1.call-update) | async-done | bytes 262160 | tf_op jit(solution)/shard_map/reduce_scatter | solution.py:72
  248.7 2.0 pad_maximum_fusion.1
  250.7 0.0 all-gather.5.cloned.1.call-update
  250.7 0.0 all-gather.9.cloned.1.call-start
  250.8 0.0 copy-done.5
  250.8 5.5 %all-gather = f32[4,1,4096]{2,1,0:T(1,128)S(1)} all-gather(f32[1,1,4096]{2,1,0:T(1,128)S(1)} %bitcast.100), channel_id=1, replica_groups=mesh['layer'=4,'tok'=8] {'layer'}, dimensions={0}, use_global_device_ids=true | all-gather | bytes 81920 | tf_op jit(solution)/shard_map/all_gather | solution.py:35
  256.2 1.0 convert_element_type.114
  257.3 0.0 all-gather.7.cloned.1.call-done
  257.3 26.8 %all-gather.5.cloned.1.call-done = bf16[4,128,4096]{2,1,0:T(8,128)(2,1)} async-done(((bf16[1,128,4096]{2,1,0:T(8,128)(2,1)}), bf16[4,128,4096]{2,1,0:T(8,128)(2,1)}) %all-gather.5.cloned.1.call-update) | async-done | bytes 4194320 | tf_op jit(solution)/shard_map/all_gather | solution.py:37
  284.1 5.4 %fusion.37 = bf16[128,4096]{1,0:T(8,128)(2,1)} fusion(bf16[128,4096]{1,0:T(8,128)(2,1)S(1)} %copy-done, f32[128,3072]{1,0:T(8,128)S(1)} %convert_reduce_fusion, f32[128,1024]{1,0:T(8,128)S(1)} %convert_element_type.114, bf16[4,128,4096]{2,1,0:T(8,128)(2,1)} %all-gather.7.cloned.1.call-done, f32[4096]{0:T(1024)S(1)} %bitcast.98, f32[4096]{0:T(1024)S(1)} %bitcast.94, ...), kind=kLoop, calls=%fused_computation.38 | loop fusion | flops 19398656 | bytes 12648452 | tf_op jit(solution)/shard_map/convert_element_type | solution.py:80
  289.5 0.0 all-gather.9.cloned.1.call-update
  289.5 125.1 %all-gather.9.cloned.1.call-done = bf16[1024,4096]{1,0:T(8,128)(2,1)} async-done(((bf16[128,4096]{1,0:T(8,128)(2,1)}), bf16[1024,4096]{1,0:T(8,128)(2,1)}) %all-gather.9.cloned.1.call-update) | async-done | bytes 8388624 | tf_op jit(solution)/shard_map/all_gather | solution.py:81
  414.6 41.4 %subtract_convert_fusion = (bf16[1024,32,128]{2,0,1:T(8,128)(2,1)S(1)}, bf16[1024,32,128]{2,0,1:T(8,128)(2,1)S(1)}) fusion(bf16[32,128,4096]{2,1,0:T(8,128)(2,1)} %bitcast.104, bf16[1024,4096]{1,0:T(8,128)(2,1)} %all-gather.9.cloned.1.call-done), kind=kOutput, calls=%fused_computation.3 | convolution fusion | flops 34376515584 | bytes 58720256 | tf_op jit(solution)/shard_map/dot_general | solution.py:82
  456.1 0.0 copy-done.2
  456.1 0.0 copy-start.4
  456.1 21.3 %fusion.2 = f32[1024,32,32]{1,2,0:T(8,128)S(1)} fusion(bf16[1024,32,128]{2,0,1:T(8,128)(2,1)S(1)} %get-tuple-element.2, s32[1024,32]{1,0:T(8,128)S(1)} %copy-done.2), kind=kOutput, calls=%fused_computation.5 | convolution fusion | flops 272629760 | bytes 12713984 | tf_op jit(solution)/shard_map/thl,tkl->tkh/dot_general | solution.py:91
  477.4 25.0 %select_reduce_fusion = f32[1024,32]{1,0:T(8,128)} fusion(f32[1024,32,32]{1,2,0:T(8,128)S(1)} %fusion.2, s32[1024,32]{1,0:T(8,128)S(1)} %copy-done.4, bf16[1024,32,128]{2,0,1:T(8,128)(2,1)S(1)} %get-tuple-element.3, s32[1024,32]{1,0:T(8,128)S(1)} %copy-done.2), kind=kOutput, calls=%fused_computation.2 | convolution fusion | flops 276791296 | bytes 12976128 | tf_op jit(solution)/shard_map/thl,tkl->tkh/dot_general | solution.py:89
  502.4 1.9 copy.27
  504.2 3.4 all-to-all-start.2
  507.6 3.8 fusion.47
  511.4 3.5 all-to-all-done.2
  514.9 0.6 reduce_sum.29
  (11 shorter events, 0.1 us)
Async XLA Ops:
  10.1 16.2 %all-to-all-start = ((f32[8,128,64]{1,2,0:T(8,128)}), f32[8,128,64]{1,2,0:T(8,128)S(1)}, u32[]{:S(2)}, u32[]{:S(2)}) async-start(f32[8,128,64]{1,2,0:T(8,128)} %broadcast_in_dim.35), calls=%async_computation | async-start | bytes 524288 | tf_op jit(solution)/shard_map/all_to_all | solution.py:27
  27.0 9.9 %copy-start.1 = (s32[1024,32]{1,0:T(8,128)}, s32[1024,32]{1,0:T(8,128)S(1)}, u32[]{:S(2)}) copy-start(s32[1024,32]{1,0:T(8,128)S(1)} %copy.23) | copy-start | bytes 393220
  27.2 9.7 %copy-start.3 = (s32[1024,32]{1,0:T(8,128)}, s32[1024,32]{1,0:T(8,128)S(1)}, u32[]{:S(2)}) copy-start(s32[1024,32]{1,0:T(8,128)S(1)} %copy.21) | copy-start | bytes 393220
  36.9 36.3 %copy-start.6 = (bf16[1024,32,128]{2,1,0:T(8,128)(2,1)}, bf16[1024,32,128]{2,1,0:T(8,128)(2,1)S(1)}, u32[]{:S(2)}) copy-start(bf16[1024,32,128]{2,1,0:T(8,128)(2,1)S(1)} %fusion.21) | copy-start | bytes 25165828
  73.2 158.3 %all-to-all-start.1 = ((bf16[8,128,3072]{2,1,0:T(8,128)(2,1)}), bf16[8,128,3072]{2,1,0:T(8,128)(2,1)}, u32[]{:S(2)}, u32[]{:S(2)}) async-start(bf16[8,128,3072]{2,1,0:T(8,128)(2,1)} %bitcast.89), calls=%async_computation.2 | async-start | bytes 12582912 | tf_op jit(solution)/shard_map/all_to_all | solution.py:74
  78.0 170.7 %reduce-scatter.2.cloned.1.call-start = ((), (), s32[]{:S(2)}) async-start(), calls=%async_computation.4 | async-start | bytes 2359296 | tf_op jit(solution)/shard_map/reduce_scatter | solution.py:72
  93.1 164.2 %all-gather.7.cloned.1.call-start = ((), (), s32[]{:S(2)}) async-start(), calls=%async_computation.6 | async-start | bytes 5242880 | tf_op jit(solution)/shard_map/all_gather | solution.py:36
  93.7 190.5 %all-gather.5.cloned.1.call-start = ((), (), s32[]{:S(2)}) async-start(), calls=%async_computation.5 | async-start | bytes 5242880 | tf_op jit(solution)/shard_map/all_gather | solution.py:37
  235.5 15.2 %copy-start.5 = (f32[1,4096]{1,0:T(1,128)S(1)}, f32[1,4096]{1,0:T(1,128)}, u32[]{:S(2)}) copy-start(f32[1,4096]{1,0:T(1,128)} %param.9) | copy-start | bytes 49156
  235.6 48.6 %copy-start = (bf16[128,4096]{1,0:T(8,128)(2,1)S(1)}, bf16[128,4096]{1,0:T(8,128)(2,1)}, u32[]{:S(2)}) copy-start(bf16[128,4096]{1,0:T(8,128)(2,1)} %param.10) | copy-start | bytes 3145732
  250.7 163.9 %all-gather.9.cloned.1.call-start = ((), (), s32[]{:S(2)}) async-start(), calls=%async_computation.7 | async-start | bytes 9437184 | tf_op jit(solution)/shard_map/all_gather | solution.py:81
  414.6 41.4 %copy-start.2 = (s32[1024,32]{1,0:T(8,128)S(1)}, s32[1024,32]{1,0:T(8,128)}, u32[]{:S(2)}) copy-start(s32[1024,32]{1,0:T(8,128)} %copy-done.1) | copy-start | bytes 393220
  456.1 21.3 %copy-start.4 = (s32[1024,32]{1,0:T(8,128)S(1)}, s32[1024,32]{1,0:T(8,128)}, u32[]{:S(2)}) copy-start(s32[1024,32]{1,0:T(8,128)} %copy-done.3) | copy-start | bytes 393220
  504.2 10.7 %all-to-all-start.2 = ((f32[8,128,32]{1,2,0:T(8,128)}), f32[8,128,32]{1,2,0:T(8,128)S(1)}, u32[]{:S(2)}, u32[]{:S(2)}) async-start(f32[8,128,32]{1,2,0:T(8,128)} %copy.27), calls=%async_computation.3 | async-start | bytes 262144 | tf_op jit(solution)/shard_map/all_to_all | solution.py:93
Sparse Core Ops, SparseCore 0:
  93.2 155.4 reduce-scatter.1
  289.7 124.9 all-gather.8
Sparse Core Ops, SparseCore 1:
  95.1 35.4 all-gather.6
  250.8 33.3 all-gather.4

commit v10 on v7

--- a/solution.py
+++ b/solution.py
@@ -81,13 +81,12 @@
     segment = lax.all_gather(grad_low, "tok", axis=0, tiled=True)
     products = lax.dot_general(
         segment, weights, (((1,), (1,)), ((), ())), preferred_element_type=jnp.float32
-    )
+    ).astype(jnp.bfloat16)
     products = products.reshape(tokens, range_size // LANES, LANES)
     picked_low = jnp.einsum(
         "thl,tkl->tkh",
         products,
-        low_hot.astype(jnp.float32),
-        precision=lax.Precision.HIGH,
+        low_hot.astype(jnp.bfloat16),
         preferred_element_type=jnp.float32,
     )
     partial_grad = jnp.sum(jnp.where(high_hot, picked_low, 0.0), axis=-1)

time: 468 us -> 468 us (level)
  matrix products: 119 us -> 109 us
  local copies, waits for them, and re-layouts: 6.42 us -> 16.2 us
    unnamed x10 -> x15, local copies, waits for them, and re-layouts: 3.24 us -> 13 us
    dot_general x1, matrix products: 20.3 us -> 10.7 us  [on_device(): jnp.einsum('thl,tkl->tkh', products, low_hot.astype(jnp.bfloat16), prefer...]
where the time goes in v10:
time: 468 us; the launch traced here: 467 us
  waiting for transfers between devices  287 us (61%)
  matrix products  109 us (23%)
  other arithmetic  18.2 us (4%)
  local copies, waits for them, and re-layouts  16.2 us (3%)
  between operations  15.7 us (3%)
  starting transfers between devices  15.4 us (3%)
  blocking collectives  5.43 us (1%)
    all_gather x1, waiting for transfers between devices, on_device(): segment = lax.all_gather(grad_low, 'tok', axis=0, tiled=True)  125 us
    all_to_all x1, waiting for transfers between devices, on_device(): lax.all_to_all(partial_second, 'tok', split_axis=0, concat_axis=0, tiled=...  104 us
    dot_general x1, matrix products, on_device(): lax.dot_general(segment, weights, (((1,), (1,)), ((), ())), preferred_ele...  42.5 us
    all_gather x1, waiting for transfers between devices, layer_chain(): lax.all_gather(decoded.astype(jnp.bfloat16), 'layer', axis=0, tiled=False)  27.5 us
    dot_general x1, matrix products, on_device(): jnp.dot(spread, w_second, preferred_element_type=jnp.float32)  24 us
    dot_general x1, matrix products, on_device(): jnp.dot(spread, w_first, preferred_element_type=jnp.float32)  21.9 us
    reduce_scatter x1, waiting for transfers between devices, on_device(): lax.psum_scatter(partial_first, 'tok', scatter_dimension=0, tiled=True)  18.2 us
    unnamed x15, local copies, waits for them, and re-layouts  13 us
  transfers between devices with their start and end apart: 7, of which 6 were waited for; matrix products, arithmetic and copies ran while one was open for 7% of the time, Pallas kernels for 0%

profile of v10, /device:TPU:0, one launch (start us, length us, event | category | flops | bytes accessed | tf_op | source)
XLA Modules:
  0.0 467.1 jit_solution(5513722853799496714)
XLA Ops:
  8.0 0.7 bitcast_convert_fusion
  8.7 0.7 convert_bitcast_fusion.2
  9.4 0.7 broadcast_in_dim.35
  10.1 7.3 %all-to-all-start = ((f32[8,128,64]{1,2,0:T(8,128)}), f32[8,128,64]{1,2,0:T(8,128)S(1)}, u32[]{:S(2)}, u32[]{:S(2)}) async-start(f32[8,128,64]{1,2,0:T(8,128)} %broadcast_in_dim.35), calls=%async_computation | async-start | bytes 524288 | tf_op jit(solution)/shard_map/all_to_all | solution.py:27
  17.4 0.0 reduce-scatter.2.cloned.1.call-start
  17.5 8.9 %all-to-all-done = f32[8,128,64]{1,2,0:T(8,128)S(1)} async-done(((f32[8,128,64]{1,2,0:T(8,128)}), f32[8,128,64]{1,2,0:T(8,128)S(1)}, u32[]{:S(2)}, u32[]{:S(2)}) %all-to-all-start) | async-done | bytes 262176 | tf_op jit(solution)/shard_map/all_to_all | solution.py:27
  26.4 0.1 fusion.40
  26.5 0.1 add_select_fusion
  26.6 0.2 copy.17
  26.8 0.0 copy-start.1
  26.8 0.2 copy.15
  27.0 0.0 copy-start.3
  27.0 0.2 copy.16
  27.2 9.7 %fusion.15 = bf16[1024,32,128]{2,1,0:T(8,128)(2,1)S(1)} fusion(s32[1024,32]{1,0:T(8,128)S(1)} %copy.17, s32[1024,32]{1,0:T(8,128)S(1)} %copy.15, bf16[1024,32]{1,0:T(8,128)(2,1)S(1)} %copy.16), kind=kOutput, calls=%fused_computation.19 | convolution fusion | flops 278921216 | bytes 8716288 | tf_op jit(solution)/shard_map/tkh,tkl->thl/dot_general | solution.py:65
  36.9 0.0 copy-done.1
  36.9 0.0 copy-done.3
  36.9 3.3 copy-done.6
  40.2 21.9 %fusion.20 = bf16[1024,2048]{1,0:T(8,128)(2,1)} fusion(bf16[4096,4096]{1,0:T(8,128)(2,1)} %bitcast.103, bf16[128,8,32,128]{3,2,1,0:T(8,128)(2,1)S(1)} %bitcast.105), kind=kOutput, calls=%fused_computation.22 | convolution fusion | flops 17181966336 | bytes 29360128 | tf_op jit(solution)/shard_map/dot_general | solution.py:71
  62.1 0.0 reduce-scatter.2.cloned.1.call-update
  62.1 24.0 %fusion.25 = bf16[1024,2048]{1,0:T(8,128)(2,1)} fusion(bf16[4096,4096]{1,0:T(8,128)(2,1)} %bitcast.104, bf16[128,8,32,128]{3,2,1,0:T(8,128)(2,1)} %bitcast.106), kind=kOutput, calls=%fused_computation.23 | convolution fusion | flops 17181966336 | bytes 29360128 | tf_op jit(solution)/shard_map/dot_general | solution.py:73
  86.2 4.6 all-to-all-start.1
  90.7 0.0 all-gather.7.cloned.1.call-start
  90.8 0.5 all-gather.7.cloned.1.call-update
  91.3 0.0 all-gather.5.cloned.1.call-start
  91.4 103.7 %all-to-all-done.1 = bf16[8,128,2048]{2,1,0:T(8,128)(2,1)} async-done(((bf16[8,128,2048]{2,1,0:T(8,128)(2,1)}), bf16[8,128,2048]{2,1,0:T(8,128)(2,1)}, u32[]{:S(2)}, u32[]{:S(2)}) %all-to-all-start.1) | async-done | bytes 4194336 | tf_op jit(solution)/shard_map/all_to_all | solution.py:74
  195.0 3.4 convert_reduce_fusion
  198.4 0.0 copy-start.5
  198.4 0.1 convert_bitcast_fusion.1
  198.5 18.2 %reduce-scatter.2.cloned.1.call-done = bf16[128,2048]{1,0:T(8,128)(2,1)} async-done(((bf16[1024,2048]{1,0:T(8,128)(2,1)}), bf16[128,2048]{1,0:T(8,128)(2,1)}) %reduce-scatter.2.cloned.1.call-update) | async-done | bytes 524304 | tf_op jit(solution)/shard_map/reduce_scatter | solution.py:72
  216.7 2.2 pad_maximum_fusion.1
  218.9 0.0 all-gather.5.cloned.1.call-update
  218.9 0.0 all-gather.9.cloned.1.call-start
  219.0 5.4 %all-gather = f32[4,1,4096]{2,1,0:T(1,128)S(1)} all-gather(f32[1,1,4096]{2,1,0:T(1,128)S(1)} %bitcast.101), channel_id=1, replica_groups=mesh['layer'=4,'tok'=8] {'layer'}, dimensions={0}, use_global_device_ids=true | all-gather | bytes 81920 | tf_op jit(solution)/shard_map/all_gather | solution.py:35
  224.4 1.2 convert_element_type.108
  225.6 0.0 all-gather.7.cloned.1.call-done
  225.6 27.5 %all-gather.5.cloned.1.call-done = bf16[4,128,4096]{2,1,0:T(8,128)(2,1)} async-done(((bf16[1,128,4096]{2,1,0:T(8,128)(2,1)}), bf16[4,128,4096]{2,1,0:T(8,128)(2,1)}) %all-gather.5.cloned.1.call-update) | async-done | bytes 4194320 | tf_op jit(solution)/shard_map/all_gather | solution.py:37
  253.1 5.4 %fusion.34 = bf16[128,4096]{1,0:T(8,128)(2,1)} fusion(bf16[128,4096]{1,0:T(8,128)(2,1)S(1)} %copy-done, f32[128,2048]{1,0:T(8,128)S(1)} %convert_reduce_fusion, f32[128,2048]{1,0:T(8,128)S(1)} %convert_element_type.108, bf16[4,128,4096]{2,1,0:T(8,128)(2,1)} %all-gather.7.cloned.1.call-done, f32[4096]{0:T(1024)S(1)} %bitcast.99, f32[4096]{0:T(1024)S(1)} %bitcast.95, ...), kind=kLoop, calls=%fused_computation.33 | loop fusion | flops 19398656 | bytes 12648452 | tf_op jit(solution)/shard_map/convert_element_type | solution.py:80
  258.5 0.0 all-gather.9.cloned.1.call-update
  258.5 125.1 %all-gather.9.cloned.1.call-done = bf16[1024,4096]{1,0:T(8,128)(2,1)} async-done(((bf16[128,4096]{1,0:T(8,128)(2,1)}), bf16[1024,4096]{1,0:T(8,128)(2,1)}) %all-gather.9.cloned.1.call-update) | async-done | bytes 8388624 | tf_op jit(solution)/shard_map/all_gather | solution.py:81
  383.6 42.5 %convert_bitcast_fusion = bf16[128,8,32,128]{3,1,2,0:T(8,128)(2,1)} fusion(bf16[1024,4096]{1,0:T(8,128)(2,1)} %all-gather.9.cloned.1.call-done, bf16[1,4096,4096]{2,1,0:T(8,128)(2,1)} %param.8), kind=kOutput, calls=%fused_computation.12 | convolution fusion | flops 34363932672 | bytes 50331648 | tf_op jit(solution)/shard_map/dot_general | solution.py:82
  426.1 9.7 %copy.24 = bf16[128,8,32,128]{3,2,1,0:T(8,128)(2,1)} copy(bf16[128,8,32,128]{3,1,2,0:T(8,128)(2,1)} %convert_bitcast_fusion) | data formatting | bytes 16777216
  435.8 0.0 copy-done.4
  435.8 10.7 %select_reduce_fusion = f32[1024,32]{1,0:T(8,128)} fusion(s32[1024,32]{1,0:T(8,128)S(1)} %copy-done.4, bf16[1024,32,128]{2,1,0:T(8,128)(2,1)} %bitcast.89, s32[1024,32]{1,0:T(8,128)S(1)} %copy-done.2), kind=kOutput, calls=%fused_computation.4 | convolution fusion | flops 275742720 | bytes 8781824 | tf_op jit(solution)/shard_map/thl,tkl->tkh/dot_general | solution.py:86
  446.5 1.9 copy.19
  448.4 3.4 all-to-all-start.2
  451.8 3.8 fusion.39
  455.6 3.5 all-to-all-done.2
  459.1 0.6 reduce_sum.29
  (11 shorter events, 0.1 us)
Async XLA Ops:
  10.1 16.2 %all-to-all-start = ((f32[8,128,64]{1,2,0:T(8,128)}), f32[8,128,64]{1,2,0:T(8,128)S(1)}, u32[]{:S(2)}, u32[]{:S(2)}) async-start(f32[8,128,64]{1,2,0:T(8,128)} %broadcast_in_dim.35), calls=%async_computation | async-start | bytes 524288 | tf_op jit(solution)/shard_map/all_to_all | solution.py:27
  17.4 199.2 %reduce-scatter.2.cloned.1.call-start = ((), (), s32[]{:S(2)}) async-start(), calls=%async_computation.4 | async-start | bytes 4718592 | tf_op jit(solution)/shard_map/reduce_scatter | solution.py:72
  26.8 10.1 %copy-start.1 = (s32[1024,32]{1,0:T(8,128)}, s32[1024,32]{1,0:T(8,128)S(1)}, u32[]{:S(2)}) copy-start(s32[1024,32]{1,0:T(8,128)S(1)} %copy.17) | copy-start | bytes 393220
  27.0 9.9 %copy-start.3 = (s32[1024,32]{1,0:T(8,128)}, s32[1024,32]{1,0:T(8,128)S(1)}, u32[]{:S(2)}) copy-start(s32[1024,32]{1,0:T(8,128)S(1)} %copy.15) | copy-start | bytes 393220
  36.9 3.3 copy-start.6
  86.2 108.9 %all-to-all-start.1 = ((bf16[8,128,2048]{2,1,0:T(8,128)(2,1)}), bf16[8,128,2048]{2,1,0:T(8,128)(2,1)}, u32[]{:S(2)}, u32[]{:S(2)}) async-start(bf16[8,128,2048]{2,1,0:T(8,128)(2,1)} %bitcast.90), calls=%async_computation.2 | async-start | bytes 8388608 | tf_op jit(solution)/shard_map/all_to_all | solution.py:74
  90.7 134.9 %all-gather.7.cloned.1.call-start = ((), (), s32[]{:S(2)}) async-start(), calls=%async_computation.6 | async-start | bytes 5242880 | tf_op jit(solution)/shard_map/all_gather | solution.py:36
  91.3 161.8 %all-gather.5.cloned.1.call-start = ((), (), s32[]{:S(2)}) async-start(), calls=%async_computation.5 | async-start | bytes 5242880 | tf_op jit(solution)/shard_map/all_gather | solution.py:37
  198.4 20.5 %copy-start.5 = (f32[1,4096]{1,0:T(1,128)S(1)}, f32[1,4096]{1,0:T(1,128)}, u32[]{:S(2)}) copy-start(f32[1,4096]{1,0:T(1,128)} %param.9) | copy-start | bytes 49156
  216.7 36.4 %copy-start = (bf16[128,4096]{1,0:T(8,128)(2,1)S(1)}, bf16[128,4096]{1,0:T(8,128)(2,1)}, u32[]{:S(2)}) copy-start(bf16[128,4096]{1,0:T(8,128)(2,1)} %param.10) | copy-start | bytes 3145732
  218.9 164.7 %all-gather.9.cloned.1.call-start = ((), (), s32[]{:S(2)}) async-start(), calls=%async_computation.7 | async-start | bytes 9437184 | tf_op jit(solution)/shard_map/all_gather | solution.py:81
  426.1 9.7 %copy-start.2 = (s32[1024,32]{1,0:T(8,128)S(1)}, s32[1024,32]{1,0:T(8,128)}, u32[]{:S(2)}) copy-start(s32[1024,32]{1,0:T(8,128)} %copy-done.1) | copy-start | bytes 393220
  426.1 9.7 %copy-start.4 = (s32[1024,32]{1,0:T(8,128)S(1)}, s32[1024,32]{1,0:T(8,128)}, u32[]{:S(2)}) copy-start(s32[1024,32]{1,0:T(8,128)} %copy-done.3) | copy-start | bytes 393220
  448.4 10.7 %all-to-all-start.2 = ((f32[8,128,32]{1,2,0:T(8,128)}), f32[8,128,32]{1,2,0:T(8,128)S(1)}, u32[]{:S(2)}, u32[]{:S(2)}) async-start(f32[8,128,32]{1,2,0:T(8,128)} %copy.19), calls=%async_computation.3 | async-start | bytes 262144 | tf_op jit(solution)/shard_map/all_to_all | solution.py:93
Sparse Core Ops, SparseCore 0:
  62.3 154.3 reduce-scatter.1
  258.6 124.9 all-gather.8
Sparse Core Ops, SparseCore 1:
  92.8 35.6 all-gather.6
  219.0 34.1 all-gather.4

commit v11 on v10

--- a/solution.py
+++ b/solution.py
@@ -66,10 +66,12 @@
         "tkh,tkl->thl", coded_high, low_hot.astype(jnp.bfloat16), preferred_element_type=jnp.float32
     )
     spread = spread.astype(jnp.bfloat16).reshape(tokens, range_size)
-    half = weights.shape[1] // 2
+    width = weights.shape[1]
+    half = (5 * width // 8) // LANES * LANES if width % (8 * LANES) == 0 else width // 2
     w_first, w_second = weights[:, :half], weights[:, half:]
     partial_first = jnp.dot(spread, w_first, preferred_element_type=jnp.float32).astype(jnp.bfloat16)
     decoded_first = lax.psum_scatter(partial_first, "tok", scatter_dimension=0, tiled=True)
+    partial_first, spread = lax.optimization_barrier((partial_first, spread))
     partial_second = jnp.dot(spread, w_second, preferred_element_type=jnp.float32).astype(jnp.bfloat16)
     received = lax.all_to_all(partial_second, "tok", split_axis=0, concat_axis=0, tiled=True)
     decoded_second = jnp.sum(

time: 468 us -> 469 us (level)
  local copies, waits for them, and re-layouts: 16.2 us -> 31.9 us
  waiting for transfers between devices: 287 us -> 276 us
    all_to_all x1, waiting for transfers between devices: 104 us -> 79.8 us  [on_device(): lax.all_to_all(partial_second, 'tok', split_axis=0, concat_axis=0, tiled=...]
    unnamed x15 -> x20, local copies, waits for them, and re-layouts: 13 us -> 28.8 us
    reduce_scatter x1, waiting for transfers between devices: 18.2 us -> 31 us  [on_device(): lax.psum_scatter(partial_first, 'tok', scatter_dimension=0, tiled=True)]
    dot_general x1, matrix products: 21.9 us -> 26.6 us  [on_device(): jnp.dot(spread, w_first, preferred_element_type=jnp.float32)]
    dot_general x1, matrix products: 24 us -> 19.3 us  [on_device(): jnp.dot(spread, w_second, preferred_element_type=jnp.float32)]
  transfers between devices with their start and end apart: 7 -> 7, of which waited for: 6 -> 6; matrix products, arithmetic and copies ran while one was open for 7% -> 9% of each run, Pallas kernels for 0% -> 0%
where the time goes in v11:
time: 469 us; the launch traced here: 468 us
  waiting for transfers between devices  276 us (59%)
  matrix products  109 us (23%)
  local copies, waits for them, and re-layouts  31.9 us (7%)
  between operations  15.7 us (3%)
  other arithmetic  15.3 us (3%)
  starting transfers between devices  14.7 us (3%)
  blocking collectives  5.38 us (1%)
    all_gather x1, waiting for transfers between devices, on_device(): segment = lax.all_gather(grad_low, 'tok', axis=0, tiled=True)  125 us
    all_to_all x1, waiting for transfers between devices, on_device(): lax.all_to_all(partial_second, 'tok', split_axis=0, concat_axis=0, tiled=...  79.8 us
    dot_general x1, matrix products, on_device(): lax.dot_general(segment, weights, (((1,), (1,)), ((), ())), preferred_ele...  42.6 us
    reduce_scatter x1, waiting for transfers between devices, on_device(): lax.psum_scatter(partial_first, 'tok', scatter_dimension=0, tiled=True)  31 us
    unnamed x20, local copies, waits for them, and re-layouts  28.8 us
    all_gather x1, waiting for transfers between devices, layer_chain(): lax.all_gather(decoded.astype(jnp.bfloat16), 'layer', axis=0, tiled=False)  27.4 us
    dot_general x1, matrix products, on_device(): jnp.dot(spread, w_first, preferred_element_type=jnp.float32)  26.6 us
    dot_general x1, matrix products, on_device(): jnp.dot(spread, w_second, preferred_element_type=jnp.float32)  19.3 us
  transfers between devices with their start and end apart: 7, of which 6 were waited for; matrix products, arithmetic and copies ran while one was open for 9% of the time, Pallas kernels for 0%

profile of v11, /device:TPU:0, one launch (start us, length us, event | category | flops | bytes accessed | tf_op | source)
XLA Modules:
  0.0 468.2 jit_solution(10644898478574253596)
XLA Ops:
  8.0 0.7 bitcast_convert_fusion
  8.7 0.7 convert_bitcast_fusion.2
  9.4 0.7 broadcast_in_dim.35
  10.1 7.3 %all-to-all-start = ((f32[8,128,64]{1,2,0:T(8,128)}), f32[8,128,64]{1,2,0:T(8,128)S(1)}, u32[]{:S(2)}, u32[]{:S(2)}) async-start(f32[8,128,64]{1,2,0:T(8,128)} %broadcast_in_dim.35), calls=%async_computation | async-start | bytes 524288 | tf_op jit(solution)/shard_map/all_to_all | solution.py:27
  17.4 0.0 reduce-scatter.2.cloned.1.call-start
  17.5 8.9 %all-to-all-done = f32[8,128,64]{1,2,0:T(8,128)S(1)} async-done(((f32[8,128,64]{1,2,0:T(8,128)}), f32[8,128,64]{1,2,0:T(8,128)S(1)}, u32[]{:S(2)}, u32[]{:S(2)}) %all-to-all-start) | async-done | bytes 262176 | tf_op jit(solution)/shard_map/all_to_all | solution.py:27
  26.4 0.1 fusion.32
  26.5 0.1 add_select_fusion
  26.6 0.2 copy.17
  26.8 0.0 copy-start.4
  26.8 0.2 copy.15
  27.0 0.0 copy-start.6
  27.0 0.2 copy.16
  27.2 9.7 %fusion.11 = bf16[1024,32,128]{2,1,0:T(8,128)(2,1)S(1)} fusion(s32[1024,32]{1,0:T(8,128)S(1)} %copy.17, s32[1024,32]{1,0:T(8,128)S(1)} %copy.15, bf16[1024,32]{1,0:T(8,128)(2,1)S(1)} %copy.16), kind=kOutput, calls=%fused_computation.15 | convolution fusion | flops 278921216 | bytes 8716288 | tf_op jit(solution)/shard_map/tkh,tkl->thl/dot_general | solution.py:65
  36.9 0.0 copy-done.4
  36.9 0.0 copy-done.6
  36.9 3.2 copy-done.2
  40.1 26.6 %fusion.14 = bf16[1024,2560]{1,0:T(8,128)(2,1)} fusion(bf16[4096,4096]{1,0:T(8,128)(2,1)} %bitcast.102, bf16[128,8,32,128]{3,2,1,0:T(8,128)(2,1)S(1)} %bitcast.85), kind=kOutput, calls=%fused_computation.17 | convolution fusion | flops 21477457920 | bytes 34603008 | tf_op jit(solution)/shard_map/dot_general | solution.py:72
  66.7 0.0 reduce-scatter.2.cloned.1.call-update
  66.8 15.1 %copy.28 = bf16[128,8,32,128]{3,1,2,0:T(8,128)(2,1)} copy(bf16[128,8,32,128]{3,2,1,0:T(8,128)(2,1)} %bitcast.86) | data formatting | bytes 16777216
  81.9 19.3 %fusion.19 = bf16[1024,1536]{1,0:T(8,128)(2,1)} fusion(bf16[1024,4096]{1,0:T(8,128)(2,1)} %bitcast.88, bf16[4096,4096]{1,0:T(8,128)(2,1)} %bitcast.103), kind=kOutput, calls=%fused_computation.20 | convolution fusion | flops 12886474752 | bytes 24117248 | tf_op jit(solution)/shard_map/dot_general | solution.py:75
  101.2 3.6 all-to-all-start.1
  104.8 0.0 all-gather.7.cloned.1.call-start
  104.9 0.5 all-gather.7.cloned.1.call-update
  105.4 0.3 all-gather.5.cloned.1.call-start
  105.7 79.8 %all-to-all-done.1 = bf16[8,128,1536]{2,1,0:T(8,128)(2,1)S(1)} async-done(((bf16[8,128,1536]{2,1,0:T(8,128)(2,1)}), bf16[8,128,1536]{2,1,0:T(8,128)(2,1)S(1)}, u32[]{:S(2)}, u32[]{:S(2)}) %all-to-all-start.1) | async-done | bytes 3145760 | tf_op jit(solution)/shard_map/all_to_all | solution.py:76
  185.5 0.4 convert_reduce_fusion
  185.9 0.9 copy-done
  186.9 31.0 %reduce-scatter.2.cloned.1.call-done = bf16[128,2560]{1,0:T(8,128)(2,1)} async-done(((bf16[1024,2560]{1,0:T(8,128)(2,1)}), bf16[128,2560]{1,0:T(8,128)(2,1)}) %reduce-scatter.2.cloned.1.call-update) | async-done | bytes 655376 | tf_op jit(solution)/shard_map/reduce_scatter | solution.py:73
  217.9 2.2 pad_maximum_fusion.1
  220.1 0.0 all-gather.5.cloned.1.call-update
  220.1 0.0 all-gather.9.cloned.1.call-start
  220.2 5.4 %all-gather = f32[4,1,4096]{2,1,0:T(1,128)S(1)} all-gather(f32[1,1,4096]{2,1,0:T(1,128)S(1)} %bitcast.100), channel_id=1, replica_groups=mesh['layer'=4,'tok'=8] {'layer'}, dimensions={0}, use_global_device_ids=true | all-gather | bytes 81920 | tf_op jit(solution)/shard_map/all_gather | solution.py:35
  225.5 1.3 convert_element_type.108
  226.8 0.0 all-gather.7.cloned.1.call-done
  226.9 27.4 %all-gather.5.cloned.1.call-done = bf16[4,128,4096]{2,1,0:T(8,128)(2,1)} async-done(((bf16[1,128,4096]{2,1,0:T(8,128)(2,1)}), bf16[4,128,4096]{2,1,0:T(8,128)(2,1)}) %all-gather.5.cloned.1.call-update) | async-done | bytes 4194320 | tf_op jit(solution)/shard_map/all_gather | solution.py:37
  254.3 5.4 %fusion.26 = bf16[128,4096]{1,0:T(8,128)(2,1)} fusion(bf16[128,4096]{1,0:T(8,128)(2,1)S(1)} %copy-done.3, f32[128,1536]{1,0:T(8,128)S(1)} %copy-done.1, f32[128,2560]{1,0:T(8,128)S(1)} %convert_element_type.108, bf16[4,128,4096]{2,1,0:T(8,128)(2,1)} %all-gather.7.cloned.1.call-done, f32[4096]{0:T(1024)S(1)} %bitcast.98, f32[4096]{0:T(1024)S(1)} %bitcast.94, ...), kind=kLoop, calls=%fused_computation.30 | loop fusion | flops 19398656 | bytes 12648452 | tf_op jit(solution)/shard_map/convert_element_type | solution.py:82
  259.7 0.0 all-gather.9.cloned.1.call-update
  259.7 125.1 %all-gather.9.cloned.1.call-done = bf16[1024,4096]{1,0:T(8,128)(2,1)} async-done(((bf16[128,4096]{1,0:T(8,128)(2,1)}), bf16[1024,4096]{1,0:T(8,128)(2,1)}) %all-gather.9.cloned.1.call-update) | async-done | bytes 8388624 | tf_op jit(solution)/shard_map/all_gather | solution.py:83
  384.8 42.6 %convert_bitcast_fusion = bf16[128,8,32,128]{3,1,2,0:T(8,128)(2,1)} fusion(bf16[1024,4096]{1,0:T(8,128)(2,1)} %all-gather.9.cloned.1.call-done, bf16[1,4096,4096]{2,1,0:T(8,128)(2,1)} %param.8), kind=kOutput, calls=%fused_computation.11 | convolution fusion | flops 34363932672 | bytes 50331648 | tf_op jit(solution)/shard_map/dot_general | solution.py:84
  427.4 9.5 %copy.24 = bf16[128,8,32,128]{3,2,1,0:T(8,128)(2,1)} copy(bf16[128,8,32,128]{3,1,2,0:T(8,128)(2,1)} %convert_bitcast_fusion) | data formatting | bytes 16777216
  436.9 0.0 copy-done.7
  436.9 10.7 %select_reduce_fusion = f32[1024,32]{1,0:T(8,128)} fusion(s32[1024,32]{1,0:T(8,128)S(1)} %copy-done.7, bf16[1024,32,128]{2,1,0:T(8,128)(2,1)} %bitcast.87, s32[1024,32]{1,0:T(8,128)S(1)} %copy-done.5), kind=kOutput, calls=%fused_computation.2 | convolution fusion | flops 275742720 | bytes 8781824 | tf_op jit(solution)/shard_map/thl,tkl->tkh/dot_general | solution.py:88
  447.7 1.9 copy.19
  449.5 3.4 all-to-all-start.2
  452.9 3.8 fusion.31
  456.7 3.5 all-to-all-done.2
  460.2 0.6 reduce_sum.29
  (16 shorter events, 0.1 us)
Async XLA Ops:
  10.1 16.2 %all-to-all-start = ((f32[8,128,64]{1,2,0:T(8,128)}), f32[8,128,64]{1,2,0:T(8,128)S(1)}, u32[]{:S(2)}, u32[]{:S(2)}) async-start(f32[8,128,64]{1,2,0:T(8,128)} %broadcast_in_dim.35), calls=%async_computation | async-start | bytes 524288 | tf_op jit(solution)/shard_map/all_to_all | solution.py:27
  17.4 200.5 %reduce-scatter.2.cloned.1.call-start = ((), (), s32[]{:S(2)}) async-start(), calls=%async_computation.4 | async-start | bytes 5898240 | tf_op jit(solution)/shard_map/reduce_scatter | solution.py:73
  26.8 10.1 %copy-start.4 = (s32[1024,32]{1,0:T(8,128)}, s32[1024,32]{1,0:T(8,128)S(1)}, u32[]{:S(2)}) copy-start(s32[1024,32]{1,0:T(8,128)S(1)} %copy.17) | copy-start | bytes 393220
  27.0 9.9 %copy-start.6 = (s32[1024,32]{1,0:T(8,128)}, s32[1024,32]{1,0:T(8,128)S(1)}, u32[]{:S(2)}) copy-start(s32[1024,32]{1,0:T(8,128)S(1)} %copy.15) | copy-start | bytes 393220
  36.9 3.2 copy-start.2
  101.2 84.3 %all-to-all-start.1 = ((bf16[8,128,1536]{2,1,0:T(8,128)(2,1)}), bf16[8,128,1536]{2,1,0:T(8,128)(2,1)S(1)}, u32[]{:S(2)}, u32[]{:S(2)}) async-start(bf16[8,128,1536]{2,1,0:T(8,128)(2,1)} %bitcast.89), calls=%async_computation.2 | async-start | bytes 6291456 | tf_op jit(solution)/shard_map/all_to_all | solution.py:76
  104.8 122.0 %all-gather.7.cloned.1.call-start = ((), (), s32[]{:S(2)}) async-start(), calls=%async_computation.6 | async-start | bytes 5242880 | tf_op jit(solution)/shard_map/all_gather | solution.py:36
  105.4 148.9 %all-gather.5.cloned.1.call-start = ((), (), s32[]{:S(2)}) async-start(), calls=%async_computation.5 | async-start | bytes 5242880 | tf_op jit(solution)/shard_map/all_gather | solution.py:37
  185.9 0.9 copy-start
  186.8 33.3 %copy-start.8 = (f32[1,4096]{1,0:T(1,128)S(1)}, f32[1,4096]{1,0:T(1,128)}, u32[]{:S(2)}) copy-start(f32[1,4096]{1,0:T(1,128)} %param.9) | copy-start | bytes 49156
  220.1 34.2 %copy-start.1 = (f32[128,1536]{1,0:T(8,128)S(1)}, f32[128,1536]{1,0:T(8,128)}, u32[]{:S(2)}) copy-start(f32[128,1536]{1,0:T(8,128)} %copy-done) | copy-start | bytes 2359300
  220.1 34.2 %copy-start.3 = (bf16[128,4096]{1,0:T(8,128)(2,1)S(1)}, bf16[128,4096]{1,0:T(8,128)(2,1)}, u32[]{:S(2)}) copy-start(bf16[128,4096]{1,0:T(8,128)(2,1)} %param.10) | copy-start | bytes 3145732
  220.1 164.7 %all-gather.9.cloned.1.call-start = ((), (), s32[]{:S(2)}) async-start(), calls=%async_computation.7 | async-start | bytes 9437184 | tf_op jit(solution)/shard_map/all_gather | solution.py:83
  427.4 9.5 %copy-start.5 = (s32[1024,32]{1,0:T(8,128)S(1)}, s32[1024,32]{1,0:T(8,128)}, u32[]{:S(2)}) copy-start(s32[1024,32]{1,0:T(8,128)} %copy-done.4) | copy-start | bytes 393220
  427.4 9.5 %copy-start.7 = (s32[1024,32]{1,0:T(8,128)S(1)}, s32[1024,32]{1,0:T(8,128)}, u32[]{:S(2)}) copy-start(s32[1024,32]{1,0:T(8,128)} %copy-done.6) | copy-start | bytes 393220
  449.5 10.7 %all-to-all-start.2 = ((f32[8,128,32]{1,2,0:T(8,128)}), f32[8,128,32]{1,2,0:T(8,128)S(1)}, u32[]{:S(2)}, u32[]{:S(2)}) async-start(f32[8,128,32]{1,2,0:T(8,128)} %copy.19), calls=%async_computation.3 | async-start | bytes 262144 | tf_op jit(solution)/shard_map/all_to_all | solution.py:95
Sparse Core Ops, SparseCore 0:
  66.9 150.9 reduce-scatter.1
  259.9 124.9 all-gather.8
Sparse Core Ops, SparseCore 1:
  106.9 35.6 all-gather.6
  220.2 34.1 all-gather.4

commit v12 on v4

--- a/solution.py
+++ b/solution.py
@@ -73,24 +73,6 @@
     return jnp.concatenate(results, axis=1)
 
 
-def ring_all_gather(piece, ring):
-    count = len(ring)
-    members, here, forward, backward = ring_tables(ring)
-    half = piece.shape[1] // 2
-    gathered = jnp.zeros((count,) + piece.shape, piece.dtype)
-    me = lax.axis_index("tok")
-    gathered = lax.dynamic_update_index_in_dim(gathered, piece, me, 0)
-    sides = ((forward, -1, 0, piece[:, :half]), (backward, 1, half, piece[:, half:]))
-    for perm, sign, offset, travelling in sides:
-        for s in range(count - 1):
-            travelling = lax.ppermute(travelling, "tok", perm)
-            source = members[(here + sign * (s + 1)) % count]
-            gathered = lax.dynamic_update_slice(
-                gathered, travelling[None], (source, jnp.int32(0), jnp.int32(offset))
-            )
-    return gathered.reshape(count * piece.shape[0], piece.shape[1])
-
-
 def exchange_codes(latent_ids, active_codes):
     owners = lax.axis_size("tok")
     top_count = latent_ids.shape[1]
@@ -140,20 +122,24 @@
         "tkh,tkl->thl", coded_high, low_hot.astype(jnp.bfloat16), preferred_element_type=jnp.float32
     )
     spread = spread.astype(jnp.bfloat16).reshape(tokens, range_size)
-    partial = jnp.dot(spread, weights, preferred_element_type=jnp.float32).astype(jnp.bfloat16)
-    decoded = ring_reduce_scatter(partial, ring)
+    half = weights.shape[1] // 2
+    w_first, w_second = weights[:, :half], weights[:, half:]
+    partial_first = jnp.dot(spread, w_first, preferred_element_type=jnp.float32).astype(jnp.bfloat16)
+    decoded_first = lax.psum_scatter(partial_first, "tok", scatter_dimension=0, tiled=True)
+    partial_second = jnp.dot(spread, w_second, preferred_element_type=jnp.float32).astype(jnp.bfloat16)
+    decoded_second = ring_reduce_scatter(partial_second, ring)
+    decoded = jnp.concatenate([decoded_first.astype(jnp.float32), decoded_second], axis=1)
     recon_full, grad_sum = layer_chain(decoded, carry_gain, earlier_sum, targets)
     grad_low = grad_sum.astype(jnp.bfloat16)
-    segment = ring_all_gather(grad_low, ring)
+    segment = lax.all_gather(grad_low, "tok", axis=0, tiled=True)
     products = lax.dot_general(
         segment, weights, (((1,), (1,)), ((), ())), preferred_element_type=jnp.float32
-    )
+    ).astype(jnp.bfloat16)
     products = products.reshape(tokens, range_size // LANES, LANES)
     picked_low = jnp.einsum(
         "thl,tkl->tkh",
         products,
-        low_hot.astype(jnp.float32),
-        precision=lax.Precision.HIGHEST,
+        low_hot.astype(jnp.bfloat16),
         preferred_element_type=jnp.float32,
     )
     partial_grad = jnp.sum(jnp.where(high_hot, picked_low, 0.0), axis=-1)

time: 575 us -> 469 us (0.82)
  starting transfers between devices: 160 us -> 62.8 us
  waiting for transfers between devices: 176 us -> 192 us
  matrix products: 121 us -> 108 us
  local copies, waits for them, and re-layouts: 30.5 us -> 19.2 us
    all_gather x0 -> x1, waiting for transfers between devices: none -> 125 us  [on_device(): segment = lax.all_gather(grad_low, 'tok', axis=0, tiled=True)]
    ppermute x14 -> x0, waiting for transfers between devices: 95.3 us -> none  [ring_all_gather(): travelling = lax.ppermute(travelling, 'tok', perm)]
    ppermute x14 -> x0, starting transfers between devices: 62.5 us -> none  [ring_all_gather(): travelling = lax.ppermute(travelling, 'tok', perm)]
    ppermute x14, starting transfers between devices: 79.6 us -> 52 us  [ring_reduce_scatter(): arrived = lax.ppermute(running, 'tok', perm)]
    ppermute x14, waiting for transfers between devices: 32.2 us -> 18.5 us  [ring_reduce_scatter(): arrived = lax.ppermute(running, 'tok', perm)]
    dynamic_update_slice x14 -> x0, local copies, waits for them, and re-layouts: 11.8 us -> none  [ring_all_gather(): lax.dynamic_update_slice(gathered, travelling[None], (source, jnp.int32(0...]
    dot_general x2 -> x3, matrix products: 66.9 us -> 55.7 us  [the longest x1 23.1 us: on_device(): jnp.dot(spread, w_second, preferred_element_type=jnp.float32)]
    unnamed x14 -> x19, local copies, waits for them, and re-layouts: 3.25 us -> 14.2 us
  transfers between devices with their start and end apart: 32 -> 20, of which waited for: 25 -> 11; matrix products, arithmetic and copies ran while one was open for 6% -> 9% of each run, Pallas kernels for 0% -> 0%
where the time goes in v12:
time: 469 us; the launch traced here: 468 us
  waiting for transfers between devices  192 us (41%)
  matrix products  108 us (23%)
  starting transfers between devices  62.8 us (13%)
  between operations  56.1 us (12%)
  other arithmetic  24.1 us (5%)
  local copies, waits for them, and re-layouts  19.2 us (4%)
  blocking collectives  5.68 us (1%)
    all_gather x1, waiting for transfers between devices, on_device(): segment = lax.all_gather(grad_low, 'tok', axis=0, tiled=True)  125 us
    ppermute x14, starting transfers between devices, ring_reduce_scatter(): arrived = lax.ppermute(running, 'tok', perm)  52 us
    dot_general x1, matrix products, on_device(): lax.dot_general(segment, weights, (((1,), (1,)), ((), ())), preferred_ele...  42.6 us
    all_gather x1, waiting for transfers between devices, layer_chain(): lax.all_gather(decoded.astype(jnp.bfloat16), 'layer', axis=0, tiled=False)  35.2 us
    dot_general x1, matrix products, on_device(): jnp.dot(spread, w_second, preferred_element_type=jnp.float32)  23.1 us
    dot_general x1, matrix products, on_device(): jnp.dot(spread, w_first, preferred_element_type=jnp.float32)  21.8 us
    ppermute x14, waiting for transfers between devices, ring_reduce_scatter(): arrived = lax.ppermute(running, 'tok', perm)  18.5 us
    unnamed x19, local copies, waits for them, and re-layouts  14.2 us
  transfers between devices with their start and end apart: 20, of which 11 were waited for; matrix products, arithmetic and copies ran while one was open for 9% of the time, Pallas kernels for 0%

profile of v12, /device:TPU:0, one launch (start us, length us, event | category | flops | bytes accessed | tf_op | source)
XLA Modules:
  0.0 467.6 jit_solution(6117830642414389049)
XLA Ops:
  8.0 0.7 bitcast_convert_fusion
  8.7 0.7 convert_bitcast_fusion.3
  9.4 0.7 broadcast_in_dim.35
  10.1 7.3 %all-to-all-start = ((f32[8,128,64]{1,2,0:T(8,128)}), f32[8,128,64]{1,2,0:T(8,128)S(1)}, u32[]{:S(2)}, u32[]{:S(2)}) async-start(f32[8,128,64]{1,2,0:T(8,128)} %broadcast_in_dim.35), calls=%async_computation | async-start | bytes 524288 | tf_op jit(solution)/shard_map/all_to_all | solution.py:83
  17.5 8.9 %all-to-all-done = f32[8,128,64]{1,2,0:T(8,128)S(1)} async-done(((f32[8,128,64]{1,2,0:T(8,128)}), f32[8,128,64]{1,2,0:T(8,128)S(1)}, u32[]{:S(2)}, u32[]{:S(2)}) %all-to-all-start) | async-done | bytes 262176 | tf_op jit(solution)/shard_map/all_to_all | solution.py:83
  27.2 9.7 %fusion.15 = bf16[1024,32,128]{2,1,0:T(8,128)(2,1)S(1)} fusion(s32[1024,32]{1,0:T(8,128)S(1)} %copy.19, s32[1024,32]{1,0:T(8,128)S(1)} %copy.17, bf16[1024,32]{1,0:T(8,128)(2,1)S(1)} %copy.18), kind=kOutput, calls=%fused_computation.18 | convolution fusion | flops 278921216 | bytes 8716288 | tf_op jit(solution)/shard_map/tkh,tkl->thl/dot_general | solution.py:121
  36.9 3.3 copy-done.8
  40.2 21.8 %fusion.20 = bf16[1024,2048]{1,0:T(8,128)(2,1)} fusion(bf16[4096,4096]{1,0:T(8,128)(2,1)} %bitcast.185, bf16[128,8,32,128]{3,2,1,0:T(8,128)(2,1)S(1)} %bitcast.187), kind=kOutput, calls=%fused_computation.21 | convolution fusion | flops 17181966336 | bytes 29360128 | tf_op jit(solution)/shard_map/dot_general | solution.py:127
  73.9 0.8 fusion.61
  76.4 23.1 %fusion.25 = bf16[1024,2048]{1,0:T(8,128)(2,1)S(1)} fusion(bf16[4096,4096]{1,0:T(8,128)(2,1)} %bitcast.186, bf16[128,8,32,128]{3,2,1,0:T(8,128)(2,1)} %bitcast.188), kind=kOutput, calls=%fused_computation.22 | convolution fusion | flops 17181966336 | bytes 29360128 | tf_op jit(solution)/shard_map/dot_general | solution.py:129
  100.0 1.3 copy-done
  101.3 1.3 collective-permute-start.7
  104.3 1.0 collective-permute-start
  109.0 4.3 collective-permute-done.7
  113.3 1.0 fusion.45
  114.3 0.9 collective-permute-start.8
  115.3 1.3 collective-permute-start.1
  120.4 4.9 %collective-permute-done.8 = bf16[128,1024]{1,0:T(8,128)(2,1)S(1)} collective-permute-done((bf16[128,1024]{1,0:T(8,128)(2,1)S(1)}, bf16[128,1024]{1,0:T(8,128)(2,1)S(1)}, u32[]{:S(2)}, u32[]{:S(2)}) %collective-permute-start.8) | collective-permute-done | bytes 262176 | tf_op jit(solution)/shard_map/ppermute | solution.py:66
  125.3 1.0 fusion.44
  126.3 3.0 collective-permute-start.9
  133.5 1.0 fusion.43
  134.6 4.4 collective-permute-start.10
  142.5 5.9 %collective-permute-done.10 = bf16[128,1024]{1,0:T(8,128)(2,1)S(1)} collective-permute-done((bf16[128,1024]{1,0:T(8,128)(2,1)S(1)}, bf16[128,1024]{1,0:T(8,128)(2,1)S(1)}, u32[]{:S(2)}, u32[]{:S(2)}) %collective-permute-start.10) | collective-permute-done | bytes 262176 | tf_op jit(solution)/shard_map/ppermute | solution.py:66
  148.4 1.0 fusion.42
  149.4 4.4 collective-permute-start.11
  153.9 8.2 %collective-permute-start.4 = (bf16[128,1024]{1,0:T(8,128)(2,1)S(1)}, bf16[128,1024]{1,0:T(8,128)(2,1)S(1)}, u32[]{:S(2)}, u32[]{:S(2)}) collective-permute-start(bf16[128,1024]{1,0:T(8,128)(2,1)S(1)} %fusion.48), channel_id=1, source_target_pairs={{0,1},{1,3},{3,2},{2,4},{4,5},{5,7},{7,6},{6,0},{8,9},{9,11},{11,1... | collective-permute-start | bytes 786440 | tf_op jit(solution)/shard_map/ppermute | solution.py:66
  166.3 1.0 fusion.41
  167.5 9.1 %collective-permute-start.5 = (bf16[128,1024]{1,0:T(8,128)(2,1)S(1)}, bf16[128,1024]{1,0:T(8,128)(2,1)S(1)}, u32[]{:S(2)}, u32[]{:S(2)}) collective-permute-start(bf16[128,1024]{1,0:T(8,128)(2,1)S(1)} %fusion.47), channel_id=1, source_target_pairs={{0,1},{1,3},{3,2},{2,4},{4,5},{5,7},{7,6},{6,0},{8,9},{9,11},{11,1... | collective-permute-start | bytes 786440 | tf_op jit(solution)/shard_map/ppermute | solution.py:66
  180.5 1.1 collective-permute-done.12
  181.7 1.0 fusion.40
  182.9 18.2 %collective-permute-start.6 = (bf16[128,1024]{1,0:T(8,128)(2,1)S(1)}, bf16[128,1024]{1,0:T(8,128)(2,1)}, u32[]{:S(2)}, u32[]{:S(2)}) collective-permute-start(bf16[128,1024]{1,0:T(8,128)(2,1)S(1)} %fusion.46), channel_id=1, source_target_pairs={{0,1},{1,3},{3,2},{2,4},{4,5},{5,7},{7,6},{6,0},{8,9},{9,11},{11,1... | collective-permute-start | bytes 786440 | tf_op jit(solution)/shard_map/ppermute | solution.py:66
  205.0 1.3 collective-permute-done.13
  206.4 1.0 convert_bitcast_fusion.1
  207.4 1.7 convert_bitcast_fusion.2
  209.1 2.3 pad_maximum_fusion.1
  211.5 5.7 %all-gather = f32[4,1,4096]{2,1,0:T(1,128)S(1)} all-gather(f32[1,1,4096]{2,1,0:T(1,128)S(1)} %bitcast.183), channel_id=1, replica_groups=mesh['layer'=4,'tok'=8] {'layer'}, dimensions={0}, use_global_device_ids=true | all-gather | bytes 81920 | tf_op jit(solution)/shard_map/all_gather | solution.py:91
  217.2 1.1 convert_element_type.267
  218.4 35.2 %all-gather.5.cloned.1.call-done = bf16[4,128,4096]{2,1,0:T(8,128)(2,1)} async-done(((bf16[1,128,4096]{2,1,0:T(8,128)(2,1)}), bf16[4,128,4096]{2,1,0:T(8,128)(2,1)}) %all-gather.5.cloned.1.call-update) | async-done | bytes 4194320 | tf_op jit(solution)/shard_map/all_gather | solution.py:93
  253.6 5.4 %fusion.34 = bf16[128,4096]{1,0:T(8,128)(2,1)} fusion(bf16[128,4096]{1,0:T(8,128)(2,1)S(1)} %copy-done.1, f32[128,1024]{1,0:T(8,128)S(1)} %get-tuple-element.5, f32[128,1024]{1,0:T(8,128)S(1)} %get-tuple-element.3, f32[128,2048]{1,0:T(8,128)S(1)} %convert_element_type.267, bf16[4,128,4096]{2,1,0:T(8,128)(2,1)} %all-gather.7.cloned.1.call-done, ...), kind=kLoop, calls=%fused_computation.32 | loop fusion | flops 19922944 | bytes 12648452 | tf_op jit(solution)/shard_map/convert_element_type | solution.py:133
  259.0 125.1 %all-gather.9.cloned.1.call-done = bf16[1024,4096]{1,0:T(8,128)(2,1)} async-done(((bf16[128,4096]{1,0:T(8,128)(2,1)}), bf16[1024,4096]{1,0:T(8,128)(2,1)}) %all-gather.9.cloned.1.call-update) | async-done | bytes 8388624 | tf_op jit(solution)/shard_map/all_gather | solution.py:134
  384.1 42.6 %convert_bitcast_fusion = bf16[128,8,32,128]{3,1,2,0:T(8,128)(2,1)} fusion(bf16[1024,4096]{1,0:T(8,128)(2,1)} %all-gather.9.cloned.1.call-done, bf16[1,4096,4096]{2,1,0:T(8,128)(2,1)} %param.10), kind=kOutput, calls=%fused_computation.12 | convolution fusion | flops 34363932672 | bytes 50331648 | tf_op jit(solution)/shard_map/dot_general | solution.py:135
  426.7 9.6 %copy.26 = bf16[128,8,32,128]{3,2,1,0:T(8,128)(2,1)} copy(bf16[128,8,32,128]{3,1,2,0:T(8,128)(2,1)} %convert_bitcast_fusion) | data formatting | bytes 16777216
  436.3 10.7 %select_reduce_fusion = f32[1024,32]{1,0:T(8,128)} fusion(s32[1024,32]{1,0:T(8,128)S(1)} %copy-done.5, bf16[1024,32,128]{2,1,0:T(8,128)(2,1)} %bitcast.171, s32[1024,32]{1,0:T(8,128)S(1)} %copy-done.3), kind=kOutput, calls=%fused_computation.4 | convolution fusion | flops 275742720 | bytes 8781824 | tf_op jit(solution)/shard_map/thl,tkl->tkh/dot_general | solution.py:139
  447.1 1.9 copy.21
  448.9 3.4 all-to-all-start.1
  452.3 3.8 fusion.39
  456.1 3.5 all-to-all-done.1
  459.6 0.6 reduce_sum.19
  (58 shorter events, 4.3 us)
Async XLA Ops:
  10.1 16.2 %all-to-all-start = ((f32[8,128,64]{1,2,0:T(8,128)}), f32[8,128,64]{1,2,0:T(8,128)S(1)}, u32[]{:S(2)}, u32[]{:S(2)}) async-start(f32[8,128,64]{1,2,0:T(8,128)} %broadcast_in_dim.35), calls=%async_computation | async-start | bytes 524288 | tf_op jit(solution)/shard_map/all_to_all | solution.py:83
  17.4 191.7 %reduce-scatter.2.cloned.1.call-start = ((), (), s32[]{:S(2)}) async-start(), calls=%async_computation.3 | async-start | bytes 4718592 | tf_op jit(solution)/shard_map/reduce_scatter | solution.py:128
  26.8 10.1 %copy-start.2 = (s32[1024,32]{1,0:T(8,128)}, s32[1024,32]{1,0:T(8,128)S(1)}, u32[]{:S(2)}) copy-start(s32[1024,32]{1,0:T(8,128)S(1)} %copy.19) | copy-start | bytes 393220
  27.0 9.9 %copy-start.4 = (s32[1024,32]{1,0:T(8,128)}, s32[1024,32]{1,0:T(8,128)S(1)}, u32[]{:S(2)}) copy-start(s32[1024,32]{1,0:T(8,128)S(1)} %copy.17) | copy-start | bytes 393220
  36.9 3.3 copy-start.8
  62.0 0.7 copy-start.6
  62.0 156.3 %all-gather.7.cloned.1.call-start = ((), (), s32[]{:S(2)}) async-start(), calls=%async_computation.5 | async-start | bytes 5242880 | tf_op jit(solution)/shard_map/all_gather | solution.py:92
  62.6 191.0 %all-gather.5.cloned.1.call-start = ((), (), s32[]{:S(2)}) async-start(), calls=%async_computation.4 | async-start | bytes 5242880 | tf_op jit(solution)/shard_map/all_gather | solution.py:93
  99.9 1.3 copy-start
  101.3 12.0 %collective-permute-start.7 = (bf16[128,1024]{1,0:T(8,128)(2,1)S(1)}, bf16[128,1024]{1,0:T(8,128)(2,1)S(1)}, u32[]{:S(2)}, u32[]{:S(2)}) collective-permute-start(bf16[128,1024]{1,0:T(8,128)(2,1)S(1)} %dynamic-slice_bitcast_fusion), channel_id=1, source_target_pairs={{1,0},{3,1},{2,3},{4,2},{5,4},{7,5},{6,7},{0,6},{9,8},{11,9},{10,1... | collective-permute-start | bytes 786440 | tf_op jit(solution)/shard_map/ppermute | solution.py:66
  104.3 10.9 %collective-permute-start = (bf16[128,1024]{1,0:T(8,128)(2,1)S(1)}, bf16[128,1024]{1,0:T(8,128)(2,1)S(1)}, u32[]{:S(2)}, u32[]{:S(2)}) collective-permute-start(bf16[128,1024]{1,0:T(8,128)(2,1)S(1)} %dynamic-slice_bitcast_fusion.1), channel_id=1, source_target_pairs={{0,1},{1,3},{3,2},{2,4},{4,5},{5,7},{7,6},{6,0},{8,9},{9,11},{11,1... | collective-permute-start | bytes 786440 | tf_op jit(solution)/shard_map/ppermute | solution.py:66
  114.3 11.0 %collective-permute-start.8 = (bf16[128,1024]{1,0:T(8,128)(2,1)S(1)}, bf16[128,1024]{1,0:T(8,128)(2,1)S(1)}, u32[]{:S(2)}, u32[]{:S(2)}) collective-permute-start(bf16[128,1024]{1,0:T(8,128)(2,1)S(1)} %fusion.45), channel_id=1, source_target_pairs={{1,0},{3,1},{2,3},{4,2},{5,4},{7,5},{6,7},{0,6},{9,8},{11,9},{10,1... | collective-permute-start | bytes 786440 | tf_op jit(solution)/shard_map/ppermute | solution.py:66
  115.3 14.0 %collective-permute-start.1 = (bf16[128,1024]{1,0:T(8,128)(2,1)S(1)}, bf16[128,1024]{1,0:T(8,128)(2,1)S(1)}, u32[]{:S(2)}, u32[]{:S(2)}) collective-permute-start(bf16[128,1024]{1,0:T(8,128)(2,1)S(1)} %fusion.51), channel_id=1, source_target_pairs={{0,1},{1,3},{3,2},{2,4},{4,5},{5,7},{7,6},{6,0},{8,9},{9,11},{11,1... | collective-permute-start | bytes 786440 | tf_op jit(solution)/shard_map/ppermute | solution.py:66
  126.3 7.2 %collective-permute-start.9 = (bf16[128,1024]{1,0:T(8,128)(2,1)S(1)}, bf16[128,1024]{1,0:T(8,128)(2,1)S(1)}, u32[]{:S(2)}, u32[]{:S(2)}) collective-permute-start(bf16[128,1024]{1,0:T(8,128)(2,1)S(1)} %fusion.44), channel_id=1, source_target_pairs={{1,0},{3,1},{2,3},{4,2},{5,4},{7,5},{6,7},{0,6},{9,8},{11,9},{10,1... | collective-permute-start | bytes 786440 | tf_op jit(solution)/shard_map/ppermute | solution.py:66
  129.4 9.6 %collective-permute-start.2 = (bf16[128,1024]{1,0:T(8,128)(2,1)S(1)}, bf16[128,1024]{1,0:T(8,128)(2,1)S(1)}, u32[]{:S(2)}, u32[]{:S(2)}) collective-permute-start(bf16[128,1024]{1,0:T(8,128)(2,1)S(1)} %fusion.50), channel_id=1, source_target_pairs={{0,1},{1,3},{3,2},{2,4},{4,5},{5,7},{7,6},{6,0},{8,9},{9,11},{11,1... | collective-permute-start | bytes 786440 | tf_op jit(solution)/shard_map/ppermute | solution.py:66
  134.6 13.9 %collective-permute-start.10 = (bf16[128,1024]{1,0:T(8,128)(2,1)S(1)}, bf16[128,1024]{1,0:T(8,128)(2,1)S(1)}, u32[]{:S(2)}, u32[]{:S(2)}) collective-permute-start(bf16[128,1024]{1,0:T(8,128)(2,1)S(1)} %fusion.43), channel_id=1, source_target_pairs={{1,0},{3,1},{2,3},{4,2},{5,4},{7,5},{6,7},{0,6},{9,8},{11,9},{10,1... | collective-permute-start | bytes 786440 | tf_op jit(solution)/shard_map/ppermute | solution.py:66
  139.1 14.8 %collective-permute-start.3 = (bf16[128,1024]{1,0:T(8,128)(2,1)S(1)}, bf16[128,1024]{1,0:T(8,128)(2,1)S(1)}, u32[]{:S(2)}, u32[]{:S(2)}) collective-permute-start(bf16[128,1024]{1,0:T(8,128)(2,1)S(1)} %fusion.49), channel_id=1, source_target_pairs={{0,1},{1,3},{3,2},{2,4},{4,5},{5,7},{7,6},{6,0},{8,9},{9,11},{11,1... | collective-permute-start | bytes 786440 | tf_op jit(solution)/shard_map/ppermute | solution.py:66
  149.4 16.9 %collective-permute-start.11 = (bf16[128,1024]{1,0:T(8,128)(2,1)S(1)}, bf16[128,1024]{1,0:T(8,128)(2,1)S(1)}, u32[]{:S(2)}, u32[]{:S(2)}) collective-permute-start(bf16[128,1024]{1,0:T(8,128)(2,1)S(1)} %fusion.42), channel_id=1, source_target_pairs={{1,0},{3,1},{2,3},{4,2},{5,4},{7,5},{6,7},{0,6},{9,8},{11,9},{10,1... | collective-permute-start | bytes 786440 | tf_op jit(solution)/shard_map/ppermute | solution.py:66
  153.9 13.5 %collective-permute-start.4 = (bf16[128,1024]{1,0:T(8,128)(2,1)S(1)}, bf16[128,1024]{1,0:T(8,128)(2,1)S(1)}, u32[]{:S(2)}, u32[]{:S(2)}) collective-permute-start(bf16[128,1024]{1,0:T(8,128)(2,1)S(1)} %fusion.48), channel_id=1, source_target_pairs={{0,1},{1,3},{3,2},{2,4},{4,5},{5,7},{7,6},{6,0},{8,9},{9,11},{11,1... | collective-permute-start | bytes 786440 | tf_op jit(solution)/shard_map/ppermute | solution.py:66
  167.3 14.4 %collective-permute-start.12 = (bf16[128,1024]{1,0:T(8,128)(2,1)S(1)}, bf16[128,1024]{1,0:T(8,128)(2,1)S(1)}, u32[]{:S(2)}, u32[]{:S(2)}) collective-permute-start(bf16[128,1024]{1,0:T(8,128)(2,1)S(1)} %fusion.41), channel_id=1, source_target_pairs={{1,0},{3,1},{2,3},{4,2},{5,4},{7,5},{6,7},{0,6},{9,8},{11,9},{10,1... | collective-permute-start | bytes 786440 | tf_op jit(solution)/shard_map/ppermute | solution.py:66
  167.5 15.3 %collective-permute-start.5 = (bf16[128,1024]{1,0:T(8,128)(2,1)S(1)}, bf16[128,1024]{1,0:T(8,128)(2,1)S(1)}, u32[]{:S(2)}, u32[]{:S(2)}) collective-permute-start(bf16[128,1024]{1,0:T(8,128)(2,1)S(1)} %fusion.47), channel_id=1, source_target_pairs={{0,1},{1,3},{3,2},{2,4},{4,5},{5,7},{7,6},{6,0},{8,9},{9,11},{11,1... | collective-permute-start | bytes 786440 | tf_op jit(solution)/shard_map/ppermute | solution.py:66
  182.7 23.6 %collective-permute-start.13 = (bf16[128,1024]{1,0:T(8,128)(2,1)S(1)}, bf16[128,1024]{1,0:T(8,128)(2,1)S(1)}, u32[]{:S(2)}, u32[]{:S(2)}) collective-permute-start(bf16[128,1024]{1,0:T(8,128)(2,1)S(1)} %fusion.40), channel_id=1, source_target_pairs={{1,0},{3,1},{2,3},{4,2},{5,4},{7,5},{6,7},{0,6},{9,8},{11,9},{10,1... | collective-permute-start | bytes 786440 | tf_op jit(solution)/shard_map/ppermute | solution.py:66
  182.9 24.5 %collective-permute-start.6 = (bf16[128,1024]{1,0:T(8,128)(2,1)S(1)}, bf16[128,1024]{1,0:T(8,128)(2,1)}, u32[]{:S(2)}, u32[]{:S(2)}) collective-permute-start(bf16[128,1024]{1,0:T(8,128)(2,1)S(1)} %fusion.46), channel_id=1, source_target_pairs={{0,1},{1,3},{3,2},{2,4},{4,5},{5,7},{7,6},{6,0},{8,9},{9,11},{11,1... | collective-permute-start | bytes 786440 | tf_op jit(solution)/shard_map/ppermute | solution.py:66
  207.4 4.1 copy-start.7
  209.1 44.5 %copy-start.1 = (bf16[128,4096]{1,0:T(8,128)(2,1)S(1)}, bf16[128,4096]{1,0:T(8,128)(2,1)}, u32[]{:S(2)}) copy-start(bf16[128,4096]{1,0:T(8,128)(2,1)} %param.12) | copy-start | bytes 3145732
  211.4 172.7 %all-gather.9.cloned.1.call-start = ((), (), s32[]{:S(2)}) async-start(), calls=%async_computation.6 | async-start | bytes 9437184 | tf_op jit(solution)/shard_map/all_gather | solution.py:134
  426.7 9.6 %copy-start.3 = (s32[1024,32]{1,0:T(8,128)S(1)}, s32[1024,32]{1,0:T(8,128)}, u32[]{:S(2)}) copy-start(s32[1024,32]{1,0:T(8,128)} %copy-done.2) | copy-start | bytes 393220
  426.7 9.6 %copy-start.5 = (s32[1024,32]{1,0:T(8,128)S(1)}, s32[1024,32]{1,0:T(8,128)}, u32[]{:S(2)}) copy-start(s32[1024,32]{1,0:T(8,128)} %copy-done.4) | copy-start | bytes 393220
  448.9 10.7 %all-to-all-start.1 = ((f32[8,128,32]{1,2,0:T(8,128)}), f32[8,128,32]{1,2,0:T(8,128)S(1)}, u32[]{:S(2)}, u32[]{:S(2)}) async-start(f32[8,128,32]{1,2,0:T(8,128)} %copy.21), calls=%async_computation.2 | async-start | bytes 262144 | tf_op jit(solution)/shard_map/all_to_all | solution.py:146
Sparse Core Ops, SparseCore 0:
  62.1 114.7 reduce-scatter.1
  259.1 124.9 all-gather.8
Sparse Core Ops, SparseCore 1:
  64.1 33.3 all-gather.6
  211.5 42.0 all-gather.4

commit v13 on v12

--- a/solution.py
+++ b/solution.py
@@ -51,26 +51,22 @@
     return jnp.asarray(ring, jnp.int32), here, forward, backward
 
 
-def ring_reduce_scatter(partial, ring):
+def ring_all_gather(piece, ring):
     count = len(ring)
     members, here, forward, backward = ring_tables(ring)
-    blocks = partial.reshape(count, -1, partial.shape[1])
-    half = partial.shape[1] // 2
-    sides = ((forward, -1, slice(0, half)), (backward, 1, slice(half, None)))
-    results = []
-    for perm, sign, cols in sides:
-        own = blocks[:, :, cols]
-        first = lax.dynamic_index_in_dim(own, members[(here + sign) % count], 0, keepdims=False)
-        running = first
+    half = piece.shape[1] // 2
+    gathered = jnp.zeros((count,) + piece.shape, piece.dtype)
+    me = lax.axis_index("tok")
+    gathered = lax.dynamic_update_index_in_dim(gathered, piece, me, 0)
+    sides = ((forward, -1, 0, piece[:, :half]), (backward, 1, half, piece[:, half:]))
+    for perm, sign, offset, travelling in sides:
         for s in range(count - 1):
-            arrived = lax.ppermute(running, "tok", perm)
-            block = members[(here + sign * (s + 2)) % count]
-            total = arrived.astype(jnp.float32) + lax.dynamic_index_in_dim(
-                own, block, 0, keepdims=False
-            ).astype(jnp.float32)
-            running = total.astype(jnp.bfloat16)
-        results.append(total)
-    return jnp.concatenate(results, axis=1)
+            travelling = lax.ppermute(travelling, "tok", perm)
+            source = members[(here + sign * (s + 1)) % count]
+            gathered = lax.dynamic_update_slice(
+                gathered, travelling[None], (source, jnp.int32(0), jnp.int32(offset))
+            )
+    return gathered.reshape(count * piece.shape[0], piece.shape[1])
 
 
 def exchange_codes(latent_ids, active_codes):
@@ -122,16 +118,27 @@
         "tkh,tkl->thl", coded_high, low_hot.astype(jnp.bfloat16), preferred_element_type=jnp.float32
     )
     spread = spread.astype(jnp.bfloat16).reshape(tokens, range_size)
-    half = weights.shape[1] // 2
+    width = weights.shape[1]
+    half = width // 2
     w_first, w_second = weights[:, :half], weights[:, half:]
     partial_first = jnp.dot(spread, w_first, preferred_element_type=jnp.float32).astype(jnp.bfloat16)
     decoded_first = lax.psum_scatter(partial_first, "tok", scatter_dimension=0, tiled=True)
     partial_second = jnp.dot(spread, w_second, preferred_element_type=jnp.float32).astype(jnp.bfloat16)
-    decoded_second = ring_reduce_scatter(partial_second, ring)
+    received = lax.all_to_all(partial_second, "tok", split_axis=0, concat_axis=0, tiled=True)
+    decoded_second = jnp.sum(
+        received.reshape(owners, -1, received.shape[1]).astype(jnp.float32), axis=0
+    )
     decoded = jnp.concatenate([decoded_first.astype(jnp.float32), decoded_second], axis=1)
     recon_full, grad_sum = layer_chain(decoded, carry_gain, earlier_sum, targets)
     grad_low = grad_sum.astype(jnp.bfloat16)
-    segment = lax.all_gather(grad_low, "tok", axis=0, tiled=True)
+    split = 3 * width // 4 if width % (4 * LANES) == 0 else width // 2
+    segment = jnp.concatenate(
+        [
+            lax.all_gather(grad_low[:, :split], "tok", axis=0, tiled=True),
+            ring_all_gather(grad_low[:, split:], ring),
+        ],
+        axis=1,
+    )
     products = lax.dot_general(
         segment, weights, (((1,), (1,)), ((), ())), preferred_element_type=jnp.float32
     ).astype(jnp.bfloat16)

time: 469 us -> 479 us (1.021)
  local copies, waits for them, and re-layouts: 19.2 us -> 30.2 us
  waiting for transfers between devices: 192 us -> 201 us
  other arithmetic: 24.1 us -> 16.7 us
    all_gather x1, waiting for transfers between devices: 125 us -> 5.18 us  [on_device(): lax.all_gather(grad_low[:, :split], 'tok', axis=0, tiled=True)]
    all_to_all x0 -> x1, waiting for transfers between devices: none -> 104 us  [on_device(): lax.all_to_all(partial_second, 'tok', split_axis=0, concat_axis=0, tiled=...]
    reduce_scatter x1, waiting for transfers between devices: 0.01 us -> 18.2 us  [on_device(): lax.psum_scatter(partial_first, 'tok', scatter_dimension=0, tiled=True)]
    ppermute x14, waiting for transfers between devices: 18.5 us -> 32.8 us  [ring_all_gather(): travelling = lax.ppermute(travelling, 'tok', perm)]
    dynamic_update_slice x0 -> x15, local copies, waits for them, and re-layouts: none -> 10.1 us  [the longest x14 9.38 us: ring_all_gather(): lax.dynamic_update_slice(gathered, travelling[None], (source, jnp.int32(0...]
    ppermute x14, starting transfers between devices: 52 us -> 42.3 us  [ring_all_gather(): travelling = lax.ppermute(travelling, 'tok', perm)]
    all_gather x1, waiting for transfers between devices: 35.2 us -> 28.7 us  [layer_chain(): lax.all_gather(decoded.astype(jnp.bfloat16), 'layer', axis=0, tiled=False)]
    convert_element_type x12 -> x0, other arithmetic: 6.51 us -> none  [ring_reduce_scatter(): running = total.astype(jnp.bfloat16)]
  transfers between devices with their start and end apart: 20 -> 21, of which waited for: 11 -> 18; matrix products, arithmetic and copies ran while one was open for 9% -> 10% of each run, Pallas kernels for 0% -> 0%
where the time goes in v13:
time: 479 us; the launch traced here: 478 us
  waiting for transfers between devices  201 us (42%)
  matrix products  108 us (23%)
  starting transfers between devices  64.3 us (13%)
  between operations  51.6 us (11%)
  local copies, waits for them, and re-layouts  30.2 us (6%)
  other arithmetic  16.7 us (3%)
  blocking collectives  5.25 us (1%)
    all_to_all x1, waiting for transfers between devices, on_device(): lax.all_to_all(partial_second, 'tok', split_axis=0, concat_axis=0, tiled=...  104 us
    ppermute x14, starting transfers between devices, ring_all_gather(): travelling = lax.ppermute(travelling, 'tok', perm)  42.3 us
    dot_general x1, matrix products, on_device(): lax.dot_general(segment, weights, (((1,), (1,)), ((), ())), preferred_ele...  42.1 us
    ppermute x14, waiting for transfers between devices, ring_all_gather(): travelling = lax.ppermute(travelling, 'tok', perm)  32.8 us
    all_gather x1, waiting for transfers between devices, layer_chain(): lax.all_gather(decoded.astype(jnp.bfloat16), 'layer', axis=0, tiled=False)  28.7 us
    dot_general x1, matrix products, on_device(): jnp.dot(spread, w_second, preferred_element_type=jnp.float32)  24 us
    dot_general x1, matrix products, on_device(): jnp.dot(spread, w_first, preferred_element_type=jnp.float32)  21.9 us
    reduce_scatter x1, waiting for transfers between devices, on_device(): lax.psum_scatter(partial_first, 'tok', scatter_dimension=0, tiled=True)  18.2 us
  transfers between devices with their start and end apart: 21, of which 18 were waited for; matrix products, arithmetic and copies ran while one was open for 10% of the time, Pallas kernels for 0%

profile of v13, /device:TPU:0, one launch (start us, length us, event | category | flops | bytes accessed | tf_op | source)
XLA Modules:
  0.0 477.9 jit_solution(4159724794533690799)
XLA Ops:
  8.7 0.7 convert_bitcast_fusion.2
  9.4 0.7 broadcast_in_dim.84
  10.1 7.3 %all-to-all-start = ((f32[8,128,64]{1,2,0:T(8,128)}), f32[8,128,64]{1,2,0:T(8,128)S(1)}, u32[]{:S(2)}, u32[]{:S(2)}) async-start(f32[8,128,64]{1,2,0:T(8,128)} %broadcast_in_dim.84), calls=%async_computation | async-start | bytes 524288 | tf_op jit(solution)/shard_map/all_to_all | solution.py:79
  17.5 8.9 %all-to-all-done = f32[8,128,64]{1,2,0:T(8,128)S(1)} async-done(((f32[8,128,64]{1,2,0:T(8,128)}), f32[8,128,64]{1,2,0:T(8,128)S(1)}, u32[]{:S(2)}, u32[]{:S(2)}) %all-to-all-start) | async-done | bytes 262176 | tf_op jit(solution)/shard_map/all_to_all | solution.py:79
  27.2 9.7 %fusion.21 = bf16[1024,32,128]{2,1,0:T(8,128)(2,1)S(1)} fusion(s32[1024,32]{1,0:T(8,128)S(1)} %copy.19, s32[1024,32]{1,0:T(8,128)S(1)} %copy.17, bf16[1024,32]{1,0:T(8,128)(2,1)S(1)} %copy.18), kind=kOutput, calls=%fused_computation.23 | convolution fusion | flops 278921216 | bytes 8716288 | tf_op jit(solution)/shard_map/tkh,tkl->thl/dot_general | solution.py:117
  36.9 3.3 copy-done.8
  40.2 21.9 %fusion.26 = bf16[1024,2048]{1,0:T(8,128)(2,1)} fusion(bf16[4096,4096]{1,0:T(8,128)(2,1)} %bitcast.163, bf16[128,8,32,128]{3,2,1,0:T(8,128)(2,1)S(1)} %bitcast.165), kind=kOutput, calls=%fused_computation.26 | convolution fusion | flops 17181966336 | bytes 29360128 | tf_op jit(solution)/shard_map/dot_general | solution.py:124
  62.1 24.0 %fusion.31 = bf16[1024,2048]{1,0:T(8,128)(2,1)} fusion(bf16[4096,4096]{1,0:T(8,128)(2,1)} %bitcast.164, bf16[128,8,32,128]{3,2,1,0:T(8,128)(2,1)} %bitcast.166), kind=kOutput, calls=%fused_computation.27 | convolution fusion | flops 17181966336 | bytes 29360128 | tf_op jit(solution)/shard_map/dot_general | solution.py:126
  86.1 4.6 all-to-all-start.1
  91.5 103.6 %all-to-all-done.1 = bf16[8,128,2048]{2,1,0:T(8,128)(2,1)} async-done(((bf16[8,128,2048]{2,1,0:T(8,128)(2,1)}), bf16[8,128,2048]{2,1,0:T(8,128)(2,1)}, u32[]{:S(2)}, u32[]{:S(2)}) %all-to-all-start.1) | async-done | bytes 4194336 | tf_op jit(solution)/shard_map/all_to_all | solution.py:127
  195.1 3.4 convert_reduce_fusion
  198.5 18.2 %reduce-scatter.2.cloned.1.call-done = bf16[128,2048]{1,0:T(8,128)(2,1)} async-done(((bf16[1024,2048]{1,0:T(8,128)(2,1)}), bf16[128,2048]{1,0:T(8,128)(2,1)}) %reduce-scatter.2.cloned.1.call-update) | async-done | bytes 524304 | tf_op jit(solution)/shard_map/reduce_scatter | solution.py:125
  216.7 2.2 pad_maximum_fusion.1
  219.0 5.2 %all-gather = f32[4,1,4096]{2,1,0:T(1,128)S(1)} all-gather(f32[1,1,4096]{2,1,0:T(1,128)S(1)} %bitcast.161), channel_id=1, replica_groups=mesh['layer'=4,'tok'=8] {'layer'}, dimensions={0}, use_global_device_ids=true | all-gather | bytes 81920 | tf_op jit(solution)/shard_map/all_gather | solution.py:87
  224.3 28.7 %all-gather.5.cloned.1.call-done = bf16[4,128,4096]{2,1,0:T(8,128)(2,1)} async-done(((bf16[1,128,4096]{2,1,0:T(8,128)(2,1)}), bf16[4,128,4096]{2,1,0:T(8,128)(2,1)}) %all-gather.5.cloned.1.call-update) | async-done | bytes 4194320 | tf_op jit(solution)/shard_map/all_gather | solution.py:89
  253.1 4.9 %fusion.40 = bf16[128,4096]{1,0:T(8,128)(2,1)S(1)} fusion(bf16[128,4096]{1,0:T(8,128)(2,1)} %param.12, f32[128,2048]{1,0:T(8,128)S(1)} %convert_reduce_fusion, f32[128,2048]{1,0:T(8,128)S(1)} %convert_element_type.108, bf16[4,128,4096]{2,1,0:T(8,128)(2,1)} %all-gather.7.cloned.1.call-done, f32[4096]{0:T(1024)S(1)} %bitcast.159, f32[4096]{0:T(1024)S(1)} %bitcast.155, ...), kind=kLoop, calls=%fused_computation.37 | loop fusion | flops 19398656 | bytes 12648452 | tf_op jit(solution)/shard_map/convert_element_type | solution.py:133
  258.0 0.9 slice.106
  268.9 0.7 fusion.57
  296.2 1.5 collective-permute-start
  297.7 2.4 collective-permute-start.7
  300.1 1.7 broadcast_in_dim.88
  301.8 0.7 fusion.46
  302.5 1.4 collective-permute-done
  303.9 1.8 collective-permute-done.7
  305.7 4.3 collective-permute-start.8
  310.6 3.6 collective-permute-done.1
  314.3 1.1 collective-permute-done.8
  315.4 4.3 collective-permute-start.9
  320.3 4.1 collective-permute-done.2
  324.4 4.4 collective-permute-done.9
  328.8 4.4 collective-permute-start.10
  333.9 5.7 %collective-permute-done.3 = bf16[128,512]{1,0:T(8,128)(2,1)S(1)} collective-permute-done((bf16[128,512]{1,0:T(8,128)(2,1)S(1)}, bf16[128,512]{1,0:T(8,128)(2,1)S(1)}, u32[]{:S(2)}, u32[]{:S(2)}) %collective-permute-start.3) | collective-permute-done | bytes 131104 | tf_op jit(solution)/shard_map/ppermute | solution.py:64
  339.6 2.8 collective-permute-start.4
  342.4 1.4 collective-permute-done.10
  344.5 4.0 collective-permute-done.4
  348.5 13.8 %collective-permute-start.5 = (bf16[128,512]{1,0:T(8,128)(2,1)S(1)}, bf16[128,512]{1,0:T(8,128)(2,1)S(1)}, u32[]{:S(2)}, u32[]{:S(2)}) collective-permute-start(bf16[128,512]{1,0:T(8,128)(2,1)S(1)} %collective-permute-done.4), channel_id=1, source_target_pairs={{0,1},{1,3},{3,2},{2,4},{4,5},{5,7},{7,6},{6,0},{8,9},{9,11},{11,1... | collective-permute-start | bytes 393224 | tf_op jit(solution)/shard_map/ppermute | solution.py:64
  362.3 2.3 collective-permute-done.11
  365.2 4.5 collective-permute-start.6
  370.4 4.3 collective-permute-start.13
  380.0 2.4 collective-permute-done.13
  383.1 5.2 %all-gather.9.cloned.1.call-done = bf16[1024,3072]{1,0:T(8,128)(2,1)} async-done(((bf16[128,3072]{1,0:T(8,128)(2,1)}), bf16[1024,3072]{1,0:T(8,128)(2,1)}) %all-gather.9.cloned.1.call-update) | async-done | bytes 6291472 | tf_op jit(solution)/shard_map/all_gather | solution.py:137
  388.3 42.1 %convert_bitcast_fusion = bf16[128,8,32,128]{3,1,2,0:T(8,128)(2,1)} fusion(bf16[1024,1024]{1,0:T(8,128)(2,1)} %bitcast.63, bf16[1024,3072]{1,0:T(8,128)(2,1)} %all-gather.9.cloned.1.call-done, bf16[1,4096,4096]{2,1,0:T(8,128)(2,1)} %param.10), kind=kOutput, calls=%fused_computation.16 | convolution fusion | flops 34380709888 | bytes 50331648 | tf_op jit(solution)/shard_map/dot_general | solution.py:142
  430.4 9.6 %copy.26 = bf16[128,8,32,128]{3,2,1,0:T(8,128)(2,1)} copy(bf16[128,8,32,128]{3,1,2,0:T(8,128)(2,1)} %convert_bitcast_fusion) | data formatting | bytes 16777216
  440.0 10.8 %select_reduce_fusion = f32[1024,32]{1,0:T(8,128)} fusion(s32[1024,32]{1,0:T(8,128)S(1)} %copy-done.5, bf16[1024,32,128]{2,1,0:T(8,128)(2,1)} %bitcast.149, s32[1024,32]{1,0:T(8,128)S(1)} %copy-done.3), kind=kOutput, calls=%fused_computation.4 | convolution fusion | flops 275742720 | bytes 8781824 | tf_op jit(solution)/shard_map/thl,tkl->tkh/dot_general | solution.py:146
  450.9 1.9 copy.21
  452.7 9.8 %all-to-all-start.2 = ((f32[8,128,32]{1,2,0:T(8,128)}), f32[8,128,32]{1,2,0:T(8,128)S(1)}, u32[]{:S(2)}, u32[]{:S(2)}) async-start(f32[8,128,32]{1,2,0:T(8,128)} %copy.21), calls=%async_computation.3 | async-start | bytes 262144 | tf_op jit(solution)/shard_map/all_to_all | solution.py:153
  462.5 3.8 fusion.45
  466.3 3.5 all-to-all-done.2
  (63 shorter events, 13.9 us)
Async XLA Ops:
  10.1 16.2 %all-to-all-start = ((f32[8,128,64]{1,2,0:T(8,128)}), f32[8,128,64]{1,2,0:T(8,128)S(1)}, u32[]{:S(2)}, u32[]{:S(2)}) async-start(f32[8,128,64]{1,2,0:T(8,128)} %broadcast_in_dim.84), calls=%async_computation | async-start | bytes 524288 | tf_op jit(solution)/shard_map/all_to_all | solution.py:79
  17.4 199.3 %reduce-scatter.2.cloned.1.call-start = ((), (), s32[]{:S(2)}) async-start(), calls=%async_computation.4 | async-start | bytes 4718592 | tf_op jit(solution)/shard_map/reduce_scatter | solution.py:125
  26.8 10.1 %copy-start.2 = (s32[1024,32]{1,0:T(8,128)}, s32[1024,32]{1,0:T(8,128)S(1)}, u32[]{:S(2)}) copy-start(s32[1024,32]{1,0:T(8,128)S(1)} %copy.19) | copy-start | bytes 393220
  27.0 9.9 %copy-start.4 = (s32[1024,32]{1,0:T(8,128)}, s32[1024,32]{1,0:T(8,128)S(1)}, u32[]{:S(2)}) copy-start(s32[1024,32]{1,0:T(8,128)S(1)} %copy.17) | copy-start | bytes 393220
  36.9 3.3 copy-start.8
  86.1 108.9 %all-to-all-start.1 = ((bf16[8,128,2048]{2,1,0:T(8,128)(2,1)}), bf16[8,128,2048]{2,1,0:T(8,128)(2,1)}, u32[]{:S(2)}, u32[]{:S(2)}) async-start(bf16[8,128,2048]{2,1,0:T(8,128)(2,1)} %bitcast.150), calls=%async_computation.2 | async-start | bytes 8388608 | tf_op jit(solution)/shard_map/all_to_all | solution.py:127
  90.7 133.6 %all-gather.7.cloned.1.call-start = ((), (), s32[]{:S(2)}) async-start(), calls=%async_computation.6 | async-start | bytes 5242880 | tf_op jit(solution)/shard_map/all_gather | solution.py:88
  91.3 161.8 %all-gather.5.cloned.1.call-start = ((), (), s32[]{:S(2)}) async-start(), calls=%async_computation.5 | async-start | bytes 5242880 | tf_op jit(solution)/shard_map/all_gather | solution.py:89
  198.4 20.5 %copy-start.7 = (f32[1,4096]{1,0:T(1,128)S(1)}, f32[1,4096]{1,0:T(1,128)}, u32[]{:S(2)}) copy-start(f32[1,4096]{1,0:T(1,128)} %param.11) | copy-start | bytes 49156
  216.7 7.5 %copy-start.1 = (bf16[128,2048]{1,0:T(8,128)(2,1)S(1)}, bf16[128,2048]{1,0:T(8,128)(2,1)}, u32[]{:S(2)}) copy-start(bf16[128,2048]{1,0:T(8,128)(2,1)} %reduce-scatter.2.cloned.1.call-done) | copy-start | bytes 1572868
  218.9 169.4 %all-gather.9.cloned.1.call-start = ((), (), s32[]{:S(2)}) async-start(), calls=%async_computation.7 | async-start | bytes 7077888 | tf_op jit(solution)/shard_map/all_gather | solution.py:137
  258.0 1.0 copy-start.6
  296.2 7.6 %collective-permute-start = (bf16[128,512]{1,0:T(8,128)(2,1)S(1)}, bf16[128,512]{1,0:T(8,128)(2,1)S(1)}, u32[]{:S(2)}, u32[]{:S(2)}) collective-permute-start(bf16[128,512]{1,0:T(8,128)(2,1)S(1)} %get-tuple-element.5), channel_id=1, source_target_pairs={{0,1},{1,3},{3,2},{2,4},{4,5},{5,7},{7,6},{6,0},{8,9},{9,11},{11,1... | collective-permute-start | bytes 393224 | tf_op jit(solution)/shard_map/ppermute | solution.py:64
  297.7 7.9 %collective-permute-start.7 = (bf16[128,512]{1,0:T(8,128)(2,1)S(1)}, bf16[128,512]{1,0:T(8,128)(2,1)S(1)}, u32[]{:S(2)}, u32[]{:S(2)}) collective-permute-start(bf16[128,512]{1,0:T(8,128)(2,1)S(1)} %get-tuple-element.4), channel_id=1, source_target_pairs={{1,0},{3,1},{2,3},{4,2},{5,4},{7,5},{6,7},{0,6},{9,8},{11,9},{10,1... | collective-permute-start | bytes 393224 | tf_op jit(solution)/shard_map/ppermute | solution.py:64
  303.9 10.4 %collective-permute-start.1 = (bf16[128,512]{1,0:T(8,128)(2,1)S(1)}, bf16[128,512]{1,0:T(8,128)(2,1)S(1)}, u32[]{:S(2)}, u32[]{:S(2)}) collective-permute-start(bf16[128,512]{1,0:T(8,128)(2,1)S(1)} %collective-permute-done), channel_id=1, source_target_pairs={{0,1},{1,3},{3,2},{2,4},{4,5},{5,7},{7,6},{6,0},{8,9},{9,11},{11,1... | collective-permute-start | bytes 393224 | tf_op jit(solution)/shard_map/ppermute | solution.py:64
  305.7 9.7 %collective-permute-start.8 = (bf16[128,512]{1,0:T(8,128)(2,1)S(1)}, bf16[128,512]{1,0:T(8,128)(2,1)S(1)}, u32[]{:S(2)}, u32[]{:S(2)}) collective-permute-start(bf16[128,512]{1,0:T(8,128)(2,1)S(1)} %collective-permute-done.7), channel_id=1, source_target_pairs={{1,0},{3,1},{2,3},{4,2},{5,4},{7,5},{6,7},{0,6},{9,8},{11,9},{10,1... | collective-permute-start | bytes 393224 | tf_op jit(solution)/shard_map/ppermute | solution.py:64
  314.3 10.1 %collective-permute-start.2 = (bf16[128,512]{1,0:T(8,128)(2,1)S(1)}, bf16[128,512]{1,0:T(8,128)(2,1)S(1)}, u32[]{:S(2)}, u32[]{:S(2)}) collective-permute-start(bf16[128,512]{1,0:T(8,128)(2,1)S(1)} %collective-permute-done.1), channel_id=1, source_target_pairs={{0,1},{1,3},{3,2},{2,4},{4,5},{5,7},{7,6},{6,0},{8,9},{9,11},{11,1... | collective-permute-start | bytes 393224 | tf_op jit(solution)/shard_map/ppermute | solution.py:64
  315.4 13.5 %collective-permute-start.9 = (bf16[128,512]{1,0:T(8,128)(2,1)S(1)}, bf16[128,512]{1,0:T(8,128)(2,1)S(1)}, u32[]{:S(2)}, u32[]{:S(2)}) collective-permute-start(bf16[128,512]{1,0:T(8,128)(2,1)S(1)} %collective-permute-done.8), channel_id=1, source_target_pairs={{1,0},{3,1},{2,3},{4,2},{5,4},{7,5},{6,7},{0,6},{9,8},{11,9},{10,1... | collective-permute-start | bytes 393224 | tf_op jit(solution)/shard_map/ppermute | solution.py:64
  324.4 15.2 %collective-permute-start.3 = (bf16[128,512]{1,0:T(8,128)(2,1)S(1)}, bf16[128,512]{1,0:T(8,128)(2,1)S(1)}, u32[]{:S(2)}, u32[]{:S(2)}) collective-permute-start(bf16[128,512]{1,0:T(8,128)(2,1)S(1)} %collective-permute-done.2), channel_id=1, source_target_pairs={{0,1},{1,3},{3,2},{2,4},{4,5},{5,7},{7,6},{6,0},{8,9},{9,11},{11,1... | collective-permute-start | bytes 393224 | tf_op jit(solution)/shard_map/ppermute | solution.py:64
  328.8 15.0 %collective-permute-start.10 = (bf16[128,512]{1,0:T(8,128)(2,1)S(1)}, bf16[128,512]{1,0:T(8,128)(2,1)S(1)}, u32[]{:S(2)}, u32[]{:S(2)}) collective-permute-start(bf16[128,512]{1,0:T(8,128)(2,1)S(1)} %collective-permute-done.9), channel_id=1, source_target_pairs={{1,0},{3,1},{2,3},{4,2},{5,4},{7,5},{6,7},{0,6},{9,8},{11,9},{10,1... | collective-permute-start | bytes 393224 | tf_op jit(solution)/shard_map/ppermute | solution.py:64
  339.6 8.9 %collective-permute-start.4 = (bf16[128,512]{1,0:T(8,128)(2,1)S(1)}, bf16[128,512]{1,0:T(8,128)(2,1)S(1)}, u32[]{:S(2)}, u32[]{:S(2)}) collective-permute-start(bf16[128,512]{1,0:T(8,128)(2,1)S(1)} %collective-permute-done.3), channel_id=1, source_target_pairs={{0,1},{1,3},{3,2},{2,4},{4,5},{5,7},{7,6},{6,0},{8,9},{9,11},{11,1... | collective-permute-start | bytes 393224 | tf_op jit(solution)/shard_map/ppermute | solution.py:64
  343.8 20.7 %collective-permute-start.11 = (bf16[128,512]{1,0:T(8,128)(2,1)S(1)}, bf16[128,512]{1,0:T(8,128)(2,1)S(1)}, u32[]{:S(2)}, u32[]{:S(2)}) collective-permute-start(bf16[128,512]{1,0:T(8,128)(2,1)S(1)} %collective-permute-done.10), channel_id=1, source_target_pairs={{1,0},{3,1},{2,3},{4,2},{5,4},{7,5},{6,7},{0,6},{9,8},{11,9},{10,1... | collective-permute-start | bytes 393224 | tf_op jit(solution)/shard_map/ppermute | solution.py:64
  348.5 16.7 %collective-permute-start.5 = (bf16[128,512]{1,0:T(8,128)(2,1)S(1)}, bf16[128,512]{1,0:T(8,128)(2,1)S(1)}, u32[]{:S(2)}, u32[]{:S(2)}) collective-permute-start(bf16[128,512]{1,0:T(8,128)(2,1)S(1)} %collective-permute-done.4), channel_id=1, source_target_pairs={{0,1},{1,3},{3,2},{2,4},{4,5},{5,7},{7,6},{6,0},{8,9},{9,11},{11,1... | collective-permute-start | bytes 393224 | tf_op jit(solution)/shard_map/ppermute | solution.py:64
  364.5 5.8 %collective-permute-start.12 = (bf16[128,512]{1,0:T(8,128)(2,1)S(1)}, bf16[128,512]{1,0:T(8,128)(2,1)S(1)}, u32[]{:S(2)}, u32[]{:S(2)}) collective-permute-start(bf16[128,512]{1,0:T(8,128)(2,1)S(1)} %collective-permute-done.11), channel_id=1, source_target_pairs={{1,0},{3,1},{2,3},{4,2},{5,4},{7,5},{6,7},{0,6},{9,8},{11,9},{10,1... | collective-permute-start | bytes 393224 | tf_op jit(solution)/shard_map/ppermute | solution.py:64
  365.2 10.1 %collective-permute-start.6 = (bf16[128,512]{1,0:T(8,128)(2,1)S(1)}, bf16[128,512]{1,0:T(8,128)(2,1)S(1)}, u32[]{:S(2)}, u32[]{:S(2)}) collective-permute-start(bf16[128,512]{1,0:T(8,128)(2,1)S(1)} %collective-permute-done.5), channel_id=1, source_target_pairs={{0,1},{1,3},{3,2},{2,4},{4,5},{5,7},{7,6},{6,0},{8,9},{9,11},{11,1... | collective-permute-start | bytes 393224 | tf_op jit(solution)/shard_map/ppermute | solution.py:64
  370.4 12.1 %collective-permute-start.13 = (bf16[128,512]{1,0:T(8,128)(2,1)S(1)}, bf16[128,512]{1,0:T(8,128)(2,1)S(1)}, u32[]{:S(2)}, u32[]{:S(2)}) collective-permute-start(bf16[128,512]{1,0:T(8,128)(2,1)S(1)} %collective-permute-done.12), channel_id=1, source_target_pairs={{1,0},{3,1},{2,3},{4,2},{5,4},{7,5},{6,7},{0,6},{9,8},{11,9},{10,1... | collective-permute-start | bytes 393224 | tf_op jit(solution)/shard_map/ppermute | solution.py:64
  430.4 9.6 %copy-start.3 = (s32[1024,32]{1,0:T(8,128)S(1)}, s32[1024,32]{1,0:T(8,128)}, u32[]{:S(2)}) copy-start(s32[1024,32]{1,0:T(8,128)} %copy-done.2) | copy-start | bytes 393220
  430.4 9.6 %copy-start.5 = (s32[1024,32]{1,0:T(8,128)S(1)}, s32[1024,32]{1,0:T(8,128)}, u32[]{:S(2)}) copy-start(s32[1024,32]{1,0:T(8,128)} %copy-done.4) | copy-start | bytes 393220
  440.0 22.5 %copy-start = (bf16[128,4096]{1,0:T(8,128)(2,1)S(1)}, bf16[128,4096]{1,0:T(8,128)(2,1)}, u32[]{:S(2)}) copy-start(bf16[128,4096]{1,0:T(8,128)(2,1)} %param.12) | copy-start | bytes 3145732
  452.7 17.1 %all-to-all-start.2 = ((f32[8,128,32]{1,2,0:T(8,128)}), f32[8,128,32]{1,2,0:T(8,128)S(1)}, u32[]{:S(2)}, u32[]{:S(2)}) async-start(f32[8,128,32]{1,2,0:T(8,128)} %copy.21), calls=%async_computation.3 | async-start | bytes 262144 | tf_op jit(solution)/shard_map/all_to_all | solution.py:153
Sparse Core Ops, SparseCore 0:
  62.3 154.3 reduce-scatter.1
  259.1 129.1 all-gather.8
Sparse Core Ops, SparseCore 1:
  92.8 35.6 all-gather.6
  219.0 34.0 all-gather.4

commit v14 on v10

--- a/solution.py
+++ b/solution.py
@@ -34,25 +34,47 @@
 def layer_chain(decoded, carry_gain, earlier_sum, targets):
     gains = lax.all_gather(carry_gain[0], "layer", axis=0, tiled=False)
     targets_all = lax.all_gather(targets[0], "layer", axis=0, tiled=False)
-    decoded_all = lax.all_gather(decoded.astype(jnp.bfloat16), "layer", axis=0, tiled=False)
     layers = gains.shape[0]
     me = lax.axis_index("layer")
-    carried = earlier_sum.astype(jnp.float32)
-    misfits = []
-    recon_own = jnp.zeros_like(decoded)
+    one = jnp.ones_like(gains[0])
+    zero = jnp.zeros_like(gains[0])
+
+    def span(first, last):
+        product = one
+        for i in range(first, last + 1):
+            product = product * gains[i]
+        return product
+
+    def pick(values):
+        chosen = zero
+        for l, value in enumerate(values):
+            chosen = jnp.where(me == l, value, chosen)
+        return chosen
+
+    def ahead(l, m):
+        return span(l + 1, m) if m >= l else zero
+
+    recon_weight = [pick([span(n + 1, l) if n <= l else zero for l in range(layers)]) for n in range(layers)]
+    earlier_weight = pick([span(0, l) for l in range(layers)])
+    grad_weight = [
+        pick([sum(ahead(l, m) * span(n + 1, m) for m in range(max(l, n), layers)) for l in range(layers)])
+        for n in range(layers)
+    ]
+    grad_earlier = pick([sum(ahead(l, m) * span(0, m) for m in range(l, layers)) for l in range(layers)])
+    target_weight = [pick([ahead(l, m) for l in range(layers)]) for m in range(layers)]
+    early = grad_earlier[None, :] * earlier_sum.astype(jnp.float32)
     for m in range(layers):
-        own = me == m
-        term = jnp.where(own, decoded, decoded_all[m].astype(jnp.float32))
-        carried = term + gains[m][None, :] * carried
-        recon_own = jnp.where(own, carried, recon_own)
-        misfits.append(carried - targets_all[m].astype(jnp.float32))
-    running = misfits[layers - 1]
-    grad_own = jnp.where(me == layers - 1, running, jnp.zeros_like(running))
-    for m in range(layers - 2, -1, -1):
-        running = misfits[m] + gains[m + 1][None, :] * running
-        grad_own = jnp.where(me == m, running, grad_own)
+        early = early - target_weight[m][None, :] * targets_all[m].astype(jnp.float32)
+    decoded_all = lax.all_gather(decoded.astype(jnp.bfloat16), "layer", axis=0, tiled=False)
+    terms = [
+        jnp.where(me == n, decoded, decoded_all[n].astype(jnp.float32)) for n in range(layers)
+    ]
+    grad_own = early
+    recon_own = earlier_weight[None, :] * earlier_sum.astype(jnp.float32)
+    for n in range(layers):
+        grad_own = grad_own + grad_weight[n][None, :] * terms[n]
+        recon_own = recon_own + recon_weight[n][None, :] * terms[n]
     return recon_own, grad_own
-
 
 def on_device(active_codes, latent_ids, decoder, carry_gain, earlier_sum, targets):
     range_size = decoder.shape[1]

time: 468 us -> 468 us (level)
  transfers between devices with their start and end apart: 7 -> 7, of which waited for: 6 -> 6; matrix products, arithmetic and copies ran while one was open for 7% -> 8% of each run, Pallas kernels for 0% -> 0%
where the time goes in v14:
time: 468 us; the launch traced here: 467 us
  waiting for transfers between devices  286 us (61%)
  matrix products  109 us (23%)
  other arithmetic  19 us (4%)
  local copies, waits for them, and re-layouts  16.2 us (3%)
  between operations  15.7 us (3%)
  starting transfers between devices  15.4 us (3%)
  blocking collectives  5.43 us (1%)
    all_gather x1, waiting for transfers between devices, on_device(): segment = lax.all_gather(grad_low, 'tok', axis=0, tiled=True)  125 us
    all_to_all x1, waiting for transfers between devices, on_device(): lax.all_to_all(partial_second, 'tok', split_axis=0, concat_axis=0, tiled=...  104 us
    dot_general x1, matrix products, on_device(): lax.dot_general(segment, weights, (((1,), (1,)), ((), ())), preferred_ele...  42.6 us
    all_gather x1, waiting for transfers between devices, layer_chain(): lax.all_gather(decoded.astype(jnp.bfloat16), 'layer', axis=0, tiled=False)  27.1 us
    dot_general x1, matrix products, on_device(): jnp.dot(spread, w_second, preferred_element_type=jnp.float32)  24 us
    dot_general x1, matrix products, on_device(): jnp.dot(spread, w_first, preferred_element_type=jnp.float32)  21.9 us
    reduce_scatter x1, waiting for transfers between devices, on_device(): lax.psum_scatter(partial_first, 'tok', scatter_dimension=0, tiled=True)  18.2 us
    unnamed x15, local copies, waits for them, and re-layouts  13 us
  transfers between devices with their start and end apart: 7, of which 6 were waited for; matrix products, arithmetic and copies ran while one was open for 8% of the time, Pallas kernels for 0%

profile of v14, /device:TPU:0, one launch (start us, length us, event | category | flops | bytes accessed | tf_op | source)
XLA Modules:
  0.0 467.1 jit_solution(8938209971942444837)
XLA Ops:
  8.0 0.7 bitcast_convert_fusion
  8.7 0.7 convert_bitcast_fusion.2
  9.4 0.7 broadcast_in_dim.26
  10.1 7.3 %all-to-all-start = ((f32[8,128,64]{1,2,0:T(8,128)}), f32[8,128,64]{1,2,0:T(8,128)S(1)}, u32[]{:S(2)}, u32[]{:S(2)}) async-start(f32[8,128,64]{1,2,0:T(8,128)} %broadcast_in_dim.26), calls=%async_computation | async-start | bytes 524288 | tf_op jit(solution)/shard_map/all_to_all | solution.py:27
  17.4 0.0 reduce-scatter.2.cloned.1.call-start
  17.5 8.9 %all-to-all-done = f32[8,128,64]{1,2,0:T(8,128)S(1)} async-done(((f32[8,128,64]{1,2,0:T(8,128)}), f32[8,128,64]{1,2,0:T(8,128)S(1)}, u32[]{:S(2)}, u32[]{:S(2)}) %all-to-all-start) | async-done | bytes 262176 | tf_op jit(solution)/shard_map/all_to_all | solution.py:27
  26.4 0.1 fusion.45
  26.5 0.1 add_select_fusion
  26.6 0.2 copy.17
  26.8 0.0 copy-start.1
  26.8 0.2 copy.15
  27.0 0.0 copy-start.3
  27.0 0.2 copy.16
  27.2 9.7 %fusion.15 = bf16[1024,32,128]{2,1,0:T(8,128)(2,1)S(1)} fusion(s32[1024,32]{1,0:T(8,128)S(1)} %copy.17, s32[1024,32]{1,0:T(8,128)S(1)} %copy.15, bf16[1024,32]{1,0:T(8,128)(2,1)S(1)} %copy.16), kind=kOutput, calls=%fused_computation.19 | convolution fusion | flops 278921216 | bytes 8716288 | tf_op jit(solution)/shard_map/tkh,tkl->thl/dot_general | solution.py:87
  36.9 0.0 copy-done.1
  36.9 3.3 copy-done.6
  40.3 21.9 %fusion.20 = bf16[1024,2048]{1,0:T(8,128)(2,1)} fusion(bf16[4096,4096]{1,0:T(8,128)(2,1)} %bitcast.176, bf16[128,8,32,128]{3,2,1,0:T(8,128)(2,1)S(1)} %bitcast.178), kind=kOutput, calls=%fused_computation.22 | convolution fusion | flops 17181966336 | bytes 29360128 | tf_op jit(solution)/shard_map/dot_general | solution.py:93
  62.1 0.0 reduce-scatter.2.cloned.1.call-update
  62.1 24.0 %fusion.25 = bf16[1024,2048]{1,0:T(8,128)(2,1)} fusion(bf16[4096,4096]{1,0:T(8,128)(2,1)} %bitcast.177, bf16[128,8,32,128]{3,2,1,0:T(8,128)(2,1)} %bitcast.179), kind=kOutput, calls=%fused_computation.23 | convolution fusion | flops 17181966336 | bytes 29360128 | tf_op jit(solution)/shard_map/dot_general | solution.py:95
  86.1 4.6 all-to-all-start.1
  90.7 0.0 all-gather.7.cloned.1.call-start
  90.8 0.5 all-gather.7.cloned.1.call-update
  91.3 0.0 all-gather.5.cloned.1.call-start
  91.4 103.7 %all-to-all-done.1 = bf16[8,128,2048]{2,1,0:T(8,128)(2,1)} async-done(((bf16[8,128,2048]{2,1,0:T(8,128)(2,1)}), bf16[8,128,2048]{2,1,0:T(8,128)(2,1)}, u32[]{:S(2)}, u32[]{:S(2)}) %all-to-all-start.1) | async-done | bytes 4194336 | tf_op jit(solution)/shard_map/all_to_all | solution.py:96
  195.1 3.4 convert_reduce_fusion
  198.5 0.0 copy-start.5
  198.5 0.1 convert_bitcast_fusion.1
  198.6 18.2 %reduce-scatter.2.cloned.1.call-done = bf16[128,2048]{1,0:T(8,128)(2,1)} async-done(((bf16[1024,2048]{1,0:T(8,128)(2,1)}), bf16[128,2048]{1,0:T(8,128)(2,1)}) %reduce-scatter.2.cloned.1.call-update) | async-done | bytes 524304 | tf_op jit(solution)/shard_map/reduce_scatter | solution.py:94
  216.8 2.2 pad_maximum_fusion.1
  218.9 0.0 all-gather.5.cloned.1.call-update
  219.0 0.0 all-gather.9.cloned.1.call-start
  219.0 5.4 %all-gather = f32[4,1,4096]{2,1,0:T(1,128)S(1)} all-gather(f32[1,1,4096]{2,1,0:T(1,128)S(1)} %bitcast.174), channel_id=1, replica_groups=mesh['layer'=4,'tok'=8] {'layer'}, dimensions={0}, use_global_device_ids=true | all-gather | bytes 81920 | tf_op jit(solution)/shard_map/all_gather | solution.py:35
  224.5 0.2 broadcast_select_fusion.31
  224.7 0.1 broadcast_select_fusion.33
  224.8 1.2 convert_element_type.108
  226.0 0.0 all-gather.7.cloned.1.call-done
  226.0 27.1 %all-gather.5.cloned.1.call-done = bf16[4,128,4096]{2,1,0:T(8,128)(2,1)} async-done(((bf16[1,128,4096]{2,1,0:T(8,128)(2,1)}), bf16[4,128,4096]{2,1,0:T(8,128)(2,1)}) %all-gather.5.cloned.1.call-update) | async-done | bytes 4194320 | tf_op jit(solution)/shard_map/all_gather | solution.py:68
  253.1 5.2 %fusion.43 = bf16[128,4096]{1,0:T(8,128)(2,1)} fusion(bf16[128,4096]{1,0:T(8,128)(2,1)S(1)} %copy-done, f32[128,2048]{1,0:T(8,128)S(1)} %convert_reduce_fusion, f32[128,2048]{1,0:T(8,128)S(1)} %convert_element_type.108, bf16[4,128,4096]{2,1,0:T(8,128)(2,1)} %all-gather.7.cloned.1.call-done, f32[4096]{0:T(1024)S(1)} %bitcast.173, f32[4096]{0:T(1024)S(1)} %bitcast.172, ...), kind=kLoop, calls=%fused_computation.39 | loop fusion | flops 16777216 | bytes 12697608 | tf_op jit(solution)/shard_map/convert_element_type | solution.py:102
  258.4 0.0 all-gather.9.cloned.1.call-update
  258.4 125.0 %all-gather.9.cloned.1.call-done = bf16[1024,4096]{1,0:T(8,128)(2,1)} async-done(((bf16[128,4096]{1,0:T(8,128)(2,1)}), bf16[1024,4096]{1,0:T(8,128)(2,1)}) %all-gather.9.cloned.1.call-update) | async-done | bytes 8388624 | tf_op jit(solution)/shard_map/all_gather | solution.py:103
  383.5 42.6 %convert_bitcast_fusion = bf16[128,8,32,128]{3,1,2,0:T(8,128)(2,1)} fusion(bf16[1024,4096]{1,0:T(8,128)(2,1)} %all-gather.9.cloned.1.call-done, bf16[1,4096,4096]{2,1,0:T(8,128)(2,1)} %param.8), kind=kOutput, calls=%fused_computation.12 | convolution fusion | flops 34363932672 | bytes 50331648 | tf_op jit(solution)/shard_map/dot_general | solution.py:104
  426.1 9.7 %copy.24 = bf16[128,8,32,128]{3,2,1,0:T(8,128)(2,1)} copy(bf16[128,8,32,128]{3,1,2,0:T(8,128)(2,1)} %convert_bitcast_fusion) | data formatting | bytes 16777216
  435.7 10.7 %select_reduce_fusion = f32[1024,32]{1,0:T(8,128)} fusion(s32[1024,32]{1,0:T(8,128)S(1)} %copy-done.4, bf16[1024,32,128]{2,1,0:T(8,128)(2,1)} %bitcast.159, s32[1024,32]{1,0:T(8,128)S(1)} %copy-done.2), kind=kOutput, calls=%fused_computation.4 | convolution fusion | flops 275742720 | bytes 8781824 | tf_op jit(solution)/shard_map/thl,tkl->tkh/dot_general | solution.py:108
  446.5 1.9 copy.19
  448.3 3.4 all-to-all-start.2
  451.7 4.4 fusion.44
  456.1 2.9 all-to-all-done.2
  459.0 0.6 reduce_sum.29
  (13 shorter events, 0.1 us)
Async XLA Ops:
  10.1 16.2 %all-to-all-start = ((f32[8,128,64]{1,2,0:T(8,128)}), f32[8,128,64]{1,2,0:T(8,128)S(1)}, u32[]{:S(2)}, u32[]{:S(2)}) async-start(f32[8,128,64]{1,2,0:T(8,128)} %broadcast_in_dim.26), calls=%async_computation | async-start | bytes 524288 | tf_op jit(solution)/shard_map/all_to_all | solution.py:27
  17.4 199.3 %reduce-scatter.2.cloned.1.call-start = ((), (), s32[]{:S(2)}) async-start(), calls=%async_computation.4 | async-start | bytes 4718592 | tf_op jit(solution)/shard_map/reduce_scatter | solution.py:94
  26.8 10.1 %copy-start.1 = (s32[1024,32]{1,0:T(8,128)}, s32[1024,32]{1,0:T(8,128)S(1)}, u32[]{:S(2)}) copy-start(s32[1024,32]{1,0:T(8,128)S(1)} %copy.17) | copy-start | bytes 393220
  27.0 9.9 %copy-start.3 = (s32[1024,32]{1,0:T(8,128)}, s32[1024,32]{1,0:T(8,128)S(1)}, u32[]{:S(2)}) copy-start(s32[1024,32]{1,0:T(8,128)S(1)} %copy.15) | copy-start | bytes 393220
  36.9 3.3 copy-start.6
  86.1 109.0 %all-to-all-start.1 = ((bf16[8,128,2048]{2,1,0:T(8,128)(2,1)}), bf16[8,128,2048]{2,1,0:T(8,128)(2,1)}, u32[]{:S(2)}, u32[]{:S(2)}) async-start(bf16[8,128,2048]{2,1,0:T(8,128)(2,1)} %bitcast.160), calls=%async_computation.2 | async-start | bytes 8388608 | tf_op jit(solution)/shard_map/all_to_all | solution.py:96
  90.7 135.3 %all-gather.7.cloned.1.call-start = ((), (), s32[]{:S(2)}) async-start(), calls=%async_computation.6 | async-start | bytes 5242880 | tf_op jit(solution)/shard_map/all_gather | solution.py:36
  91.3 161.8 %all-gather.5.cloned.1.call-start = ((), (), s32[]{:S(2)}) async-start(), calls=%async_computation.5 | async-start | bytes 5242880 | tf_op jit(solution)/shard_map/all_gather | solution.py:68
  198.5 20.6 %copy-start.5 = (f32[1,4096]{1,0:T(1,128)S(1)}, f32[1,4096]{1,0:T(1,128)}, u32[]{:S(2)}) copy-start(f32[1,4096]{1,0:T(1,128)} %param.9) | copy-start | bytes 49156
  216.7 36.4 %copy-start = (bf16[128,4096]{1,0:T(8,128)(2,1)S(1)}, bf16[128,4096]{1,0:T(8,128)(2,1)}, u32[]{:S(2)}) copy-start(bf16[128,4096]{1,0:T(8,128)(2,1)} %param.10) | copy-start | bytes 3145732
  219.0 164.5 %all-gather.9.cloned.1.call-start = ((), (), s32[]{:S(2)}) async-start(), calls=%async_computation.7 | async-start | bytes 9437184 | tf_op jit(solution)/shard_map/all_gather | solution.py:103
  426.1 9.7 %copy-start.2 = (s32[1024,32]{1,0:T(8,128)S(1)}, s32[1024,32]{1,0:T(8,128)}, u32[]{:S(2)}) copy-start(s32[1024,32]{1,0:T(8,128)} %copy-done.1) | copy-start | bytes 393220
  426.1 9.7 %copy-start.4 = (s32[1024,32]{1,0:T(8,128)S(1)}, s32[1024,32]{1,0:T(8,128)}, u32[]{:S(2)}) copy-start(s32[1024,32]{1,0:T(8,128)} %copy-done.3) | copy-start | bytes 393220
  448.3 10.7 %all-to-all-start.2 = ((f32[8,128,32]{1,2,0:T(8,128)}), f32[8,128,32]{1,2,0:T(8,128)S(1)}, u32[]{:S(2)}, u32[]{:S(2)}) async-start(f32[8,128,32]{1,2,0:T(8,128)} %copy.19), calls=%async_computation.3 | async-start | bytes 262144 | tf_op jit(solution)/shard_map/all_to_all | solution.py:115
Sparse Core Ops, SparseCore 0:
  62.3 154.4 reduce-scatter.1
  258.5 124.9 all-gather.8
Sparse Core Ops, SparseCore 1:
  92.9 35.7 all-gather.6
  219.0 34.0 all-gather.4

commit v15 on v10

--- a/solution.py
+++ b/solution.py
@@ -21,13 +21,20 @@
     owners = lax.axis_size("tok")
     top_count = latent_ids.shape[1]
     packed = jnp.concatenate(
-        [latent_ids.astype(jnp.float32), active_codes.astype(jnp.float32)], axis=1
+        [
+            (latent_ids // 256).astype(jnp.bfloat16),
+            (latent_ids % 256).astype(jnp.bfloat16),
+            active_codes,
+        ],
+        axis=1,
     )
     spread = jnp.broadcast_to(packed[None], (owners,) + packed.shape)
     gathered = lax.all_to_all(spread, "tok", split_axis=0, concat_axis=0, tiled=True)
-    gathered = gathered.reshape(-1, 2 * top_count)
-    ids_all = gathered[:, :top_count].astype(jnp.int32)
-    codes_all = gathered[:, top_count:].astype(jnp.bfloat16)
+    gathered = gathered.reshape(-1, 3 * top_count)
+    ids_all = gathered[:, :top_count].astype(jnp.int32) * 256 + gathered[
+        :, top_count:2 * top_count
+    ].astype(jnp.int32)
+    codes_all = gathered[:, 2 * top_count:]
     return ids_all, codes_all
 
 

time: 468 us -> 466 us (level)
  no operation moved by 1% of the time
where the time goes in v15:
time: 466 us
  waiting for transfers between devices  286 us (61%)
  matrix products  109 us (23%)
  other arithmetic  18.2 us (4%)
  local copies, waits for them, and re-layouts  16.2 us (3%)
  between operations  15.7 us (3%)
  starting transfers between devices  15.4 us (3%)
  blocking collectives  5.43 us (1%)
    all_gather x1, waiting for transfers between devices, on_device(): segment = lax.all_gather(grad_low, 'tok', axis=0, tiled=True)  125 us
    all_to_all x1, waiting for transfers between devices, on_device(): lax.all_to_all(partial_second, 'tok', split_axis=0, concat_axis=0, tiled=...  103 us
    dot_general x1, matrix products, on_device(): lax.dot_general(segment, weights, (((1,), (1,)), ((), ())), preferred_ele...  42.6 us
    all_gather x1, waiting for transfers between devices, layer_chain(): lax.all_gather(decoded.astype(jnp.bfloat16), 'layer', axis=0, tiled=False)  27.4 us
    dot_general x1, matrix products, on_device(): jnp.dot(spread, w_second, preferred_element_type=jnp.float32)  24 us
    dot_general x1, matrix products, on_device(): jnp.dot(spread, w_first, preferred_element_type=jnp.float32)  21.9 us
    reduce_scatter x1, waiting for transfers between devices, on_device(): lax.psum_scatter(partial_first, 'tok', scatter_dimension=0, tiled=True)  18.2 us
    unnamed x15, local copies, waits for them, and re-layouts  13 us
  transfers between devices with their start and end apart: 7, of which 6 were waited for; matrix products, arithmetic and copies ran while one was open for 7% of the time, Pallas kernels for 0%

profile of v15, /device:TPU:0, one launch (start us, length us, event | category | flops | bytes accessed | tf_op | source)
XLA Modules:
  0.0 465.8 jit_solution(1806440239437753471)
XLA Ops:
  8.0 0.7 fusion.42
  8.7 0.7 pad_maximum_fusion.2
  9.4 0.7 broadcast_in_dim.35
  10.1 7.3 %all-to-all-start = ((bf16[8,128,96]{1,2,0:T(8,128)(2,1)}), bf16[8,128,96]{1,2,0:T(8,128)(2,1)S(1)}, u32[]{:S(2)}, u32[]{:S(2)}) async-start(bf16[8,128,96]{1,2,0:T(8,128)(2,1)} %broadcast_in_dim.35), calls=%async_computation | async-start | bytes 393216 | tf_op jit(solution)/shard_map/all_to_all | solution.py:32
  17.4 0.0 reduce-scatter.2.cloned.1.call-start
  17.5 7.9 %all-to-all-done = bf16[8,128,96]{1,2,0:T(8,128)(2,1)S(1)} async-done(((bf16[8,128,96]{1,2,0:T(8,128)(2,1)}), bf16[8,128,96]{1,2,0:T(8,128)(2,1)S(1)}, u32[]{:S(2)}, u32[]{:S(2)}) %all-to-all-start) | async-done | bytes 196640 | tf_op jit(solution)/shard_map/all_to_all | solution.py:32
  25.4 0.2 fusion.40
  25.6 0.2 copy.17
  25.8 0.0 copy-start.1
  25.8 0.2 copy.15
  26.0 0.0 copy-start.3
  26.0 0.2 copy.16
  26.2 9.7 %fusion.15 = bf16[1024,32,128]{2,1,0:T(8,128)(2,1)S(1)} fusion(s32[1024,32]{1,0:T(8,128)S(1)} %copy.17, s32[1024,32]{1,0:T(8,128)S(1)} %copy.15, bf16[1024,32]{1,0:T(8,128)(2,1)S(1)} %copy.16), kind=kOutput, calls=%fused_computation.19 | convolution fusion | flops 278921216 | bytes 8716288 | tf_op jit(solution)/shard_map/tkh,tkl->thl/dot_general | solution.py:72
  35.9 0.0 copy-done.1
  35.9 0.0 copy-done.3
  35.9 0.0 copy-start.6
  35.9 3.3 copy-done.6
  39.3 21.9 %fusion.20 = bf16[1024,2048]{1,0:T(8,128)(2,1)} fusion(bf16[4096,4096]{1,0:T(8,128)(2,1)} %bitcast.126, bf16[128,8,32,128]{3,2,1,0:T(8,128)(2,1)S(1)} %bitcast.128), kind=kOutput, calls=%fused_computation.22 | convolution fusion | flops 17181966336 | bytes 29360128 | tf_op jit(solution)/shard_map/dot_general | solution.py:78
  61.1 0.0 reduce-scatter.2.cloned.1.call-update
  61.1 24.0 %fusion.25 = bf16[1024,2048]{1,0:T(8,128)(2,1)} fusion(bf16[4096,4096]{1,0:T(8,128)(2,1)} %bitcast.127, bf16[128,8,32,128]{3,2,1,0:T(8,128)(2,1)} %bitcast.129), kind=kOutput, calls=%fused_computation.23 | convolution fusion | flops 17181966336 | bytes 29360128 | tf_op jit(solution)/shard_map/dot_general | solution.py:80
  85.2 4.6 all-to-all-start.1
  89.7 0.0 all-gather.7.cloned.1.call-start
  89.8 0.5 all-gather.7.cloned.1.call-update
  90.3 0.0 all-gather.5.cloned.1.call-start
  90.4 103.3 %all-to-all-done.1 = bf16[8,128,2048]{2,1,0:T(8,128)(2,1)} async-done(((bf16[8,128,2048]{2,1,0:T(8,128)(2,1)}), bf16[8,128,2048]{2,1,0:T(8,128)(2,1)}, u32[]{:S(2)}, u32[]{:S(2)}) %all-to-all-start.1) | async-done | bytes 4194336 | tf_op jit(solution)/shard_map/all_to_all | solution.py:81
  193.6 3.4 convert_reduce_fusion
  197.0 0.0 copy-start.5
  197.0 0.1 convert_bitcast_fusion.1
  197.1 18.2 %reduce-scatter.2.cloned.1.call-done = bf16[128,2048]{1,0:T(8,128)(2,1)} async-done(((bf16[1024,2048]{1,0:T(8,128)(2,1)}), bf16[128,2048]{1,0:T(8,128)(2,1)}) %reduce-scatter.2.cloned.1.call-update) | async-done | bytes 524304 | tf_op jit(solution)/shard_map/reduce_scatter | solution.py:79
  215.3 2.2 pad_maximum_fusion.1
  217.5 0.0 all-gather.5.cloned.1.call-update
  217.5 0.0 all-gather.9.cloned.1.call-start
  217.6 5.4 %all-gather = f32[4,1,4096]{2,1,0:T(1,128)S(1)} all-gather(f32[1,1,4096]{2,1,0:T(1,128)S(1)} %bitcast.123), channel_id=1, replica_groups=mesh['layer'=4,'tok'=8] {'layer'}, dimensions={0}, use_global_device_ids=true | all-gather | bytes 81920 | tf_op jit(solution)/shard_map/all_gather | solution.py:42
  223.0 1.2 convert_element_type.103
  224.2 0.0 all-gather.7.cloned.1.call-done
  224.3 27.4 %all-gather.5.cloned.1.call-done = bf16[4,128,4096]{2,1,0:T(8,128)(2,1)} async-done(((bf16[1,128,4096]{2,1,0:T(8,128)(2,1)}), bf16[4,128,4096]{2,1,0:T(8,128)(2,1)}) %all-gather.5.cloned.1.call-update) | async-done | bytes 4194320 | tf_op jit(solution)/shard_map/all_gather | solution.py:44
  251.7 0.0 copy-done
  251.7 5.4 %fusion.34 = bf16[128,4096]{1,0:T(8,128)(2,1)} fusion(bf16[128,4096]{1,0:T(8,128)(2,1)S(1)} %copy-done, f32[128,2048]{1,0:T(8,128)S(1)} %convert_reduce_fusion, f32[128,2048]{1,0:T(8,128)S(1)} %convert_element_type.103, bf16[4,128,4096]{2,1,0:T(8,128)(2,1)} %all-gather.7.cloned.1.call-done, f32[4096]{0:T(1024)S(1)} %bitcast.121, f32[4096]{0:T(1024)S(1)} %bitcast.117, ...), kind=kLoop, calls=%fused_computation.33 | loop fusion | flops 19398656 | bytes 12648452 | tf_op jit(solution)/shard_map/convert_element_type | solution.py:87
  257.1 0.0 all-gather.9.cloned.1.call-update
  257.1 125.1 %all-gather.9.cloned.1.call-done = bf16[1024,4096]{1,0:T(8,128)(2,1)} async-done(((bf16[128,4096]{1,0:T(8,128)(2,1)}), bf16[1024,4096]{1,0:T(8,128)(2,1)}) %all-gather.9.cloned.1.call-update) | async-done | bytes 8388624 | tf_op jit(solution)/shard_map/all_gather | solution.py:88
  382.2 42.6 %convert_bitcast_fusion = bf16[128,8,32,128]{3,1,2,0:T(8,128)(2,1)} fusion(bf16[1024,4096]{1,0:T(8,128)(2,1)} %all-gather.9.cloned.1.call-done, bf16[1,4096,4096]{2,1,0:T(8,128)(2,1)} %param.8), kind=kOutput, calls=%fused_computation.12 | convolution fusion | flops 34363932672 | bytes 50331648 | tf_op jit(solution)/shard_map/dot_general | solution.py:89
  424.8 9.7 %copy.24 = bf16[128,8,32,128]{3,2,1,0:T(8,128)(2,1)} copy(bf16[128,8,32,128]{3,1,2,0:T(8,128)(2,1)} %convert_bitcast_fusion) | data formatting | bytes 16777216
  434.5 10.7 %select_reduce_fusion = f32[1024,32]{1,0:T(8,128)} fusion(s32[1024,32]{1,0:T(8,128)S(1)} %copy-done.4, bf16[1024,32,128]{2,1,0:T(8,128)(2,1)} %bitcast.111, s32[1024,32]{1,0:T(8,128)S(1)} %copy-done.2), kind=kOutput, calls=%fused_computation.4 | convolution fusion | flops 275742720 | bytes 8781824 | tf_op jit(solution)/shard_map/thl,tkl->tkh/dot_general | solution.py:93
  445.2 1.9 copy.19
  447.1 3.4 all-to-all-start.2
  450.5 3.8 fusion.39
  454.3 3.5 all-to-all-done.2
  457.7 0.6 reduce_sum.29
  (9 shorter events, 0.0 us)
Async XLA Ops:
  10.1 15.2 %all-to-all-start = ((bf16[8,128,96]{1,2,0:T(8,128)(2,1)}), bf16[8,128,96]{1,2,0:T(8,128)(2,1)S(1)}, u32[]{:S(2)}, u32[]{:S(2)}) async-start(bf16[8,128,96]{1,2,0:T(8,128)(2,1)} %broadcast_in_dim.35), calls=%async_computation | async-start | bytes 393216 | tf_op jit(solution)/shard_map/all_to_all | solution.py:32
  17.4 197.9 %reduce-scatter.2.cloned.1.call-start = ((), (), s32[]{:S(2)}) async-start(), calls=%async_computation.4 | async-start | bytes 4718592 | tf_op jit(solution)/shard_map/reduce_scatter | solution.py:79
  25.8 10.1 %copy-start.1 = (s32[1024,32]{1,0:T(8,128)}, s32[1024,32]{1,0:T(8,128)S(1)}, u32[]{:S(2)}) copy-start(s32[1024,32]{1,0:T(8,128)S(1)} %copy.17) | copy-start | bytes 393220
  26.0 9.9 %copy-start.3 = (s32[1024,32]{1,0:T(8,128)}, s32[1024,32]{1,0:T(8,128)S(1)}, u32[]{:S(2)}) copy-start(s32[1024,32]{1,0:T(8,128)S(1)} %copy.15) | copy-start | bytes 393220
  35.9 3.3 copy-start.6
  85.2 108.5 %all-to-all-start.1 = ((bf16[8,128,2048]{2,1,0:T(8,128)(2,1)}), bf16[8,128,2048]{2,1,0:T(8,128)(2,1)}, u32[]{:S(2)}, u32[]{:S(2)}) async-start(bf16[8,128,2048]{2,1,0:T(8,128)(2,1)} %bitcast.112), calls=%async_computation.2 | async-start | bytes 8388608 | tf_op jit(solution)/shard_map/all_to_all | solution.py:81
  89.7 134.5 %all-gather.7.cloned.1.call-start = ((), (), s32[]{:S(2)}) async-start(), calls=%async_computation.6 | async-start | bytes 5242880 | tf_op jit(solution)/shard_map/all_gather | solution.py:43
  90.3 161.4 %all-gather.5.cloned.1.call-start = ((), (), s32[]{:S(2)}) async-start(), calls=%async_computation.5 | async-start | bytes 5242880 | tf_op jit(solution)/shard_map/all_gather | solution.py:44
  197.0 20.6 %copy-start.5 = (f32[1,4096]{1,0:T(1,128)S(1)}, f32[1,4096]{1,0:T(1,128)}, u32[]{:S(2)}) copy-start(f32[1,4096]{1,0:T(1,128)} %param.9) | copy-start | bytes 49156
  215.3 36.4 %copy-start = (bf16[128,4096]{1,0:T(8,128)(2,1)S(1)}, bf16[128,4096]{1,0:T(8,128)(2,1)}, u32[]{:S(2)}) copy-start(bf16[128,4096]{1,0:T(8,128)(2,1)} %param.10) | copy-start | bytes 3145732
  217.5 164.7 %all-gather.9.cloned.1.call-start = ((), (), s32[]{:S(2)}) async-start(), calls=%async_computation.7 | async-start | bytes 9437184 | tf_op jit(solution)/shard_map/all_gather | solution.py:88
  424.8 9.7 %copy-start.2 = (s32[1024,32]{1,0:T(8,128)S(1)}, s32[1024,32]{1,0:T(8,128)}, u32[]{:S(2)}) copy-start(s32[1024,32]{1,0:T(8,128)} %copy-done.1) | copy-start | bytes 393220
  424.8 9.7 %copy-start.4 = (s32[1024,32]{1,0:T(8,128)S(1)}, s32[1024,32]{1,0:T(8,128)}, u32[]{:S(2)}) copy-start(s32[1024,32]{1,0:T(8,128)} %copy-done.3) | copy-start | bytes 393220
  447.1 10.7 %all-to-all-start.2 = ((f32[8,128,32]{1,2,0:T(8,128)}), f32[8,128,32]{1,2,0:T(8,128)S(1)}, u32[]{:S(2)}, u32[]{:S(2)}) async-start(f32[8,128,32]{1,2,0:T(8,128)} %copy.19), calls=%async_computation.3 | async-start | bytes 262144 | tf_op jit(solution)/shard_map/all_to_all | solution.py:100
Sparse Core Ops, SparseCore 0:
  61.3 154.0 reduce-scatter.1
  257.3 124.9 all-gather.8
Sparse Core Ops, SparseCore 1:
  91.9 35.6 all-gather.6
  217.6 34.0 all-gather.4
